TPU v7x, 128 devices: a whole 4x4x4 slice. The times are simulated.
128 devices in a mesh: dp: 16 (over z, y), tensor: 8 (over x, core).
Axes of the slice: x: 4, y: 4, z: 4, core: 2. Of those that a mesh axis runs over, the one named last changes fastest.
Arguments:
- hidden_in: bfloat16 [16384, 2048], P(('dp', 'tensor')), may hold values from -6 to 6
- layer_input: bfloat16 [16384, 256], P(('dp', 'tensor')), may hold values from -6 to 6
- cached_len: int32 [32], replicated, may hold values from 3584 to 4096, as said below
- page_table: int32 [32, 32], replicated, may hold values from 0 to 2047, as said below
- kv_pool: bfloat16 [2048, 2, 2, 128, 256], P(('dp', 'tensor'))
- norm_in: float32 [2048], replicated, may hold values from 0.5 to 1.5
- w_query: bfloat16 [2048, 2048], P(None, 'tensor'), may hold values from -0.125 to 0.125
- w_keyval: bfloat16 [2048, 1024], replicated, may hold values from -0.125 to 0.125
- q_gain: float32 [256], replicated, may hold values from 0.1 to 0.4
- k_gain: float32 [256], replicated, may hold values from 0.5 to 1.5
- w_out: bfloat16 [2048, 2048], P('tensor'), may hold values from -0.125 to 0.125
- post_attn_gain: float32 [2048], replicated, may hold values from 0.5 to 1.5
- laurel_left: bfloat16 [2048, 64], replicated, may hold values from -0.125 to 0.125
- laurel_right: bfloat16 [64, 2048], replicated, may hold values from -0.75 to 0.75
- laurel_gain: float32 [2048], replicated, may hold values from 0.5 to 1.5
- pre_ffn_gain: float32 [2048], replicated, may hold values from 0.5 to 1.5
- w_gate: bfloat16 [2048, 8192], P(None, 'tensor'), may hold values from -0.125 to 0.125
- w_up: bfloat16 [2048, 8192], P(None, 'tensor'), may hold values from -0.125 to 0.125
- w_down: bfloat16 [8192, 2048], P('tensor'), may hold values from -0.0625 to 0.0625
- post_ffn_gain: float32 [2048], replicated, may hold values from 0.5 to 1.5
- ple_gate: bfloat16 [2048, 256], replicated, may hold values from -0.125 to 0.125
- ple_proj: bfloat16 [256, 2048], replicated, may hold values from -0.375 to 0.375
- ple_gain: float32 [2048], replicated, may hold values from 0.5 to 1.5
Outputs:
- layer_out: bfloat16 [16384, 2048], P(('dp', 'tensor'))
Inputs may be any that keep to these rules, and one draw needn't show every extreme that they name: `cached_len`: the last request of the first index of dp, and the last request of all, have 4096 cached tokens. `page_table`: page id q lives on the device with flat index q // 16 over dp+tensor (dp slowest), at row q % 16 of its shard. Only slots below ceil(cached_len / 128) are read; every slot names a page. Requests r with the same r // 8 name the same pages in their first 8 slots, and no other page is named twice. The slots that are read by the requests of one index of dp name at most 1 distinct pages of any one device, and some index of dp reaches 1.
All inputs are finite; a program needn't handle non-finite values.
Results may differ from a plain program's by a relative error of at most 0.015.
The roundings to bfloat16 on the way count: a program that leaves them out, or rounds other values in their place, can miss the bound.
Values may be sent and summed in bfloat16 or wider, within the bound.
No kernel may reach another device: no remote copies, remote signals or barrier semaphores. Data moves between devices by JAX's collectives and lax.ppermute only.
A program may use at most 192 MiB of HBM per device.

v0:
```python
import math

import jax
import jax.numpy as jnp
from jax import lax
from jax.sharding import PartitionSpec as P

KVH = 2
PROMPT_PAGES = 8
REQ_DEV = 2


EPS = 1e-06
BIG = 1e30
HALF_ROOT = 1.0 / math.sqrt(2.0)


def norm_rows(values, gain):
    return values * lax.rsqrt(jnp.mean(values * values, axis=-1, keepdims=True) + EPS) * gain


def rotate(values, position):
    half_dim = values.shape[-1] // 2
    freqs = jnp.exp(jnp.arange(half_dim, dtype=jnp.float32) * (-math.log(1000000.0) / half_dim))
    angle = position.astype(jnp.float32)[:, None] * freqs[None, :]
    cosine = jnp.cos(angle)[:, None, :]
    sine = jnp.sin(angle)[:, None, :]
    first = values[..., :half_dim]
    second = values[..., half_dim:]
    return jnp.concatenate(
        [first * cosine - second * sine, second * cosine + first * sine], axis=-1
    )


def attend(queries, cache_keys, cache_values, fresh_keys, fresh_values, length):
    new_count = queries.shape[0]
    offsets = jnp.arange(new_count, dtype=jnp.int32)
    visible_cache = (jnp.arange(cache_keys.shape[0], dtype=jnp.int32) < length)[None, None, :]
    visible_new = (offsets[:, None] >= offsets[None, :])[None, :, :]
    score_cache = jnp.where(
        visible_cache,
        jnp.einsum("nhd,ld->hnl", queries, cache_keys, preferred_element_type=jnp.float32),
        -BIG,
    )
    score_new = jnp.where(
        visible_new,
        jnp.einsum("nhd,md->hnm", queries, fresh_keys, preferred_element_type=jnp.float32),
        -BIG,
    )
    top = jnp.maximum(
        jnp.max(score_cache, axis=-1, keepdims=True), jnp.max(score_new, axis=-1, keepdims=True)
    )
    exp_cache = jnp.exp(score_cache - top)
    exp_new = jnp.exp(score_new - top)
    total = jnp.sum(exp_cache, axis=-1, keepdims=True) + jnp.sum(exp_new, axis=-1, keepdims=True)
    weight_cache = (exp_cache / total).astype(jnp.bfloat16)
    weight_new = (exp_new / total).astype(jnp.bfloat16)
    mixed = jnp.einsum(
        "hnl,ld->nhd", weight_cache, cache_values, preferred_element_type=jnp.float32
    )
    mixed = mixed + jnp.einsum(
        "hnm,md->nhd", weight_new, fresh_values, preferred_element_type=jnp.float32
    )
    return mixed.reshape(new_count, -1).astype(jnp.bfloat16)


def residual_mix(
    residual, projected, normed, post_attn_gain, laurel_left, laurel_right, laurel_gain
):
    left_part = jnp.dot(normed, laurel_left, preferred_element_type=jnp.float32).astype(
        jnp.bfloat16
    )
    laurel_out = normed.astype(jnp.float32) + norm_rows(
        jnp.dot(left_part, laurel_right, preferred_element_type=jnp.float32), laurel_gain
    )
    return (residual + norm_rows(projected, post_attn_gain) + laurel_out) * HALF_ROOT


def geglu(block, w_gate, w_up):
    gate_part = jnp.dot(block, w_gate, preferred_element_type=jnp.float32)
    up_part = jnp.dot(block, w_up, preferred_element_type=jnp.float32)
    return (jax.nn.gelu(gate_part, approximate=True) * up_part).astype(jnp.bfloat16)


def per_device(
    hidden_in,
    layer_input,
    cached_len,
    page_table,
    kv_pool,
    norm_in,
    w_query,
    w_keyval,
    q_gain,
    k_gain,
    w_out,
    post_attn_gain,
    laurel_left,
    laurel_right,
    laurel_gain,
    pre_ffn_gain,
    w_gate,
    w_up,
    w_down,
    post_ffn_gain,
    ple_gate,
    ple_proj,
    ple_gain,
):
    dp_count = lax.axis_size("dp")
    tp_count = lax.axis_size("tensor")
    devices = dp_count * tp_count
    dp_at = lax.axis_index("dp")
    tp_at = lax.axis_index("tensor")
    own_rows = hidden_in.shape[0]
    head_dim = q_gain.shape[0]
    local_heads = w_query.shape[1] // head_dim
    sharing = tp_count // KVH
    kv_head = tp_at // sharing
    slot_count = page_table.shape[1]
    page_len = kv_pool.shape[3]
    pool_dev = kv_pool.shape[0]
    needed = PROMPT_PAGES + REQ_DEV * (slot_count - PROMPT_PAGES)
    capacity = (needed + devices - 1) // devices
    page_count = (cached_len + page_len - 1) // page_len
    used_slots = jnp.arange(slot_count, dtype=jnp.int32)[None, :] < page_count[:, None]
    group_used = used_slots.reshape(dp_count, REQ_DEV * slot_count)
    group_table = page_table.reshape(dp_count, REQ_DEV * slot_count)
    own_flat = dp_at * tp_count + tp_at
    own_ids = own_flat * pool_dev + jnp.arange(pool_dev, dtype=jnp.int32)
    wanted = jnp.any(
        group_used[:, :, None] & (group_table[:, :, None] == own_ids[None, None, :]), axis=1
    )
    wanted_rank = jnp.cumsum(wanted.astype(jnp.int32), axis=1) - 1
    slot_ids = jnp.arange(capacity, dtype=jnp.int32)
    selector = (wanted[:, None, :] & (wanted_rank[:, None, :] == slot_ids[None, :, None])).astype(
        jnp.bfloat16
    )
    picked = jnp.einsum(
        "dcl,lkhpe->dhckpe", selector, kv_pool, preferred_element_type=jnp.float32
    ).astype(jnp.bfloat16)
    outgoing = jnp.repeat(picked, sharing, axis=1).reshape(devices, capacity, 2, page_len, head_dim)
    arrived = lax.all_to_all(outgoing, ("dp", "tensor"), split_axis=0, concat_axis=0, tiled=True)
    own_used = lax.dynamic_index_in_dim(group_used, dp_at, 0, keepdims=False)
    own_table = lax.dynamic_index_in_dim(group_table, dp_at, 0, keepdims=False)
    every_page = jnp.arange(devices * pool_dev, dtype=jnp.int32)
    present = jnp.any(own_used[None, :] & (own_table[None, :] == every_page[:, None]), axis=1)
    present_rank = (
        jnp.cumsum(present.reshape(devices, pool_dev).astype(jnp.int32), axis=1) - 1
    ).reshape(-1)
    position_at = jnp.where(own_used, own_table // pool_dev * capacity + present_rank[own_table], 0)
    fetched = arrived.reshape(devices * capacity, 2, page_len, head_dim)[position_at]
    fetched = fetched.reshape(REQ_DEV, slot_count, 2, page_len, head_dim)
    own_lengths = lax.dynamic_slice_in_dim(cached_len, dp_at * REQ_DEV, REQ_DEV, 0)
    gathered = lax.all_gather(hidden_in, "tensor", axis=0, tiled=True)
    token_count = gathered.shape[0]
    new_count = token_count // REQ_DEV
    normed = norm_rows(gathered.astype(jnp.float32), norm_in).astype(jnp.bfloat16)
    offsets = jnp.arange(new_count, dtype=jnp.int32)
    position = (own_lengths[:, None] + offsets[None, :]).reshape(-1)
    queries = jnp.dot(normed, w_query, preferred_element_type=jnp.float32).reshape(
        token_count, local_heads, head_dim
    )
    queries = rotate(norm_rows(queries, q_gain), position).astype(jnp.bfloat16)
    key_weight = lax.dynamic_slice_in_dim(w_keyval, kv_head * head_dim, head_dim, 1)
    value_weight = lax.dynamic_slice_in_dim(w_keyval, (KVH + kv_head) * head_dim, head_dim, 1)
    fresh_keys = norm_rows(jnp.dot(normed, key_weight, preferred_element_type=jnp.float32), k_gain)
    fresh_keys = rotate(fresh_keys[:, None, :], position)[:, 0].astype(jnp.bfloat16)
    fresh_values = norm_rows(
        jnp.dot(normed, value_weight, preferred_element_type=jnp.float32), 1.0
    ).astype(jnp.bfloat16)
    pieces = []
    for request in range(REQ_DEV):
        lower = request * new_count
        pieces.append(
            attend(
                queries[lower : lower + new_count],
                fetched[request, :, 0].reshape(-1, head_dim),
                fetched[request, :, 1].reshape(-1, head_dim),
                fresh_keys[lower : lower + new_count],
                fresh_values[lower : lower + new_count],
                own_lengths[request],
            )
        )
    attended = jnp.concatenate(pieces, axis=0)
    own_x = hidden_in.astype(jnp.float32)
    projected = lax.psum_scatter(
        jnp.dot(attended, w_out, preferred_element_type=jnp.float32),
        "tensor",
        scatter_dimension=0,
        tiled=True,
    )
    own_normed = lax.dynamic_slice_in_dim(normed, tp_at * own_rows, own_rows, 0)
    mixed_rows = residual_mix(
        own_x, projected, own_normed, post_attn_gain, laurel_left, laurel_right, laurel_gain
    )
    ffn_in = norm_rows(mixed_rows, pre_ffn_gain).astype(jnp.bfloat16)
    hidden = geglu(lax.all_gather(ffn_in, "tensor", axis=0, tiled=True), w_gate, w_up)
    down = lax.psum_scatter(
        jnp.dot(hidden, w_down, preferred_element_type=jnp.float32).astype(jnp.bfloat16),
        "tensor",
        scatter_dimension=0,
        tiled=True,
    ).astype(jnp.float32)
    settled = mixed_rows + norm_rows(down, post_ffn_gain)
    settled_half = settled.astype(jnp.bfloat16)
    gated = jax.nn.gelu(
        jnp.dot(settled_half, ple_gate, preferred_element_type=jnp.float32), approximate=True
    )
    gated = (gated * layer_input.astype(jnp.float32)).astype(jnp.bfloat16)
    return (
        settled + norm_rows(jnp.dot(gated, ple_proj, preferred_element_type=jnp.float32), ple_gain)
    ).astype(jnp.bfloat16)


def solution(mesh):
    placed = (
        P(("dp", "tensor"), None),
        P(("dp", "tensor"), None),
        P(),
        P(),
        P(("dp", "tensor"), None, None, None, None),
        P(),
        P(None, "tensor"),
        P(),
        P(),
        P(),
        P("tensor", None),
        P(),
        P(),
        P(),
        P(),
        P(),
        P(None, "tensor"),
        P(None, "tensor"),
        P("tensor", None),
        P(),
        P(),
        P(),
        P(),
    )
    return jax.shard_map(
        per_device, mesh=mesh, in_specs=placed, out_specs=P(("dp", "tensor"), None), check_vma=False
    )
```

profile of v0, /device:TPU:0, one launch (start us, length us, event | category | flops | bytes accessed | tf_op | source)
XLA Modules:
  0.0 474.0 jit_solution(13864545463204471179)
XLA Ops:
  6.5 0.9 eq.39
  7.4 0.7 and_select_fusion.1
  8.4 0.4 and_reduce_fusion
  9.0 4.7 convert_bitcast_fusion
  13.8 1.5 copy.35
  15.2 6.0 %broadcast_in_dim.26 = bf16[16,2,4,2,128,256]{5,4,3,2,1,0:T(8,128)(2,1)} broadcast(bf16[16,2,2,128,256]{4,3,2,1,0:T(8,128)(2,1)S(1)} %copy.35), dimensions={0,1,3,4,5} | broadcast | bytes 20971520 | tf_op jit(solution)/shard_map/broadcast_in_dim | solution.py:142
  21.2 11.7 %all-to-all-start = ((bf16[128,1,2,128,256]{4,3,2,1,0:T(8,128)(2,1)}), bf16[128,1,2,128,256]{4,3,2,1,0:T(8,128)(2,1)}, u32[]{:S(2)}, u32[]{:S(2)}) async-start(bf16[128,1,2,128,256]{4,3,2,1,0:T(8,128)(2,1)} %bitcast.174), calls=%async_computation | async-start | bytes 33554432 | tf_op jit(solution)/shard_map/all_to_all | solution.py:143
  33.0 0.7 all-gather.3.cloned.1.call-update
  34.6 0.8 gather_fusion
  35.5 0.6 fusion.145
  36.1 0.6 iota_compare_fusion.2
  36.7 0.7 iota_compare_fusion.3
  37.4 64.3 %all-gather.3.cloned.1.call-done = bf16[1024,2048]{1,0:T(8,128)(2,1)} async-done(((bf16[128,2048]{1,0:T(8,128)(2,1)}), bf16[1024,2048]{1,0:T(8,128)(2,1)}) %all-gather.3.cloned.1.call-update) | async-done | bytes 4194320 | tf_op jit(solution)/shard_map/all_gather | solution.py:155
  101.6 3.2 fusion
  105.1 1.0 fusion.2
  106.1 1.2 copy-done.16
  107.3 1.3 multiply_reduce_fusion.5
  108.6 0.6 copy-done.17
  109.2 1.3 multiply_reduce_fusion.6
  110.9 2.6 fusion.56
  113.5 1.3 fusion.148
  114.8 0.3 fusion.149
  115.1 1.4 multiply_reduce_fusion.4
  116.6 141.4 %all-to-all-done = bf16[128,1,2,128,256]{4,3,2,1,0:T(8,128)(2,1)} async-done(((bf16[128,1,2,128,256]{4,3,2,1,0:T(8,128)(2,1)}), bf16[128,1,2,128,256]{4,3,2,1,0:T(8,128)(2,1)}, u32[]{:S(2)}, u32[]{:S(2)}) %all-to-all-start) | async-done | bytes 16777248 | tf_op jit(solution)/shard_map/all_to_all | solution.py:143
  258.0 11.2 %gather_fusion.1 = bf16[64,2,128,256]{3,2,1,0:T(8,128)(2,1)} fusion(bf16[128,2,128,256]{3,2,1,0:T(8,128)(2,1)} %bitcast.7, s32[1024]{0:T(1024)S(1)} %pad_clamp_fusion), kind=kCustom, calls=%fused_computation.1 | custom fusion | bytes 16777472 | tf_op jit(solution)/shard_map/gather | solution.py:152
  269.2 4.0 fusion.144
  273.2 1.3 fusion.4
  274.5 2.4 fusion.6
  277.1 1.3 fusion.3
  278.4 2.6 fusion.5
  281.3 2.4 fusion.16
  283.7 0.4 fusion.28
  284.1 2.4 fusion.18
  286.5 0.4 fusion.29
  286.9 4.5 fusion.59
  291.5 0.9 copy-done.5
  292.5 2.0 multiply_reduce_fusion.2
  294.4 65.8 %reduce-scatter.3.cloned.1.call-done = f32[128,2048]{1,0:T(8,128)} async-done(((f32[1024,2048]{1,0:T(8,128)}), f32[128,2048]{1,0:T(8,128)}) %reduce-scatter.3.cloned.1.call-update) | async-done | bytes 1048592 | tf_op jit(solution)/shard_map/reduce_scatter | solution.py:187
  360.2 1.4 multiply_reduce_fusion.3
  361.6 2.1 multiply_reduce_fusion.1
  363.7 0.9 multiply_convert_fusion
  364.7 31.7 %all-gather.5.cloned.1.call-done = bf16[1024,2048]{1,0:T(8,128)(2,1)} async-done(((bf16[128,2048]{1,0:T(8,128)(2,1)}), bf16[1024,2048]{1,0:T(8,128)(2,1)}) %all-gather.5.cloned.1.call-update) | async-done | bytes 4194320 | tf_op jit(solution)/shard_map/all_gather | solution.py:198
  396.5 9.9 %fusion.152 = f32[1024,1024]{1,0:T(8,128)} fusion(bf16[1024,2048]{1,0:T(8,128)(2,1)} %all-gather.5.cloned.1.call-done, bf16[2048,1024]{1,0:T(8,128)(2,1)} %param.39), kind=kOutput, calls=%fused_computation.211 | convolution fusion | flops 4294967296 | bytes 12582912 | tf_op jit(solution)/shard_map/dot_general | solution.py:80
  406.4 15.6 %convolution_convert_fusion = bf16[1024,2048]{1,0:T(8,128)(2,1)} fusion(bf16[1024,2048]{1,0:T(8,128)(2,1)} %param.41, f32[1024,1024]{1,0:T(8,128)} %fusion.152, bf16[1024,2048]{1,0:T(8,128)(2,1)} %all-gather.5.cloned.1.call-done, bf16[2048,1024]{1,0:T(8,128)(2,1)} %param.40), kind=kOutput, calls=%fused_computation.34 | convolution fusion | flops 8602517504 | bytes 20971520 | tf_op jit(solution)/shard_map/dot_general | solution.py:200
  422.1 38.0 %reduce-scatter.5.cloned.1.call-done = bf16[128,2048]{1,0:T(8,128)(2,1)} async-done(((bf16[1024,2048]{1,0:T(8,128)(2,1)}), bf16[128,2048]{1,0:T(8,128)(2,1)}) %reduce-scatter.5.cloned.1.call-update) | async-done | bytes 524304 | tf_op jit(solution)/shard_map/reduce_scatter | solution.py:199
  460.1 1.3 fusion.31
  461.4 3.5 multiply_reduce_fusion
  465.0 2.5 add_convert_fusion
  (88 shorter events, 2.8 us)
Async XLA Ops:
  6.5 280.4 %copy-start = (bf16[256,2048]{1,0:T(8,128)(2,1)S(1)}, bf16[256,2048]{1,0:T(8,128)(2,1)}, u32[]{:S(2)}) copy-start(bf16[256,2048]{1,0:T(8,128)(2,1)} %param.33) | copy-start | bytes 3145732
  21.2 13.2 %copy-start.18 = (s32[32]{0:T(128)S(1)}, s32[32]{0:T(128)}, u32[]{:S(2)}) copy-start(s32[32]{0:T(128)} %param.25) | copy-start | bytes 388
  21.2 236.8 %all-to-all-start = ((bf16[128,1,2,128,256]{4,3,2,1,0:T(8,128)(2,1)}), bf16[128,1,2,128,256]{4,3,2,1,0:T(8,128)(2,1)}, u32[]{:S(2)}, u32[]{:S(2)}) async-start(bf16[128,1,2,128,256]{4,3,2,1,0:T(8,128)(2,1)} %bitcast.174), calls=%async_computation | async-start | bytes 33554432 | tf_op jit(solution)/shard_map/all_to_all | solution.py:143
  33.0 71.9 %copy-start.9 = (f32[2048]{0:T(1024)S(1)}, f32[2048]{0:T(1024)}, u32[]{:S(2)}) copy-start(f32[2048]{0:T(1024)} %param.28) | copy-start | bytes 24580
  33.0 68.7 %all-gather.3.cloned.1.call-start = ((), (), s32[]{:S(2)}) async-start(), calls=%async_computation.3 | async-start | bytes 4718592 | tf_op jit(solution)/shard_map/all_gather | solution.py:155
  33.7 326.5 %reduce-scatter.3.cloned.1.call-start = ((), (), s32[]{:S(2)}) async-start(), calls=%async_computation.4 | async-start | bytes 9437184 | tf_op jit(solution)/shard_map/reduce_scatter | solution.py:187
  101.6 3.4 copy-start.1
  105.1 2.2 copy-start.16
  107.3 7.9 %copy-start.2 = (bf16[1024,2048]{1,0:T(8,128)(2,1)}, bf16[1024,2048]{1,0:T(8,128)(2,1)S(1)}, u32[]{:S(2)}) copy-start(bf16[1024,2048]{1,0:T(8,128)(2,1)S(1)} %fusion.2) | copy-start | bytes 12582916
  107.3 2.0 copy-start.17
  109.2 1.4 copy-start.14
  109.2 1.4 copy-start.15
  274.5 2.4 copy-start.4
  291.4 0.9 copy-start.5
  291.4 1.0 copy-start.6
  291.4 70.2 %copy-start.10 = (f32[2048]{0:T(1024)S(1)}, f32[2048]{0:T(1024)}, u32[]{:S(2)}) copy-start(f32[2048]{0:T(1024)} %param.37) | copy-start | bytes 24580
  291.4 70.2 %copy-start.11 = (f32[2048]{0:T(1024)S(1)}, f32[2048]{0:T(1024)}, u32[]{:S(2)}) copy-start(f32[2048]{0:T(1024)} %param.34) | copy-start | bytes 24580
  291.5 72.2 %copy-start.12 = (f32[2048]{0:T(1024)S(1)}, f32[2048]{0:T(1024)}, u32[]{:S(2)}) copy-start(f32[2048]{0:T(1024)} %param.38) | copy-start | bytes 24580
  291.5 105.0 %all-gather.5.cloned.1.call-start = ((), (), s32[]{:S(2)}) async-start(), calls=%async_computation.5 | async-start | bytes 4718592 | tf_op jit(solution)/shard_map/all_gather | solution.py:198
  364.7 95.4 %reduce-scatter.5.cloned.1.call-start = ((), (), s32[]{:S(2)}) async-start(), calls=%async_computation.6 | async-start | bytes 4718592 | tf_op jit(solution)/shard_map/reduce_scatter | solution.py:199
  422.0 39.4 %copy-start.7 = (bf16[128,256]{1,0:T(8,128)(2,1)S(1)}, bf16[128,256]{1,0:T(8,128)(2,1)}, u32[]{:S(2)}) copy-start(bf16[128,256]{1,0:T(8,128)(2,1)} %param.24) | copy-start | bytes 196612
  422.0 39.4 %copy-start.8 = (f32[2048]{0:T(1024)S(1)}, f32[2048]{0:T(1024)}, u32[]{:S(2)}) copy-start(f32[2048]{0:T(1024)} %param.42) | copy-start | bytes 24580
  422.0 43.0 %copy-start.13 = (f32[2048]{0:T(1024)S(1)}, f32[2048]{0:T(1024)}, u32[]{:S(2)}) copy-start(f32[2048]{0:T(1024)} %param.45) | copy-start | bytes 24580
  460.1 4.9 %copy-start.3 = (bf16[128,2048]{1,0:T(8,128)(2,1)S(1)}, bf16[128,2048]{1,0:T(8,128)(2,1)}, u32[]{:S(2)}) copy-start(bf16[128,2048]{1,0:T(8,128)(2,1)} %reduce-scatter.5.cloned.1.call-done) | copy-start | bytes 1572868
Sparse Core Ops, SparseCore 0:
  35.5 66.0 all-gather.2
  291.6 68.5 reduce-scatter.2
  364.8 31.6 all-gather.4
  422.2 37.8 reduce-scatter.4
where the time goes:
time: 475 us; the launch traced here: 474 us
  waiting for transfers between devices  342 us (72%)
  matrix products  54.1 us (11%)
  local copies, waits for them, and re-layouts  28.7 us (6%)
  other arithmetic  23.9 us (5%)
  between operations  13.5 us (3%)
  starting transfers between devices  11.9 us (3%)
    all_to_all x1, waiting for transfers between devices, per_device(): lax.all_to_all(outgoing, ('dp', 'tensor'), split_axis=0, concat_axis=0, t...  141 us
    reduce_scatter x1, waiting for transfers between devices, per_device(): lax.psum_scatter(jnp.dot(attended, w_out, preferred_element_type=jnp.floa...  65.8 us
    all_gather x1, waiting for transfers between devices, per_device(): gathered = lax.all_gather(hidden_in, 'tensor', axis=0, tiled=True)  64.3 us
    reduce_scatter x1, waiting for transfers between devices, per_device(): lax.psum_scatter(jnp.dot(hidden, w_down, preferred_element_type=jnp.float...  38 us
    all_gather x1, waiting for transfers between devices, per_device(): lax.all_gather(ffn_in, 'tensor', axis=0, tiled=True)  31.7 us
    dot_general x1, matrix products, per_device(): jnp.dot(hidden, w_down, preferred_element_type=jnp.float32)  15.6 us
    all_to_all x1, starting transfers between devices, per_device(): lax.all_to_all(outgoing, ('dp', 'tensor'), split_axis=0, concat_axis=0, t...  11.7 us
    gather x1, local copies, waits for them, and re-layouts, per_device(): arrived.reshape(devices * capacity, 2, page_len, head_dim)[position_at]  11.2 us
  transfers between devices with their start and end apart: 5, of which 5 were waited for; matrix products, arithmetic and copies ran while one was open for 4% of the time, Pallas kernels for 0%

commit v1 on v0

--- a/solution.py
+++ b/solution.py
@@ -3,7 +3,7 @@
 import jax
 import jax.numpy as jnp
 from jax import lax
-from jax.sharding import PartitionSpec as P
+from jax.sharding import Mesh, PartitionSpec as P
 
 KVH = 2
 PROMPT_PAGES = 8
@@ -13,6 +13,8 @@
 EPS = 1e-06
 BIG = 1e30
 HALF_ROOT = 1.0 / math.sqrt(2.0)
+TP = ("tx", "tc")
+ALL = ("dp", "tx", "tc")
 
 
 def norm_rows(values, gain):
@@ -108,10 +110,10 @@
     ple_gain,
 ):
     dp_count = lax.axis_size("dp")
-    tp_count = lax.axis_size("tensor")
+    tp_count = lax.axis_size("tx") * lax.axis_size("tc")
     devices = dp_count * tp_count
     dp_at = lax.axis_index("dp")
-    tp_at = lax.axis_index("tensor")
+    tp_at = lax.axis_index("tx") * lax.axis_size("tc") + lax.axis_index("tc")
     own_rows = hidden_in.shape[0]
     head_dim = q_gain.shape[0]
     local_heads = w_query.shape[1] // head_dim
@@ -137,10 +139,12 @@
         jnp.bfloat16
     )
     picked = jnp.einsum(
-        "dcl,lkhpe->dhckpe", selector, kv_pool, preferred_element_type=jnp.float32
+        "dcl,lkhpe->dhkcpe", selector, kv_pool, preferred_element_type=jnp.float32
     ).astype(jnp.bfloat16)
-    outgoing = jnp.repeat(picked, sharing, axis=1).reshape(devices, capacity, 2, page_len, head_dim)
-    arrived = lax.all_to_all(outgoing, ("dp", "tensor"), split_axis=0, concat_axis=0, tiled=True)
+    outgoing = jnp.broadcast_to(
+        picked[:, :, None], (dp_count, KVH, sharing // 2, 2, capacity, page_len, head_dim)
+    ).reshape(devices, capacity, page_len, head_dim)
+    arrived = lax.all_to_all(outgoing, ALL, split_axis=0, concat_axis=0, tiled=True)
     own_used = lax.dynamic_index_in_dim(group_used, dp_at, 0, keepdims=False)
     own_table = lax.dynamic_index_in_dim(group_table, dp_at, 0, keepdims=False)
     every_page = jnp.arange(devices * pool_dev, dtype=jnp.int32)
@@ -149,10 +153,11 @@
         jnp.cumsum(present.reshape(devices, pool_dev).astype(jnp.int32), axis=1) - 1
     ).reshape(-1)
     position_at = jnp.where(own_used, own_table // pool_dev * capacity + present_rank[own_table], 0)
-    fetched = arrived.reshape(devices * capacity, 2, page_len, head_dim)[position_at]
-    fetched = fetched.reshape(REQ_DEV, slot_count, 2, page_len, head_dim)
+    fetched = arrived.reshape(devices * capacity, page_len, head_dim)[position_at]
+    fetched = lax.all_gather(fetched, "tc", axis=0, tiled=False)
+    fetched = fetched.reshape(2, REQ_DEV, slot_count * page_len, head_dim)
     own_lengths = lax.dynamic_slice_in_dim(cached_len, dp_at * REQ_DEV, REQ_DEV, 0)
-    gathered = lax.all_gather(hidden_in, "tensor", axis=0, tiled=True)
+    gathered = lax.all_gather(hidden_in, TP, axis=0, tiled=True)
     token_count = gathered.shape[0]
     new_count = token_count // REQ_DEV
     normed = norm_rows(gathered.astype(jnp.float32), norm_in).astype(jnp.bfloat16)
@@ -175,8 +180,8 @@
         pieces.append(
             attend(
                 queries[lower : lower + new_count],
-                fetched[request, :, 0].reshape(-1, head_dim),
-                fetched[request, :, 1].reshape(-1, head_dim),
+                fetched[0, request],
+                fetched[1, request],
                 fresh_keys[lower : lower + new_count],
                 fresh_values[lower : lower + new_count],
                 own_lengths[request],
@@ -185,20 +190,20 @@
     attended = jnp.concatenate(pieces, axis=0)
     own_x = hidden_in.astype(jnp.float32)
     projected = lax.psum_scatter(
-        jnp.dot(attended, w_out, preferred_element_type=jnp.float32),
-        "tensor",
+        jnp.dot(attended, w_out, preferred_element_type=jnp.float32).astype(jnp.bfloat16),
+        TP,
         scatter_dimension=0,
         tiled=True,
-    )
+    ).astype(jnp.float32)
     own_normed = lax.dynamic_slice_in_dim(normed, tp_at * own_rows, own_rows, 0)
     mixed_rows = residual_mix(
         own_x, projected, own_normed, post_attn_gain, laurel_left, laurel_right, laurel_gain
     )
     ffn_in = norm_rows(mixed_rows, pre_ffn_gain).astype(jnp.bfloat16)
-    hidden = geglu(lax.all_gather(ffn_in, "tensor", axis=0, tiled=True), w_gate, w_up)
+    hidden = geglu(lax.all_gather(ffn_in, TP, axis=0, tiled=True), w_gate, w_up)
     down = lax.psum_scatter(
         jnp.dot(hidden, w_down, preferred_element_type=jnp.float32).astype(jnp.bfloat16),
-        "tensor",
+        TP,
         scatter_dimension=0,
         tiled=True,
     ).astype(jnp.float32)
@@ -214,31 +219,35 @@
 
 
 def solution(mesh):
+    cores = 2
+    split = Mesh(
+        mesh.devices.reshape(mesh.shape["dp"], mesh.shape["tensor"] // cores, cores),
+        ("dp", "tx", "tc"),
+    )
+    rows = P(ALL, None)
     placed = (
-        P(("dp", "tensor"), None),
-        P(("dp", "tensor"), None),
-        P(),
-        P(),
-        P(("dp", "tensor"), None, None, None, None),
-        P(),
-        P(None, "tensor"),
-        P(),
-        P(),
-        P(),
-        P("tensor", None),
-        P(),
-        P(),
-        P(),
-        P(),
-        P(),
-        P(None, "tensor"),
-        P(None, "tensor"),
-        P("tensor", None),
-        P(),
-        P(),
-        P(),
-        P(),
-    )
-    return jax.shard_map(
-        per_device, mesh=mesh, in_specs=placed, out_specs=P(("dp", "tensor"), None), check_vma=False
-    )
+        rows,
+        rows,
+        P(),
+        P(),
+        P(ALL, None, None, None, None),
+        P(),
+        P(None, TP),
+        P(),
+        P(),
+        P(),
+        P(TP, None),
+        P(),
+        P(),
+        P(),
+        P(),
+        P(),
+        P(None, TP),
+        P(None, TP),
+        P(TP, None),
+        P(),
+        P(),
+        P(),
+        P(),
+    )
+    return jax.shard_map(per_device, mesh=split, in_specs=placed, out_specs=rows, check_vma=False)

time: 475 us -> 344 us (0.72)
  waiting for transfers between devices: 342 us -> 220 us
  local copies, waits for them, and re-layouts: 28.7 us -> 20 us
    all_gather x2 -> x3, waiting for transfers between devices: 96 us -> 31.5 us  [the longest x1 31 us: per_device(): hidden = geglu(lax.all_gather(ffn_in, TP, axis=0, tiled=True), w_gate, w_up)]
    all_to_all x1, waiting for transfers between devices: 141 us -> 112 us  [per_device(): lax.all_to_all(outgoing, ALL, split_axis=0, concat_axis=0, tiled=True)]
    reduce_scatter x1, waiting for transfers between devices: 65.8 us -> 37.4 us  [per_device(): lax.psum_scatter(jnp.dot(attended, w_out, preferred_element_type=jnp.floa...]
    gather x1, local copies, waits for them, and re-layouts: 11.2 us -> 6.15 us  [per_device(): arrived.reshape(devices * capacity, page_len, head_dim)[position_at]]
  transfers between devices with their start and end apart: 5 -> 6, of which waited for: 5 -> 5; matrix products, arithmetic and copies ran while one was open for 4% -> 7% of each run, Pallas kernels for 0% -> 0%
where the time goes in v1:
time: 344 us; the launch traced here: 343 us
  waiting for transfers between devices  220 us (64%)
  matrix products  53.3 us (15%)
  other arithmetic  24.4 us (7%)
  local copies, waits for them, and re-layouts  20 us (6%)
  between operations  13.6 us (4%)
  starting transfers between devices  11.9 us (3%)
    all_to_all x1, waiting for transfers between devices, per_device(): lax.all_to_all(outgoing, ALL, split_axis=0, concat_axis=0, tiled=True)  112 us
    reduce_scatter x1, waiting for transfers between devices, per_device(): lax.psum_scatter(jnp.dot(hidden, w_down, preferred_element_type=jnp.float...  38.1 us
    reduce_scatter x1, waiting for transfers between devices, per_device(): lax.psum_scatter(jnp.dot(attended, w_out, preferred_element_type=jnp.floa...  37.4 us
    all_gather x1, waiting for transfers between devices, per_device(): hidden = geglu(lax.all_gather(ffn_in, TP, axis=0, tiled=True), w_gate, w_up)  31 us
    dot_general x1, matrix products, per_device(): jnp.dot(hidden, w_down, preferred_element_type=jnp.float32)  15.6 us
    all_to_all x1, starting transfers between devices, per_device(): lax.all_to_all(outgoing, ALL, split_axis=0, concat_axis=0, tiled=True)  11.7 us
    dot_general x1, matrix products, geglu(): gate_part = jnp.dot(block, w_gate, preferred_element_type=jnp.float32)  9.93 us
    reduce_sum x4, other arithmetic, norm_rows(): jnp.mean(values * values, axis=-1, keepdims=True) + EPS  7.72 us
  transfers between devices with their start and end apart: 6, of which 5 were waited for; matrix products, arithmetic and copies ran while one was open for 7% of the time, Pallas kernels for 0%

profile of v1, /device:TPU:0, one launch (start us, length us, event | category | flops | bytes accessed | tf_op | source)
XLA Modules:
  0.0 342.9 jit_solution(809030590771143652)
XLA Ops:
  6.5 0.8 and_select_fusion.1
  7.5 0.8 eq.39
  8.4 0.4 and_reduce_fusion
  9.0 4.7 %convert_bitcast_fusion = bf16[16,2,2,128,256]{4,0,3,1,2:T(8,128)(2,1)S(1)} fusion(bf16[16,2,2,128,256]{4,3,2,1,0:T(8,128)(2,1)} %param.27, pred[16,16]{1,0:T(8,128)(4,1)S(1)} %and_reduce_fusion, s32[16,16]{1,0:T(8,128)S(1)} %reduce_window_sum.22), kind=kOutput, calls=%fused_computation.33 | convolution fusion | flops 69206784 | bytes 8389888 | tf_op jit(solution)/shard_map/dcl,lkhpe->dhkcpe/dot_general | solution.py:141
  13.8 1.5 copy.35
  15.2 4.3 %broadcast_in_dim.29 = bf16[16,2,2,2,128,256]{5,4,3,2,1,0:T(8,128)(2,1)} broadcast(bf16[16,2,2,128,256]{4,3,2,1,0:T(8,128)(2,1)S(1)} %copy.35), dimensions={0,1,3,4,5} | broadcast | bytes 12582912 | tf_op jit(solution)/shard_map/broadcast_in_dim | solution.py:144
  19.5 11.7 %all-to-all-start = ((bf16[128,1,128,256]{3,2,1,0:T(8,128)(2,1)}), bf16[128,1,128,256]{3,2,1,0:T(8,128)(2,1)}, u32[]{:S(2)}, u32[]{:S(2)}) async-start(bf16[128,1,128,256]{3,2,1,0:T(8,128)(2,1)} %bitcast.182), calls=%async_computation | async-start | bytes 16777216 | tf_op jit(solution)/shard_map/all_to_all | solution.py:147
  31.3 0.7 all-gather.5.cloned.1.call-update
  32.7 0.8 gather_fusion
  33.5 112.1 %all-to-all-done = bf16[128,1,128,256]{3,2,1,0:T(8,128)(2,1)} async-done(((bf16[128,1,128,256]{3,2,1,0:T(8,128)(2,1)}), bf16[128,1,128,256]{3,2,1,0:T(8,128)(2,1)}, u32[]{:S(2)}, u32[]{:S(2)}) %all-to-all-start) | async-done | bytes 8388640 | tf_op jit(solution)/shard_map/all_to_all | solution.py:147
  145.6 6.2 %gather_fusion.1 = bf16[64,128,256]{2,1,0:T(8,128)(2,1)} fusion(bf16[128,128,256]{2,1,0:T(8,128)(2,1)} %bitcast.7, s32[1024]{0:T(1024)S(1)} %pad_clamp_fusion), kind=kCustom, calls=%fused_computation.1 | custom fusion | bytes 8388864 | tf_op jit(solution)/shard_map/gather | solution.py:156
  151.9 0.6 copy-done.21
  152.6 0.6 fusion.148
  153.1 0.7 iota_compare_fusion.3
  153.8 0.6 iota_compare_fusion.2
  154.4 3.2 fusion
  157.7 0.5 copy-done.1
  158.2 1.0 fusion.2
  159.2 1.8 copy-done.19
  161.1 1.3 multiply_reduce_fusion.4
  162.4 0.8 copy-done.20
  163.3 1.3 multiply_reduce_fusion.5
  164.9 2.6 fusion.62
  168.5 1.4 multiply_reduce_fusion.3
  169.9 0.9 multiply_convert_fusion.1
  170.8 0.4 all-gather.9.cloned.1.call-done
  171.2 2.7 fusion.3
  174.1 2.4 fusion.5
  176.6 0.9 copy-done.4
  177.5 2.4 fusion.18
  179.9 1.3 fusion.4
  181.4 2.6 fusion.6
  184.1 2.4 fusion.16
  186.5 0.4 fusion.31
  186.9 0.4 fusion.30
  187.4 3.2 convolution_convert_fusion
  190.7 2.0 multiply_reduce_fusion.2
  192.7 37.4 %reduce-scatter.3.cloned.1.call-done = bf16[128,2048]{1,0:T(8,128)(2,1)} async-done(((bf16[1024,2048]{1,0:T(8,128)(2,1)}), bf16[128,2048]{1,0:T(8,128)(2,1)}) %reduce-scatter.3.cloned.1.call-update) | async-done | bytes 524304 | tf_op jit(solution)/shard_map/reduce_scatter | solution.py:192
  230.1 1.2 fusion.33
  231.3 2.0 multiply_reduce_fusion.1
  233.3 0.9 multiply_convert_fusion
  234.3 31.0 %all-gather.7.cloned.1.call-done = bf16[1024,2048]{1,0:T(8,128)(2,1)} async-done(((bf16[128,2048]{1,0:T(8,128)(2,1)}), bf16[1024,2048]{1,0:T(8,128)(2,1)}) %all-gather.7.cloned.1.call-update) | async-done | bytes 4194320 | tf_op jit(solution)/shard_map/all_gather | solution.py:203
  265.4 9.9 %fusion.155 = f32[1024,1024]{1,0:T(8,128)} fusion(bf16[1024,2048]{1,0:T(8,128)(2,1)} %all-gather.7.cloned.1.call-done, bf16[2048,1024]{1,0:T(8,128)(2,1)} %param.39), kind=kOutput, calls=%fused_computation.218 | convolution fusion | flops 4294967296 | bytes 12582912 | tf_op jit(solution)/shard_map/dot_general | solution.py:82
  275.3 15.6 %convolution_convert_fusion.1 = bf16[1024,2048]{1,0:T(8,128)(2,1)} fusion(bf16[1024,2048]{1,0:T(8,128)(2,1)} %param.41, f32[1024,1024]{1,0:T(8,128)} %fusion.155, bf16[1024,2048]{1,0:T(8,128)(2,1)} %all-gather.7.cloned.1.call-done, bf16[2048,1024]{1,0:T(8,128)(2,1)} %param.40), kind=kOutput, calls=%fused_computation.35 | convolution fusion | flops 8602517504 | bytes 20971520 | tf_op jit(solution)/shard_map/dot_general | solution.py:205
  291.0 38.1 %reduce-scatter.5.cloned.1.call-done = bf16[128,2048]{1,0:T(8,128)(2,1)} async-done(((bf16[1024,2048]{1,0:T(8,128)(2,1)}), bf16[128,2048]{1,0:T(8,128)(2,1)}) %reduce-scatter.5.cloned.1.call-update) | async-done | bytes 524304 | tf_op jit(solution)/shard_map/reduce_scatter | solution.py:204
  329.0 1.3 fusion.37
  330.4 3.5 %multiply_reduce_fusion = (f32[128]{0:T(128)S(1)}, f32[128,2048]{1,0:T(8,128)}) fusion(bf16[256,2048]{1,0:T(8,128)(2,1)} %param.44, bf16[2048,256]{1,0:T(8,128)(2,1)} %param.43, bf16[128,2048]{1,0:T(8,128)(2,1)} %reduce-scatter.5.cloned.1.call-done, f32[128,2048]{1,0:T(8,128)S(1)} %get-tuple-element.6, f32[2048]{0:T(1024)S(1)} %copy-done.11, ...), kind=kOutput, calls=%fused_computation.66 | convolution fusion | flops 270892928 | bytes 4793344 | tf_op jit(solution)/shard_map/dot_general | solution.py:217
  333.9 2.5 add_convert_fusion
  (96 shorter events, 3.5 us)
Async XLA Ops:
  6.5 180.8 %copy-start = (bf16[256,2048]{1,0:T(8,128)(2,1)S(1)}, bf16[256,2048]{1,0:T(8,128)(2,1)}, u32[]{:S(2)}) copy-start(bf16[256,2048]{1,0:T(8,128)(2,1)} %param.33) | copy-start | bytes 3145732
  19.5 126.1 %all-to-all-start = ((bf16[128,1,128,256]{3,2,1,0:T(8,128)(2,1)}), bf16[128,1,128,256]{3,2,1,0:T(8,128)(2,1)}, u32[]{:S(2)}, u32[]{:S(2)}) async-start(bf16[128,1,128,256]{3,2,1,0:T(8,128)(2,1)} %bitcast.182), calls=%async_computation | async-start | bytes 16777216 | tf_op jit(solution)/shard_map/all_to_all | solution.py:147
  31.2 123.2 %all-gather.5.cloned.1.call-start = ((), (), s32[]{:S(2)}) async-start(), calls=%async_computation.3 | async-start | bytes 4718592 | tf_op jit(solution)/shard_map/all_gather | solution.py:160
  32.0 139.2 %all-gather.9.cloned.1.call-start = ((), (), s32[]{:S(2)}) async-start(), calls=%async_computation.7 | async-start | bytes 12582912 | tf_op jit(solution)/shard_map/all_gather | solution.py:157
  151.8 0.7 copy-start.21
  151.8 5.9 %copy-start.12 = (f32[2048]{0:T(1024)S(1)}, f32[2048]{0:T(1024)}, u32[]{:S(2)}) copy-start(f32[2048]{0:T(1024)} %param.28) | copy-start | bytes 24580
  151.8 78.3 %reduce-scatter.3.cloned.1.call-start = ((), (), s32[]{:S(2)}) async-start(), calls=%async_computation.4 | async-start | bytes 4718592 | tf_op jit(solution)/shard_map/reduce_scatter | solution.py:192
  154.4 3.8 %copy-start.1 = (bf16[1024,2048]{1,0:T(8,128)(2,1)S(1)}, bf16[1024,2048]{1,0:T(8,128)(2,1)}, u32[]{:S(2)}) copy-start(bf16[1024,2048]{1,0:T(8,128)(2,1)} %all-gather.5.cloned.1.call-done) | copy-start | bytes 12582916
  158.2 2.9 copy-start.19
  161.1 7.4 %copy-start.2 = (bf16[1024,2048]{1,0:T(8,128)(2,1)}, bf16[1024,2048]{1,0:T(8,128)(2,1)S(1)}, u32[]{:S(2)}) copy-start(bf16[1024,2048]{1,0:T(8,128)(2,1)S(1)} %fusion.2) | copy-start | bytes 12582916
  161.1 2.2 copy-start.20
  163.3 1.4 copy-start.17
  163.3 1.4 copy-start.18
  167.5 0.7 copy-start.5
  174.1 3.4 copy-start.4
  177.5 2.4 copy-start.6
  184.1 2.5 copy-start.7
  187.3 3.3 copy-start.8
  187.4 3.3 copy-start.9
  190.6 40.7 %copy-start.13 = (f32[2048]{0:T(1024)S(1)}, f32[2048]{0:T(1024)}, u32[]{:S(2)}) copy-start(f32[2048]{0:T(1024)} %param.37) | copy-start | bytes 24580
  190.6 40.7 %copy-start.14 = (f32[2048]{0:T(1024)S(1)}, f32[2048]{0:T(1024)}, u32[]{:S(2)}) copy-start(f32[2048]{0:T(1024)} %param.34) | copy-start | bytes 24580
  190.6 42.7 %copy-start.15 = (f32[2048]{0:T(1024)S(1)}, f32[2048]{0:T(1024)}, u32[]{:S(2)}) copy-start(f32[2048]{0:T(1024)} %param.38) | copy-start | bytes 24580
  190.6 74.7 %all-gather.7.cloned.1.call-start = ((), (), s32[]{:S(2)}) async-start(), calls=%async_computation.5 | async-start | bytes 4718592 | tf_op jit(solution)/shard_map/all_gather | solution.py:203
  234.3 94.7 %reduce-scatter.5.cloned.1.call-start = ((), (), s32[]{:S(2)}) async-start(), calls=%async_computation.6 | async-start | bytes 4718592 | tf_op jit(solution)/shard_map/reduce_scatter | solution.py:204
  290.9 39.4 %copy-start.10 = (bf16[128,256]{1,0:T(8,128)(2,1)S(1)}, bf16[128,256]{1,0:T(8,128)(2,1)}, u32[]{:S(2)}) copy-start(bf16[128,256]{1,0:T(8,128)(2,1)} %param.24) | copy-start | bytes 196612
  290.9 39.4 %copy-start.11 = (f32[2048]{0:T(1024)S(1)}, f32[2048]{0:T(1024)}, u32[]{:S(2)}) copy-start(f32[2048]{0:T(1024)} %param.42) | copy-start | bytes 24580
  290.9 43.0 %copy-start.16 = (f32[2048]{0:T(1024)S(1)}, f32[2048]{0:T(1024)}, u32[]{:S(2)}) copy-start(f32[2048]{0:T(1024)} %param.45) | copy-start | bytes 24580
  329.0 4.9 %copy-start.3 = (bf16[128,2048]{1,0:T(8,128)(2,1)S(1)}, bf16[128,2048]{1,0:T(8,128)(2,1)}, u32[]{:S(2)}) copy-start(bf16[128,2048]{1,0:T(8,128)(2,1)} %reduce-scatter.5.cloned.1.call-done) | copy-start | bytes 1572868
Sparse Core Ops, SparseCore 0:
  33.7 66.7 all-gather.4
  151.9 19.2 all-gather.8
  190.7 39.2 reduce-scatter.2
  234.4 30.9 all-gather.6
  291.1 37.9 reduce-scatter.4

commit v2 on v1

--- a/solution.py
+++ b/solution.py
@@ -82,6 +82,30 @@
     gate_part = jnp.dot(block, w_gate, preferred_element_type=jnp.float32)
     up_part = jnp.dot(block, w_up, preferred_element_type=jnp.float32)
     return (jax.nn.gelu(gate_part, approximate=True) * up_part).astype(jnp.bfloat16)
+
+
+def gather_rows(rows):
+    rows = lax.all_gather(rows, "tx", axis=0, tiled=True)
+    return lax.all_gather(rows, "tc", axis=0, tiled=True)
+
+
+def scatter_rows(rows):
+    rows = lax.psum_scatter(rows, "tc", scatter_dimension=0, tiled=True)
+    return lax.psum_scatter(rows, "tx", scatter_dimension=0, tiled=True)
+
+
+def natural_order(rows):
+    chips = lax.axis_size("tx")
+    cores = lax.axis_size("tc")
+    block = rows.reshape(cores, chips, -1, *rows.shape[1:])
+    return jnp.swapaxes(block, 0, 1).reshape(rows.shape)
+
+
+def chip_order(rows):
+    chips = lax.axis_size("tx")
+    cores = lax.axis_size("tc")
+    block = rows.reshape(chips, cores, -1, *rows.shape[1:])
+    return jnp.swapaxes(block, 0, 1).reshape(rows.shape)
 
 
 def per_device(
@@ -157,7 +181,8 @@
     fetched = lax.all_gather(fetched, "tc", axis=0, tiled=False)
     fetched = fetched.reshape(2, REQ_DEV, slot_count * page_len, head_dim)
     own_lengths = lax.dynamic_slice_in_dim(cached_len, dp_at * REQ_DEV, REQ_DEV, 0)
-    gathered = lax.all_gather(hidden_in, TP, axis=0, tiled=True)
+    gathered = gather_rows(hidden_in)
+    gathered = natural_order(gathered)
     token_count = gathered.shape[0]
     new_count = token_count // REQ_DEV
     normed = norm_rows(gathered.astype(jnp.float32), norm_in).astype(jnp.bfloat16)
@@ -187,25 +212,19 @@
                 own_lengths[request],
             )
         )
-    attended = jnp.concatenate(pieces, axis=0)
+    attended = chip_order(jnp.concatenate(pieces, axis=0))
     own_x = hidden_in.astype(jnp.float32)
-    projected = lax.psum_scatter(
-        jnp.dot(attended, w_out, preferred_element_type=jnp.float32).astype(jnp.bfloat16),
-        TP,
-        scatter_dimension=0,
-        tiled=True,
+    projected = scatter_rows(
+        jnp.dot(attended, w_out, preferred_element_type=jnp.float32).astype(jnp.bfloat16)
     ).astype(jnp.float32)
     own_normed = lax.dynamic_slice_in_dim(normed, tp_at * own_rows, own_rows, 0)
     mixed_rows = residual_mix(
         own_x, projected, own_normed, post_attn_gain, laurel_left, laurel_right, laurel_gain
     )
     ffn_in = norm_rows(mixed_rows, pre_ffn_gain).astype(jnp.bfloat16)
-    hidden = geglu(lax.all_gather(ffn_in, TP, axis=0, tiled=True), w_gate, w_up)
-    down = lax.psum_scatter(
-        jnp.dot(hidden, w_down, preferred_element_type=jnp.float32).astype(jnp.bfloat16),
-        TP,
-        scatter_dimension=0,
-        tiled=True,
+    hidden = geglu(gather_rows(ffn_in), w_gate, w_up)
+    down = scatter_rows(
+        jnp.dot(hidden, w_down, preferred_element_type=jnp.float32).astype(jnp.bfloat16)
     ).astype(jnp.float32)
     settled = mixed_rows + norm_rows(down, post_ffn_gain)
     settled_half = settled.astype(jnp.bfloat16)

time: 344 us -> 385 us (1.12)
  waiting for transfers between devices: 220 us -> 258 us
  local copies, waits for them, and re-layouts: 20 us -> 24.6 us
    all_gather x2 -> x4, waiting for transfers between devices: 31.1 us -> 116 us  [the longest x2 97.8 us: gather_rows(): rows = lax.all_gather(rows, 'tx', axis=0, tiled=True)]
    all_to_all x1, waiting for transfers between devices: 112 us -> 44.8 us  [per_device(): lax.all_to_all(outgoing, ALL, split_axis=0, concat_axis=0, tiled=True)]
    reduce_scatter x2 -> x4, waiting for transfers between devices: 75.5 us -> 96.7 us  [the longest x2 64.8 us: scatter_rows(): return lax.psum_scatter(rows, 'tx', scatter_dimension=0, tiled=True)]
  transfers between devices with their start and end apart: 6 -> 10, of which waited for: 5 -> 8; matrix products, arithmetic and copies ran while one was open for 7% -> 7% of each run, Pallas kernels for 0% -> 0%
where the time goes in v2:
time: 385 us; the launch traced here: 384 us
  waiting for transfers between devices  258 us (67%)
  matrix products  53.3 us (14%)
  local copies, waits for them, and re-layouts  24.6 us (6%)
  other arithmetic  21.7 us (6%)
  between operations  13.7 us (4%)
  starting transfers between devices  12.2 us (3%)
    all_gather x2, waiting for transfers between devices, gather_rows(): rows = lax.all_gather(rows, 'tx', axis=0, tiled=True)  97.8 us
    reduce_scatter x2, waiting for transfers between devices, scatter_rows(): return lax.psum_scatter(rows, 'tx', scatter_dimension=0, tiled=True)  64.8 us
    all_to_all x1, waiting for transfers between devices, per_device(): lax.all_to_all(outgoing, ALL, split_axis=0, concat_axis=0, tiled=True)  44.8 us
    reduce_scatter x2, waiting for transfers between devices, scatter_rows(): rows = lax.psum_scatter(rows, 'tc', scatter_dimension=0, tiled=True)  31.9 us
    all_gather x2, waiting for transfers between devices, gather_rows(): return lax.all_gather(rows, 'tc', axis=0, tiled=True)  18 us
    dot_general x1, matrix products, per_device(): jnp.dot(hidden, w_down, preferred_element_type=jnp.float32)  15.7 us
    all_to_all x1, starting transfers between devices, per_device(): lax.all_to_all(outgoing, ALL, split_axis=0, concat_axis=0, tiled=True)  11.7 us
    dot_general x1, matrix products, geglu(): gate_part = jnp.dot(block, w_gate, preferred_element_type=jnp.float32)  9.93 us
  transfers between devices with their start and end apart: 10, of which 8 were waited for; matrix products, arithmetic and copies ran while one was open for 7% of the time, Pallas kernels for 0%

profile of v2, /device:TPU:0, one launch (start us, length us, event | category | flops | bytes accessed | tf_op | source)
XLA Modules:
  0.0 383.5 jit_solution(10133942663322913670)
XLA Ops:
  6.5 0.8 and_select_fusion.1
  7.5 0.8 eq.39
  9.0 4.7 %convert_bitcast_fusion = bf16[16,2,2,128,256]{4,0,3,1,2:T(8,128)(2,1)S(1)} fusion(bf16[16,2,2,128,256]{4,3,2,1,0:T(8,128)(2,1)} %param.27, pred[16,16]{1,0:T(8,128)(4,1)S(1)} %and_reduce_fusion, s32[16,16]{1,0:T(8,128)S(1)} %reduce_window_sum.22), kind=kOutput, calls=%fused_computation.32 | convolution fusion | flops 69206784 | bytes 8389888 | tf_op jit(solution)/shard_map/dcl,lkhpe->dhkcpe/dot_general | solution.py:165
  13.8 1.5 copy.48
  15.2 4.3 %broadcast_in_dim.29 = bf16[16,2,2,2,128,256]{5,4,3,2,1,0:T(8,128)(2,1)} broadcast(bf16[16,2,2,128,256]{4,3,2,1,0:T(8,128)(2,1)S(1)} %copy.48), dimensions={0,1,3,4,5} | broadcast | bytes 12582912 | tf_op jit(solution)/shard_map/broadcast_in_dim | solution.py:168
  19.5 11.7 %all-to-all-start = ((bf16[128,1,128,256]{3,2,1,0:T(8,128)(2,1)}), bf16[128,1,128,256]{3,2,1,0:T(8,128)(2,1)}, u32[]{:S(2)}, u32[]{:S(2)}) async-start(bf16[128,1,128,256]{3,2,1,0:T(8,128)(2,1)} %bitcast.202), calls=%async_computation | async-start | bytes 16777216 | tf_op jit(solution)/shard_map/all_to_all | solution.py:171
  31.3 0.7 all-gather.7.cloned.1.call-update
  32.0 67.2 %all-gather.7.cloned.1.call-done = bf16[512,2048]{1,0:T(8,128)(2,1)} async-done(((bf16[128,2048]{1,0:T(8,128)(2,1)}), bf16[512,2048]{1,0:T(8,128)(2,1)}) %all-gather.7.cloned.1.call-update) | async-done | bytes 2097168 | tf_op jit(solution)/shard_map/all_gather | solution.py:88
  100.0 0.8 gather_fusion
  100.8 44.8 %all-to-all-done = bf16[128,1,128,256]{3,2,1,0:T(8,128)(2,1)} async-done(((bf16[128,1,128,256]{3,2,1,0:T(8,128)(2,1)}), bf16[128,1,128,256]{3,2,1,0:T(8,128)(2,1)}, u32[]{:S(2)}, u32[]{:S(2)}) %all-to-all-start) | async-done | bytes 8388640 | tf_op jit(solution)/shard_map/all_to_all | solution.py:171
  145.6 6.2 %gather_fusion.1 = bf16[64,128,256]{2,1,0:T(8,128)(2,1)} fusion(bf16[128,128,256]{2,1,0:T(8,128)(2,1)} %bitcast.7, s32[1024]{0:T(1024)S(1)} %pad_clamp_fusion), kind=kCustom, calls=%fused_computation.1 | custom fusion | bytes 8388864 | tf_op jit(solution)/shard_map/gather | solution.py:180
  152.6 0.6 fusion.143
  153.1 0.7 iota_compare_fusion.3
  153.8 0.6 iota_compare_fusion.2
  154.4 3.4 copy.51
  158.2 0.9 multiply_reduce_fusion
  159.1 0.7 fusion.1
  159.9 2.2 copy-done.19
  162.1 1.4 multiply_reduce_fusion.5
  163.5 0.8 copy-done.20
  164.3 1.3 multiply_reduce_fusion.6
  165.9 2.6 fusion.61
  169.6 1.3 multiply_reduce_fusion.4
  171.0 0.9 multiply_convert_fusion.1
  171.9 2.7 fusion.2
  174.8 2.4 fusion.4
  177.2 0.9 copy-done.4
  178.2 2.4 fusion.17
  180.6 1.3 fusion.3
  182.1 2.4 fusion.5
  184.5 2.4 fusion.15
  188.2 0.8 copy.53
  189.0 3.2 convolution_convert_fusion
  192.3 15.6 %reduce-scatter.5.cloned.1.call-done = bf16[512,2048]{1,0:T(8,128)(2,1)} async-done(((bf16[1024,2048]{1,0:T(8,128)(2,1)}), bf16[512,2048]{1,0:T(8,128)(2,1)}) %reduce-scatter.5.cloned.1.call-update) | async-done | bytes 2097168 | tf_op jit(solution)/shard_map/reduce_scatter | solution.py:93
  208.0 2.0 multiply_reduce_fusion.3
  210.0 31.3 %reduce-scatter.7.cloned.1.call-done = bf16[128,2048]{1,0:T(8,128)(2,1)} async-done(((bf16[512,2048]{1,0:T(8,128)(2,1)}), bf16[128,2048]{1,0:T(8,128)(2,1)}) %reduce-scatter.7.cloned.1.call-update) | async-done | bytes 524304 | tf_op jit(solution)/shard_map/reduce_scatter | solution.py:94
  241.3 1.2 fusion.32
  242.5 2.0 multiply_reduce_fusion.2
  244.5 0.9 multiply_convert_fusion
  245.5 30.6 %all-gather.11.cloned.1.call-done = bf16[512,2048]{1,0:T(8,128)(2,1)} async-done(((bf16[128,2048]{1,0:T(8,128)(2,1)}), bf16[512,2048]{1,0:T(8,128)(2,1)}) %all-gather.11.cloned.1.call-update) | async-done | bytes 2097168 | tf_op jit(solution)/shard_map/all_gather | solution.py:88
  276.2 18.0 %all-gather.13.cloned.1.call-done = bf16[1024,2048]{1,0:T(8,128)(2,1)} async-done(((bf16[512,2048]{1,0:T(8,128)(2,1)}), bf16[1024,2048]{1,0:T(8,128)(2,1)}) %all-gather.13.cloned.1.call-update) | async-done | bytes 4194320 | tf_op jit(solution)/shard_map/all_gather | solution.py:89
  294.2 9.9 %fusion.150 = f32[1024,1024]{1,0:T(8,128)} fusion(bf16[1024,2048]{1,0:T(8,128)(2,1)} %all-gather.13.cloned.1.call-done, bf16[2048,1024]{1,0:T(8,128)(2,1)} %param.39), kind=kOutput, calls=%fused_computation.214 | convolution fusion | flops 4294967296 | bytes 12582912 | tf_op jit(solution)/shard_map/dot_general | solution.py:82
  304.1 15.7 %convolution_convert_fusion.1 = bf16[1024,2048]{1,0:T(8,128)(2,1)} fusion(bf16[1024,2048]{1,0:T(8,128)(2,1)} %param.41, f32[1024,1024]{1,0:T(8,128)} %fusion.150, bf16[1024,2048]{1,0:T(8,128)(2,1)} %all-gather.13.cloned.1.call-done, bf16[2048,1024]{1,0:T(8,128)(2,1)} %param.40), kind=kOutput, calls=%fused_computation.34 | convolution fusion | flops 8602517504 | bytes 20971520 | tf_op jit(solution)/shard_map/dot_general | solution.py:227
  319.9 16.3 %reduce-scatter.9.cloned.1.call-done = bf16[512,2048]{1,0:T(8,128)(2,1)} async-done(((bf16[1024,2048]{1,0:T(8,128)(2,1)}), bf16[512,2048]{1,0:T(8,128)(2,1)}) %reduce-scatter.9.cloned.1.call-update) | async-done | bytes 2097168 | tf_op jit(solution)/shard_map/reduce_scatter | solution.py:93
  336.1 33.5 %reduce-scatter.11.cloned.1.call-done = bf16[128,2048]{1,0:T(8,128)(2,1)} async-done(((bf16[512,2048]{1,0:T(8,128)(2,1)}), bf16[128,2048]{1,0:T(8,128)(2,1)}) %reduce-scatter.11.cloned.1.call-update) | async-done | bytes 524304 | tf_op jit(solution)/shard_map/reduce_scatter | solution.py:94
  369.6 1.3 fusion.36
  370.9 3.5 multiply_reduce_fusion.1
  374.5 2.5 add_convert_fusion
  (113 shorter events, 6.3 us)
Async XLA Ops:
  6.5 182.5 %copy-start = (bf16[256,2048]{1,0:T(8,128)(2,1)S(1)}, bf16[256,2048]{1,0:T(8,128)(2,1)}, u32[]{:S(2)}) copy-start(bf16[256,2048]{1,0:T(8,128)(2,1)} %param.33) | copy-start | bytes 3145732
  19.5 126.1 %all-to-all-start = ((bf16[128,1,128,256]{3,2,1,0:T(8,128)(2,1)}), bf16[128,1,128,256]{3,2,1,0:T(8,128)(2,1)}, u32[]{:S(2)}, u32[]{:S(2)}) async-start(bf16[128,1,128,256]{3,2,1,0:T(8,128)(2,1)} %bitcast.202), calls=%async_computation | async-start | bytes 16777216 | tf_op jit(solution)/shard_map/all_to_all | solution.py:171
  31.2 68.0 %all-gather.7.cloned.1.call-start = ((), (), s32[]{:S(2)}) async-start(), calls=%async_computation.5 | async-start | bytes 2621440 | tf_op jit(solution)/shard_map/all_gather | solution.py:88
  32.0 122.4 %all-gather.9.cloned.1.call-start = ((), (), s32[]{:S(2)}) async-start(), calls=%async_computation.6 | async-start | bytes 6291456 | tf_op jit(solution)/shard_map/all_gather | solution.py:89
  99.3 72.6 %all-gather.15.cloned.1.call-start = ((), (), s32[]{:S(2)}) async-start(), calls=%async_computation.13 | async-start | bytes 12582912 | tf_op jit(solution)/shard_map/all_gather | solution.py:181
  151.8 0.7 copy-start.21
  151.8 56.1 %reduce-scatter.5.cloned.1.call-start = ((), (), s32[]{:S(2)}) async-start(), calls=%async_computation.7 | async-start | bytes 6291456 | tf_op jit(solution)/shard_map/reduce_scatter | solution.py:93
  154.4 3.8 copy-start.1
  158.2 0.9 copy-start.12
  159.1 3.0 copy-start.19
  162.1 7.5 %copy-start.2 = (bf16[1024,2048]{1,0:T(8,128)(2,1)}, bf16[1024,2048]{1,0:T(8,128)(2,1)S(1)}, u32[]{:S(2)}) copy-start(bf16[1024,2048]{1,0:T(8,128)(2,1)S(1)} %fusion.1) | copy-start | bytes 12582916
  162.1 2.2 copy-start.20
  164.3 1.3 copy-start.17
  164.3 1.4 copy-start.18
  168.5 0.7 copy-start.5
  174.8 3.4 copy-start.4
  178.2 2.4 copy-start.6
  184.5 2.5 copy-start.7
  192.2 15.8 %copy-start.8 = (bf16[64,2048]{1,0:T(8,128)(2,1)S(1)}, bf16[64,2048]{1,0:T(8,128)(2,1)}, u32[]{:S(2)}) copy-start(bf16[64,2048]{1,0:T(8,128)(2,1)} %param.36) | copy-start | bytes 786436
  192.2 15.8 %copy-start.9 = (bf16[2048,64]{0,1:T(8,128)(2,1)S(1)}, bf16[2048,64]{0,1:T(8,128)(2,1)}, u32[]{:S(2)}) copy-start(bf16[2048,64]{0,1:T(8,128)(2,1)} %param.35) | copy-start | bytes 786436
  192.2 50.3 %copy-start.13 = (f32[2048]{0:T(1024)S(1)}, f32[2048]{0:T(1024)}, u32[]{:S(2)}) copy-start(f32[2048]{0:T(1024)} %param.37) | copy-start | bytes 24580
  192.2 50.3 %copy-start.14 = (f32[2048]{0:T(1024)S(1)}, f32[2048]{0:T(1024)}, u32[]{:S(2)}) copy-start(f32[2048]{0:T(1024)} %param.34) | copy-start | bytes 24580
  192.2 49.0 %reduce-scatter.7.cloned.1.call-start = ((), (), s32[]{:S(2)}) async-start(), calls=%async_computation.8 | async-start | bytes 2621440 | tf_op jit(solution)/shard_map/reduce_scatter | solution.py:94
  207.9 36.6 %copy-start.15 = (f32[2048]{0:T(1024)S(1)}, f32[2048]{0:T(1024)}, u32[]{:S(2)}) copy-start(f32[2048]{0:T(1024)} %param.38) | copy-start | bytes 24580
  207.9 68.2 %all-gather.11.cloned.1.call-start = ((), (), s32[]{:S(2)}) async-start(), calls=%async_computation.9 | async-start | bytes 2621440 | tf_op jit(solution)/shard_map/all_gather | solution.py:88
  245.5 48.7 %all-gather.13.cloned.1.call-start = ((), (), s32[]{:S(2)}) async-start(), calls=%async_computation.10 | async-start | bytes 6291456 | tf_op jit(solution)/shard_map/all_gather | solution.py:89
  276.1 60.0 %reduce-scatter.9.cloned.1.call-start = ((), (), s32[]{:S(2)}) async-start(), calls=%async_computation.11 | async-start | bytes 6291456 | tf_op jit(solution)/shard_map/reduce_scatter | solution.py:93
  319.8 51.2 %copy-start.10 = (bf16[128,256]{1,0:T(8,128)(2,1)S(1)}, bf16[128,256]{1,0:T(8,128)(2,1)}, u32[]{:S(2)}) copy-start(bf16[128,256]{1,0:T(8,128)(2,1)} %param.24) | copy-start | bytes 196612
  319.8 51.2 %copy-start.11 = (f32[2048]{0:T(1024)S(1)}, f32[2048]{0:T(1024)}, u32[]{:S(2)}) copy-start(f32[2048]{0:T(1024)} %param.42) | copy-start | bytes 24580
  319.8 54.7 %copy-start.16 = (f32[2048]{0:T(1024)S(1)}, f32[2048]{0:T(1024)}, u32[]{:S(2)}) copy-start(f32[2048]{0:T(1024)} %param.45) | copy-start | bytes 24580
  319.8 49.8 %reduce-scatter.11.cloned.1.call-start = ((), (), s32[]{:S(2)}) async-start(), calls=%async_computation.12 | async-start | bytes 2621440 | tf_op jit(solution)/shard_map/reduce_scatter | solution.py:94
  369.6 4.9 %copy-start.3 = (bf16[128,2048]{1,0:T(8,128)(2,1)S(1)}, bf16[128,2048]{1,0:T(8,128)(2,1)}, u32[]{:S(2)}) copy-start(bf16[128,2048]{1,0:T(8,128)(2,1)} %reduce-scatter.11.cloned.1.call-done) | copy-start | bytes 1572868
Sparse Core Ops, SparseCore 0:
  33.7 65.5 all-gather.6
  100.9 16.9 all-gather.8
  151.9 19.2 all-gather.14
  192.4 15.5 reduce-scatter.4
  210.2 31.0 reduce-scatter.6
  245.6 30.4 all-gather.10
  277.8 16.3 all-gather.12
  319.9 16.1 reduce-scatter.8
  338.5 31.0 reduce-scatter.10

commit v3 on v1

--- a/solution.py
+++ b/solution.py
@@ -138,12 +138,14 @@
     selector = (wanted[:, None, :] & (wanted_rank[:, None, :] == slot_ids[None, :, None])).astype(
         jnp.bfloat16
     )
-    picked = jnp.einsum(
-        "dcl,lkhpe->dhkcpe", selector, kv_pool, preferred_element_type=jnp.float32
-    ).astype(jnp.bfloat16)
-    outgoing = jnp.broadcast_to(
-        picked[:, :, None], (dp_count, KVH, sharing // 2, 2, capacity, page_len, head_dim)
-    ).reshape(devices, capacity, page_len, head_dim)
+    local_ids = jnp.arange(pool_dev, dtype=jnp.int32)
+    picked_id = jnp.sum(jnp.where(selector > 0, local_ids[None, None, :], 0), axis=-1)
+    head_ids = jnp.arange(KVH, dtype=jnp.int32)[None, :, None, None, None]
+    copy_ids = jnp.zeros((1, 1, sharing // 2, 1, 1), jnp.int32)
+    kind_ids = jnp.arange(2, dtype=jnp.int32)[None, None, None, :, None]
+    row_ids = (picked_id[:, None, None, None, :] * 2 + kind_ids) * KVH + head_ids + copy_ids
+    outgoing = kv_pool.reshape(pool_dev * 2 * KVH, page_len, head_dim)[row_ids.reshape(-1)]
+    outgoing = outgoing.reshape(devices, capacity, page_len, head_dim)
     arrived = lax.all_to_all(outgoing, ALL, split_axis=0, concat_axis=0, tiled=True)
     own_used = lax.dynamic_index_in_dim(group_used, dp_at, 0, keepdims=False)
     own_table = lax.dynamic_index_in_dim(group_table, dp_at, 0, keepdims=False)
@@ -154,8 +156,10 @@
     ).reshape(-1)
     position_at = jnp.where(own_used, own_table // pool_dev * capacity + present_rank[own_table], 0)
     fetched = arrived.reshape(devices * capacity, page_len, head_dim)[position_at]
-    fetched = lax.all_gather(fetched, "tc", axis=0, tiled=False)
-    fetched = fetched.reshape(2, REQ_DEV, slot_count * page_len, head_dim)
+    other = lax.ppermute(fetched, "tc", perm=[(0, 1), (1, 0)])
+    holds_keys = lax.axis_index("tc") == 0
+    cache_keys = jnp.where(holds_keys, fetched, other).reshape(REQ_DEV, -1, head_dim)
+    cache_values = jnp.where(holds_keys, other, fetched).reshape(REQ_DEV, -1, head_dim)
     own_lengths = lax.dynamic_slice_in_dim(cached_len, dp_at * REQ_DEV, REQ_DEV, 0)
     gathered = lax.all_gather(hidden_in, TP, axis=0, tiled=True)
     token_count = gathered.shape[0]
@@ -180,8 +184,8 @@
         pieces.append(
             attend(
                 queries[lower : lower + new_count],
-                fetched[0, request],
-                fetched[1, request],
+                cache_keys[request],
+                cache_values[request],
                 fresh_keys[lower : lower + new_count],
                 fresh_values[lower : lower + new_count],
                 own_lengths[request],

time: 344 us -> 334 us (0.971)
  waiting for transfers between devices: 220 us -> 213 us
  matrix products: 53.3 us -> 47.2 us
    gather x0 -> x1, local copies, waits for them, and re-layouts: none -> 8.76 us  [per_device(): kv_pool.reshape(pool_dev * 2 * KVH, page_len, head_dim)[row_ids.reshape(-1)]]
    broadcast_in_dim x2 -> x0, local copies, waits for them, and re-layouts: 5.75 us -> none  [per_device(): jnp.broadcast_to(picked[:, :, None], (dp_count, KVH, sharing // 2, 2, cap...]
    dot_general x1 -> x0, matrix products: 4.71 us -> none  [per_device(): jnp.einsum('dcl,lkhpe->dhkcpe', selector, kv_pool, preferred_element_type...]
    reduce_scatter x1, waiting for transfers between devices: 37.4 us -> 32.9 us  [per_device(): lax.psum_scatter(jnp.dot(attended, w_out, preferred_element_type=jnp.floa...]
  transfers between devices with their start and end apart: 6 -> 6, of which waited for: 5 -> 4; matrix products, arithmetic and copies ran while one was open for 7% -> 7% of each run, Pallas kernels for 0% -> 0%
where the time goes in v3:
time: 334 us
  waiting for transfers between devices  213 us (64%)
  matrix products  47.2 us (14%)
  other arithmetic  26.4 us (8%)
  local copies, waits for them, and re-layouts  21.7 us (6%)
  between operations  13.6 us (4%)
  starting transfers between devices  11.9 us (4%)
    all_to_all x1, waiting for transfers between devices, per_device(): lax.all_to_all(outgoing, ALL, split_axis=0, concat_axis=0, tiled=True)  110 us
    reduce_scatter x1, waiting for transfers between devices, per_device(): lax.psum_scatter(jnp.dot(hidden, w_down, preferred_element_type=jnp.float...  38 us
    reduce_scatter x1, waiting for transfers between devices, per_device(): lax.psum_scatter(jnp.dot(attended, w_out, preferred_element_type=jnp.floa...  32.9 us
    all_gather x1, waiting for transfers between devices, per_device(): hidden = geglu(lax.all_gather(ffn_in, TP, axis=0, tiled=True), w_gate, w_up)  31 us
    dot_general x1, matrix products, per_device(): jnp.dot(hidden, w_down, preferred_element_type=jnp.float32)  15.6 us
    all_to_all x1, starting transfers between devices, per_device(): lax.all_to_all(outgoing, ALL, split_axis=0, concat_axis=0, tiled=True)  11.7 us
    dot_general x1, matrix products, geglu(): gate_part = jnp.dot(block, w_gate, preferred_element_type=jnp.float32)  9.93 us
    gather x1, local copies, waits for them, and re-layouts, per_device(): kv_pool.reshape(pool_dev * 2 * KVH, page_len, head_dim)[row_ids.reshape(-1)]  8.76 us
  transfers between devices with their start and end apart: 6, of which 4 were waited for; matrix products, arithmetic and copies ran while one was open for 7% of the time, Pallas kernels for 0%

profile of v3, /device:TPU:0, one launch (start us, length us, event | category | flops | bytes accessed | tf_op | source)
XLA Modules:
  0.0 333.5 jit_solution(15612644539228625533)
XLA Ops:
  6.5 0.8 and_select_fusion.1
  7.5 0.8 eq.45
  8.4 0.4 and_reduce_fusion
  9.5 8.8 %gather_fusion = bf16[128,128,256]{2,1,0:T(8,128)(2,1)} fusion(bf16[64,128,256]{2,1,0:T(8,128)(2,1)} %bitcast.188, s32[1024]{0:T(1024)S(1)} %pad_clamp_fusion.2), kind=kCustom, calls=%fused_computation | custom fusion | bytes 16777728 | tf_op jit(solution)/shard_map/gather | solution.py:147
  18.2 11.7 %all-to-all-start = ((bf16[128,1,128,256]{3,2,1,0:T(8,128)(2,1)}), bf16[128,1,128,256]{3,2,1,0:T(8,128)(2,1)}, u32[]{:S(2)}, u32[]{:S(2)}) async-start(bf16[128,1,128,256]{3,2,1,0:T(8,128)(2,1)} %bitcast.187), calls=%async_computation | async-start | bytes 16777216 | tf_op jit(solution)/shard_map/all_to_all | solution.py:149
  30.0 0.7 all-gather.3.cloned.1.call-update
  31.6 0.8 gather_fusion.1
  32.4 0.6 fusion.156
  33.1 0.7 iota_compare_fusion.3
  33.7 0.6 iota_compare_fusion.2
  34.3 110.0 %all-to-all-done = bf16[128,1,128,256]{3,2,1,0:T(8,128)(2,1)} async-done(((bf16[128,1,128,256]{3,2,1,0:T(8,128)(2,1)}), bf16[128,1,128,256]{3,2,1,0:T(8,128)(2,1)}, u32[]{:S(2)}, u32[]{:S(2)}) %all-to-all-start) | async-done | bytes 8388640 | tf_op jit(solution)/shard_map/all_to_all | solution.py:149
  144.3 6.2 %gather_fusion.2 = bf16[64,128,256]{2,1,0:T(8,128)(2,1)} fusion(bf16[128,128,256]{2,1,0:T(8,128)(2,1)} %bitcast.3, s32[1024]{0:T(1024)S(1)} %pad_clamp_fusion), kind=kCustom, calls=%fused_computation.2 | custom fusion | bytes 8388864 | tf_op jit(solution)/shard_map/gather | solution.py:158
  150.5 3.2 fusion
  153.7 0.2 copy-done.2
  153.9 1.0 fusion.2
  155.0 1.2 copy-done.16
  156.1 1.4 multiply_reduce_fusion.4
  157.5 0.6 copy-done.17
  158.1 1.3 multiply_reduce_fusion.5
  159.5 0.2 multiply_bitcast_fusion
  159.7 2.6 fusion.66
  162.3 0.3 fusion.160
  162.7 0.3 fusion.159
  163.0 1.3 multiply_reduce_fusion.3
  164.5 0.7 copy-done.1
  165.2 2.5 broadcast_select_fusion.1
  167.7 0.9 fusion.154
  168.7 1.3 fusion.3
  170.1 2.4 fusion.5
  172.6 1.3 fusion.4
  174.0 2.6 fusion.6
  176.7 0.4 fusion.78
  177.1 0.4 fusion.76
  177.5 2.5 fusion.34
  180.0 2.5 fusion.37
  182.5 3.3 convolution_convert_fusion
  185.9 2.0 multiply_reduce_fusion.2
  187.8 32.9 %reduce-scatter.3.cloned.1.call-done = bf16[128,2048]{1,0:T(8,128)(2,1)} async-done(((bf16[1024,2048]{1,0:T(8,128)(2,1)}), bf16[128,2048]{1,0:T(8,128)(2,1)}) %reduce-scatter.3.cloned.1.call-update) | async-done | bytes 524304 | tf_op jit(solution)/shard_map/reduce_scatter | solution.py:196
  220.7 1.2 fusion.41
  222.0 2.0 multiply_reduce_fusion.1
  224.0 0.9 multiply_convert_fusion
  225.0 31.0 %all-gather.5.cloned.1.call-done = bf16[1024,2048]{1,0:T(8,128)(2,1)} async-done(((bf16[128,2048]{1,0:T(8,128)(2,1)}), bf16[1024,2048]{1,0:T(8,128)(2,1)}) %all-gather.5.cloned.1.call-update) | async-done | bytes 4194320 | tf_op jit(solution)/shard_map/all_gather | solution.py:207
  256.0 9.9 %fusion.163 = f32[1024,1024]{1,0:T(8,128)} fusion(bf16[1024,2048]{1,0:T(8,128)(2,1)} %all-gather.5.cloned.1.call-done, bf16[2048,1024]{1,0:T(8,128)(2,1)} %param.39), kind=kOutput, calls=%fused_computation.219 | convolution fusion | flops 4294967296 | bytes 12582912 | tf_op jit(solution)/shard_map/dot_general | solution.py:82
  265.9 15.6 %convolution_convert_fusion.1 = bf16[1024,2048]{1,0:T(8,128)(2,1)} fusion(bf16[1024,2048]{1,0:T(8,128)(2,1)} %param.41, f32[1024,1024]{1,0:T(8,128)} %fusion.163, bf16[1024,2048]{1,0:T(8,128)(2,1)} %all-gather.5.cloned.1.call-done, bf16[2048,1024]{1,0:T(8,128)(2,1)} %param.40), kind=kOutput, calls=%fused_computation.35 | convolution fusion | flops 8602517504 | bytes 20971520 | tf_op jit(solution)/shard_map/dot_general | solution.py:209
  281.6 38.0 %reduce-scatter.5.cloned.1.call-done = bf16[128,2048]{1,0:T(8,128)(2,1)} async-done(((bf16[1024,2048]{1,0:T(8,128)(2,1)}), bf16[128,2048]{1,0:T(8,128)(2,1)}) %reduce-scatter.5.cloned.1.call-update) | async-done | bytes 524304 | tf_op jit(solution)/shard_map/reduce_scatter | solution.py:208
  319.6 1.3 fusion.45
  321.0 3.5 %multiply_reduce_fusion = (f32[128]{0:T(128)S(1)}, f32[128,2048]{1,0:T(8,128)}) fusion(bf16[256,2048]{1,0:T(8,128)(2,1)} %param.44, bf16[2048,256]{1,0:T(8,128)(2,1)} %param.43, bf16[128,2048]{1,0:T(8,128)(2,1)} %reduce-scatter.5.cloned.1.call-done, f32[128,2048]{1,0:T(8,128)S(1)} %get-tuple-element.6, f32[2048]{0:T(1024)S(1)} %copy-done.8, ...), kind=kOutput, calls=%fused_computation.60 | convolution fusion | flops 270892928 | bytes 4793344 | tf_op jit(solution)/shard_map/dot_general | solution.py:221
  324.5 2.5 add_convert_fusion
  (97 shorter events, 2.6 us)
Async XLA Ops:
  6.5 175.9 %copy-start = (bf16[256,2048]{1,0:T(8,128)(2,1)S(1)}, bf16[256,2048]{1,0:T(8,128)(2,1)}, u32[]{:S(2)}) copy-start(bf16[256,2048]{1,0:T(8,128)(2,1)} %param.33) | copy-start | bytes 3145732
  18.2 13.2 %copy-start.18 = (s32[32]{0:T(128)S(1)}, s32[32]{0:T(128)}, u32[]{:S(2)}) copy-start(s32[32]{0:T(128)} %param.25) | copy-start | bytes 388
  18.2 126.1 %all-to-all-start = ((bf16[128,1,128,256]{3,2,1,0:T(8,128)(2,1)}), bf16[128,1,128,256]{3,2,1,0:T(8,128)(2,1)}, u32[]{:S(2)}, u32[]{:S(2)}) async-start(bf16[128,1,128,256]{3,2,1,0:T(8,128)(2,1)} %bitcast.187), calls=%async_computation | async-start | bytes 16777216 | tf_op jit(solution)/shard_map/all_to_all | solution.py:149
  29.9 120.6 %all-gather.3.cloned.1.call-start = ((), (), s32[]{:S(2)}) async-start(), calls=%async_computation.3 | async-start | bytes 4718592 | tf_op jit(solution)/shard_map/all_gather | solution.py:164
  30.7 190.0 %reduce-scatter.3.cloned.1.call-start = ((), (), s32[]{:S(2)}) async-start(), calls=%async_computation.4 | async-start | bytes 4718592 | tf_op jit(solution)/shard_map/reduce_scatter | solution.py:196
  150.5 3.3 copy-start.9
  150.5 14.0 %collective-permute-start = (bf16[64,128,256]{2,1,0:T(8,128)(2,1)}, bf16[64,128,256]{2,1,0:T(8,128)(2,1)}, u32[]{:S(2)}, u32[]{:S(2)}) collective-permute-start(bf16[64,128,256]{2,1,0:T(8,128)(2,1)} %gather_fusion.2), channel_id=1, source_target_pairs={{0,1},{1,0},{2,3},{3,2},{4,5},{5,4},{6,7},{7,6},{8,9},{9,8},{10,11... | collective-permute-start | bytes 12582920 | tf_op jit(solution)/shard_map/ppermute | solution.py:159
  150.5 3.5 %copy-start.2 = (bf16[1024,2048]{1,0:T(8,128)(2,1)S(1)}, bf16[1024,2048]{1,0:T(8,128)(2,1)}, u32[]{:S(2)}) copy-start(bf16[1024,2048]{1,0:T(8,128)(2,1)} %all-gather.3.cloned.1.call-done) | copy-start | bytes 12582916
  153.9 2.2 copy-start.16
  156.1 6.9 %copy-start.3 = (bf16[1024,2048]{1,0:T(8,128)(2,1)}, bf16[1024,2048]{1,0:T(8,128)(2,1)S(1)}, u32[]{:S(2)}) copy-start(bf16[1024,2048]{1,0:T(8,128)(2,1)S(1)} %fusion.2) | copy-start | bytes 12582916
  156.1 2.0 copy-start.17
  158.1 1.3 copy-start.14
  158.1 1.4 copy-start.15
  163.0 2.2 copy-start.1
  182.4 3.4 %copy-start.5 = (bf16[64,2048]{1,0:T(8,128)(2,1)S(1)}, bf16[64,2048]{1,0:T(8,128)(2,1)}, u32[]{:S(2)}) copy-start(bf16[64,2048]{1,0:T(8,128)(2,1)} %param.36) | copy-start | bytes 786436
  182.5 3.4 %copy-start.6 = (bf16[2048,64]{0,1:T(8,128)(2,1)S(1)}, bf16[2048,64]{0,1:T(8,128)(2,1)}, u32[]{:S(2)}) copy-start(bf16[2048,64]{0,1:T(8,128)(2,1)} %param.35) | copy-start | bytes 786436
  185.7 36.2 %copy-start.10 = (f32[2048]{0:T(1024)S(1)}, f32[2048]{0:T(1024)}, u32[]{:S(2)}) copy-start(f32[2048]{0:T(1024)} %param.37) | copy-start | bytes 24580
  185.8 36.2 %copy-start.11 = (f32[2048]{0:T(1024)S(1)}, f32[2048]{0:T(1024)}, u32[]{:S(2)}) copy-start(f32[2048]{0:T(1024)} %param.34) | copy-start | bytes 24580
  185.8 38.2 %copy-start.12 = (f32[2048]{0:T(1024)S(1)}, f32[2048]{0:T(1024)}, u32[]{:S(2)}) copy-start(f32[2048]{0:T(1024)} %param.38) | copy-start | bytes 24580
  185.8 70.2 %all-gather.5.cloned.1.call-start = ((), (), s32[]{:S(2)}) async-start(), calls=%async_computation.5 | async-start | bytes 4718592 | tf_op jit(solution)/shard_map/all_gather | solution.py:207
  224.9 94.7 %reduce-scatter.5.cloned.1.call-start = ((), (), s32[]{:S(2)}) async-start(), calls=%async_computation.6 | async-start | bytes 4718592 | tf_op jit(solution)/shard_map/reduce_scatter | solution.py:208
  281.5 39.4 %copy-start.7 = (bf16[128,256]{1,0:T(8,128)(2,1)S(1)}, bf16[128,256]{1,0:T(8,128)(2,1)}, u32[]{:S(2)}) copy-start(bf16[128,256]{1,0:T(8,128)(2,1)} %param.24) | copy-start | bytes 196612
  281.5 39.4 %copy-start.8 = (f32[2048]{0:T(1024)S(1)}, f32[2048]{0:T(1024)}, u32[]{:S(2)}) copy-start(f32[2048]{0:T(1024)} %param.42) | copy-start | bytes 24580
  281.5 43.0 %copy-start.13 = (f32[2048]{0:T(1024)S(1)}, f32[2048]{0:T(1024)}, u32[]{:S(2)}) copy-start(f32[2048]{0:T(1024)} %param.45) | copy-start | bytes 24580
  319.6 4.9 %copy-start.4 = (bf16[128,2048]{1,0:T(8,128)(2,1)S(1)}, bf16[128,2048]{1,0:T(8,128)(2,1)}, u32[]{:S(2)}) copy-start(bf16[128,2048]{1,0:T(8,128)(2,1)} %reduce-scatter.5.cloned.1.call-done) | copy-start | bytes 1572868
Sparse Core Ops, SparseCore 0:
  32.5 66.7 all-gather.2
  185.9 34.7 reduce-scatter.2
  225.1 30.9 all-gather.4
  281.7 37.8 reduce-scatter.4

commit v4 on v3

--- a/solution.py
+++ b/solution.py
@@ -192,34 +192,52 @@
             )
         )
     attended = jnp.concatenate(pieces, axis=0)
+    chunks = 2
     own_x = hidden_in.astype(jnp.float32)
-    projected = lax.psum_scatter(
-        jnp.dot(attended, w_out, preferred_element_type=jnp.float32).astype(jnp.bfloat16),
-        TP,
-        scatter_dimension=0,
-        tiled=True,
-    ).astype(jnp.float32)
     own_normed = lax.dynamic_slice_in_dim(normed, tp_at * own_rows, own_rows, 0)
-    mixed_rows = residual_mix(
-        own_x, projected, own_normed, post_attn_gain, laurel_left, laurel_right, laurel_gain
-    )
-    ffn_in = norm_rows(mixed_rows, pre_ffn_gain).astype(jnp.bfloat16)
-    hidden = geglu(lax.all_gather(ffn_in, TP, axis=0, tiled=True), w_gate, w_up)
-    down = lax.psum_scatter(
-        jnp.dot(hidden, w_down, preferred_element_type=jnp.float32).astype(jnp.bfloat16),
-        TP,
-        scatter_dimension=0,
-        tiled=True,
-    ).astype(jnp.float32)
-    settled = mixed_rows + norm_rows(down, post_ffn_gain)
-    settled_half = settled.astype(jnp.bfloat16)
-    gated = jax.nn.gelu(
-        jnp.dot(settled_half, ple_gate, preferred_element_type=jnp.float32), approximate=True
-    )
-    gated = (gated * layer_input.astype(jnp.float32)).astype(jnp.bfloat16)
-    return (
-        settled + norm_rows(jnp.dot(gated, ple_proj, preferred_element_type=jnp.float32), ple_gain)
-    ).astype(jnp.bfloat16)
+    part_rows = own_rows // chunks
+    spread = attended.reshape(tp_count, chunks, part_rows, attended.shape[-1])
+    outputs = []
+    for part in range(chunks):
+        rows = slice(part * part_rows, (part + 1) * part_rows)
+        projected = lax.psum_scatter(
+            jnp.dot(
+                spread[:, part].reshape(tp_count * part_rows, -1),
+                w_out,
+                preferred_element_type=jnp.float32,
+            ).astype(jnp.bfloat16),
+            TP,
+            scatter_dimension=0,
+            tiled=True,
+        ).astype(jnp.float32)
+        mixed_rows = residual_mix(
+            own_x[rows],
+            projected,
+            own_normed[rows],
+            post_attn_gain,
+            laurel_left,
+            laurel_right,
+            laurel_gain,
+        )
+        ffn_in = norm_rows(mixed_rows, pre_ffn_gain).astype(jnp.bfloat16)
+        hidden = geglu(lax.all_gather(ffn_in, TP, axis=0, tiled=True), w_gate, w_up)
+        down = lax.psum_scatter(
+            jnp.dot(hidden, w_down, preferred_element_type=jnp.float32).astype(jnp.bfloat16),
+            TP,
+            scatter_dimension=0,
+            tiled=True,
+        ).astype(jnp.float32)
+        settled = mixed_rows + norm_rows(down, post_ffn_gain)
+        settled_half = settled.astype(jnp.bfloat16)
+        gated = jax.nn.gelu(
+            jnp.dot(settled_half, ple_gate, preferred_element_type=jnp.float32), approximate=True
+        )
+        gated = (gated * layer_input[rows].astype(jnp.float32)).astype(jnp.bfloat16)
+        outputs.append(
+            settled
+            + norm_rows(jnp.dot(gated, ple_proj, preferred_element_type=jnp.float32), ple_gain)
+        )
+    return jnp.concatenate(outputs, axis=0).astype(jnp.bfloat16)
 
 
 def solution(mesh):

time: 334 us -> 400 us (1.20); the launches traced: 334 us -> 392 us
  waiting for transfers between devices: 213 us -> 252 us
  matrix products: 47.2 us -> 62.6 us
    reduce_scatter x1 -> x2, waiting for transfers between devices: 32.9 us -> 57.7 us  [per_device(): lax.psum_scatter(jnp.dot(spread[:, part].reshape(tp_count * part_rows, -1...]
    reduce_scatter x1 -> x2, waiting for transfers between devices: 38 us -> 49.8 us  [per_device(): lax.psum_scatter(jnp.dot(hidden, w_down, preferred_element_type=jnp.float...]
    dot_general x1 -> x2, matrix products: 15.6 us -> 21.7 us  [per_device(): jnp.dot(hidden, w_down, preferred_element_type=jnp.float32)]
    dot_general x1 -> x2, matrix products: 9.93 us -> 13 us  [geglu(): gate_part = jnp.dot(block, w_gate, preferred_element_type=jnp.float32)]
    reduce_sum x4 -> x6, other arithmetic: 7.72 us -> 9.82 us  [norm_rows(): jnp.mean(values * values, axis=-1, keepdims=True) + EPS]
    all_gather x1 -> x2, waiting for transfers between devices: 31 us -> 33 us  [per_device(): hidden = geglu(lax.all_gather(ffn_in, TP, axis=0, tiled=True), w_gate, w_up)]
  transfers between devices with their start and end apart: 6 -> 9, of which waited for: 4 -> 7; matrix products, arithmetic and copies ran while one was open for 7% -> 18% of each run, Pallas kernels for 0% -> 0%
where the time goes in v4:
time: 400 us; the launch traced here: 392 us
  waiting for transfers between devices  252 us (63%)
  matrix products  62.6 us (16%)
  other arithmetic  29.1 us (7%)
  local copies, waits for them, and re-layouts  22 us (6%)
  between operations  14.4 us (4%)
  starting transfers between devices  12.3 us (3%)
    all_to_all x1, waiting for transfers between devices, per_device(): lax.all_to_all(outgoing, ALL, split_axis=0, concat_axis=0, tiled=True)  110 us
    reduce_scatter x2, waiting for transfers between devices, per_device(): lax.psum_scatter(jnp.dot(spread[:, part].reshape(tp_count * part_rows, -1...  57.7 us
    reduce_scatter x2, waiting for transfers between devices, per_device(): lax.psum_scatter(jnp.dot(hidden, w_down, preferred_element_type=jnp.float...  49.8 us
    all_gather x2, waiting for transfers between devices, per_device(): hidden = geglu(lax.all_gather(ffn_in, TP, axis=0, tiled=True), w_gate, w_up)  33 us
    dot_general x2, matrix products, per_device(): jnp.dot(hidden, w_down, preferred_element_type=jnp.float32)  21.7 us
    dot_general x2, matrix products, geglu(): gate_part = jnp.dot(block, w_gate, preferred_element_type=jnp.float32)  13 us
    all_to_all x1, starting transfers between devices, per_device(): lax.all_to_all(outgoing, ALL, split_axis=0, concat_axis=0, tiled=True)  11.5 us
    reduce_sum x6, other arithmetic, norm_rows(): jnp.mean(values * values, axis=-1, keepdims=True) + EPS  9.82 us
  transfers between devices with their start and end apart: 9, of which 7 were waited for; matrix products, arithmetic and copies ran while one was open for 18% of the time, Pallas kernels for 0%

profile of v4, /device:TPU:0, one launch (start us, length us, event | category | flops | bytes accessed | tf_op | source)
XLA Modules:
  0.0 392.3 jit_solution(3314684532706296726)
XLA Ops:
  6.5 0.8 and_select_fusion.1
  7.5 0.8 eq.45
  9.5 8.8 %gather_fusion = bf16[128,128,256]{2,1,0:T(8,128)(2,1)} fusion(bf16[64,128,256]{2,1,0:T(8,128)(2,1)} %bitcast.203, s32[1024]{0:T(1024)S(1)} %pad_clamp_fusion.2), kind=kCustom, calls=%fused_computation | custom fusion | bytes 16777728 | tf_op jit(solution)/shard_map/gather | solution.py:147
  18.2 11.5 %all-to-all-start = ((bf16[128,1,128,256]{3,2,1,0:T(8,128)(2,1)}), bf16[128,1,128,256]{3,2,1,0:T(8,128)(2,1)}, u32[]{:S(2)}, u32[]{:S(2)}) async-start(bf16[128,1,128,256]{3,2,1,0:T(8,128)(2,1)} %bitcast.202), calls=%async_computation | async-start | bytes 16777216 | tf_op jit(solution)/shard_map/all_to_all | solution.py:149
  29.8 0.7 all-gather.4.cloned.1.call-update
  31.4 0.8 gather_fusion.1
  34.2 110.0 %all-to-all-done = bf16[128,1,128,256]{3,2,1,0:T(8,128)(2,1)} async-done(((bf16[128,1,128,256]{3,2,1,0:T(8,128)(2,1)}), bf16[128,1,128,256]{3,2,1,0:T(8,128)(2,1)}, u32[]{:S(2)}, u32[]{:S(2)}) %all-to-all-start) | async-done | bytes 8388640 | tf_op jit(solution)/shard_map/all_to_all | solution.py:149
  144.1 6.2 %gather_fusion.2 = bf16[64,128,256]{2,1,0:T(8,128)(2,1)} fusion(bf16[128,128,256]{2,1,0:T(8,128)(2,1)} %bitcast.3, s32[1024]{0:T(1024)S(1)} %pad_clamp_fusion), kind=kCustom, calls=%fused_computation.2 | custom fusion | bytes 8388864 | tf_op jit(solution)/shard_map/gather | solution.py:158
  150.3 3.2 fusion
  153.8 1.0 fusion.2
  154.8 1.2 copy-done.18
  156.0 1.4 multiply_reduce_fusion.1
  158.0 1.3 multiply_reduce_fusion.2
  159.6 2.9 fusion.80
  163.2 1.3 multiply_reduce_fusion
  164.7 0.7 copy-done.1
  165.4 2.5 broadcast_select_fusion.1
  167.9 0.9 fusion.213
  168.8 1.3 fusion.3
  170.3 2.4 fusion.5
  172.7 1.3 fusion.4
  174.2 2.6 fusion.6
  177.6 2.5 fusion.43
  180.1 2.5 fusion.46
  182.9 2.0 convolution_convert_fusion.3
  185.0 2.1 convolution_convert_fusion.1
  187.3 2.4 multiply_reduce_fusion.8
  189.7 2.4 multiply_reduce_fusion.5
  192.1 23.7 %reduce-scatter.5.cloned.1.call-done = bf16[64,2048]{1,0:T(8,128)(2,1)} async-done(((bf16[512,2048]{1,0:T(8,128)(2,1)}), bf16[64,2048]{1,0:T(8,128)(2,1)}) %reduce-scatter.5.cloned.1.call-update) | async-done | bytes 262160 | tf_op jit(solution)/shard_map/reduce_scatter | solution.py:203
  215.8 1.1 fusion.65
  216.9 34.1 %reduce-scatter.9.cloned.1.call-done = bf16[64,2048]{1,0:T(8,128)(2,1)} async-done(((bf16[512,2048]{1,0:T(8,128)(2,1)}), bf16[64,2048]{1,0:T(8,128)(2,1)}) %reduce-scatter.9.cloned.1.call-update) | async-done | bytes 262160 | tf_op jit(solution)/shard_map/reduce_scatter | solution.py:203
  251.0 1.1 fusion.72
  252.1 2.1 multiply_reduce_fusion.7
  254.3 0.9 multiply_convert_fusion.2
  256.1 23.4 %all-gather.8.cloned.1.call-done = bf16[512,2048]{1,0:T(8,128)(2,1)} async-done(((bf16[64,2048]{1,0:T(8,128)(2,1)}), bf16[512,2048]{1,0:T(8,128)(2,1)}) %all-gather.8.cloned.1.call-update) | async-done | bytes 2097168 | tf_op jit(solution)/shard_map/all_gather | solution.py:223
  279.5 6.5 %fusion.228 = f32[512,1024]{1,0:T(8,128)} fusion(bf16[512,2048]{1,0:T(8,128)(2,1)} %all-gather.8.cloned.1.call-done, bf16[2048,1024]{1,0:T(8,128)(2,1)} %param.39), kind=kOutput, calls=%fused_computation.288 | convolution fusion | flops 2147483648 | bytes 8388608 | tf_op jit(solution)/shard_map/dot_general | solution.py:82
  286.0 10.8 %convolution_convert_fusion = bf16[512,2048]{1,0:T(8,128)(2,1)} fusion(bf16[1024,2048]{1,0:T(8,128)(2,1)} %param.41, f32[512,1024]{1,0:T(8,128)} %fusion.228, bf16[512,2048]{1,0:T(8,128)(2,1)} %all-gather.8.cloned.1.call-done, bf16[2048,1024]{1,0:T(8,128)(2,1)} %param.40), kind=kOutput, calls=%fused_computation.26 | convolution fusion | flops 4301258752 | bytes 14680064 | tf_op jit(solution)/shard_map/dot_general | solution.py:225
  297.2 9.6 %all-gather.6.cloned.1.call-done = bf16[512,2048]{1,0:T(8,128)(2,1)} async-done(((bf16[64,2048]{1,0:T(8,128)(2,1)}), bf16[512,2048]{1,0:T(8,128)(2,1)}) %all-gather.6.cloned.1.call-update) | async-done | bytes 2097168 | tf_op jit(solution)/shard_map/all_gather | solution.py:223
  306.8 6.5 %fusion.227 = f32[512,1024]{1,0:T(8,128)} fusion(bf16[512,2048]{1,0:T(8,128)(2,1)} %all-gather.6.cloned.1.call-done, bf16[2048,1024]{1,0:T(8,128)(2,1)} %param.39), kind=kOutput, calls=%fused_computation.287 | convolution fusion | flops 2147483648 | bytes 8388608 | tf_op jit(solution)/shard_map/dot_general | solution.py:82
  313.3 10.9 %convolution_convert_fusion.2 = bf16[512,2048]{1,0:T(8,128)(2,1)} fusion(bf16[1024,2048]{1,0:T(8,128)(2,1)} %param.41, f32[512,1024]{1,0:T(8,128)} %fusion.227, bf16[512,2048]{1,0:T(8,128)(2,1)} %all-gather.6.cloned.1.call-done, bf16[2048,1024]{1,0:T(8,128)(2,1)} %param.40), kind=kOutput, calls=%fused_computation.28 | convolution fusion | flops 4301258752 | bytes 14680064 | tf_op jit(solution)/shard_map/dot_general | solution.py:225
  324.2 19.1 %reduce-scatter.11.cloned.1.call-done = bf16[64,2048]{1,0:T(8,128)(2,1)} async-done(((bf16[512,2048]{1,0:T(8,128)(2,1)}), bf16[64,2048]{1,0:T(8,128)(2,1)}) %reduce-scatter.11.cloned.1.call-update) | async-done | bytes 262160 | tf_op jit(solution)/shard_map/reduce_scatter | solution.py:224
  343.3 1.2 fusion.76
  344.5 3.1 multiply_reduce_fusion.3
  347.6 30.8 %reduce-scatter.7.cloned.1.call-done = bf16[64,2048]{1,0:T(8,128)(2,1)} async-done(((bf16[512,2048]{1,0:T(8,128)(2,1)}), bf16[64,2048]{1,0:T(8,128)(2,1)}) %reduce-scatter.7.cloned.1.call-update) | async-done | bytes 262160 | tf_op jit(solution)/shard_map/reduce_scatter | solution.py:224
  378.3 1.1 fusion.69
  379.5 3.1 multiply_reduce_fusion.6
  382.6 1.8 add_convert_fusion.1
  384.3 0.8 pad_maximum_fusion.1
  (126 shorter events, 9.0 us)
Async XLA Ops:
  6.5 176.3 %copy-start = (bf16[256,2048]{1,0:T(8,128)(2,1)S(1)}, bf16[256,2048]{1,0:T(8,128)(2,1)}, u32[]{:S(2)}) copy-start(bf16[256,2048]{1,0:T(8,128)(2,1)} %param.33) | copy-start | bytes 3145732
  18.2 13.0 %copy-start.20 = (s32[32]{0:T(128)S(1)}, s32[32]{0:T(128)}, u32[]{:S(2)}) copy-start(s32[32]{0:T(128)} %param.25) | copy-start | bytes 388
  18.2 125.9 %all-to-all-start = ((bf16[128,1,128,256]{3,2,1,0:T(8,128)(2,1)}), bf16[128,1,128,256]{3,2,1,0:T(8,128)(2,1)}, u32[]{:S(2)}, u32[]{:S(2)}) async-start(bf16[128,1,128,256]{3,2,1,0:T(8,128)(2,1)} %bitcast.202), calls=%async_computation | async-start | bytes 16777216 | tf_op jit(solution)/shard_map/all_to_all | solution.py:149
  29.8 120.6 %all-gather.4.cloned.1.call-start = ((), (), s32[]{:S(2)}) async-start(), calls=%async_computation.5 | async-start | bytes 4718592 | tf_op jit(solution)/shard_map/all_gather | solution.py:164
  30.5 185.3 %reduce-scatter.5.cloned.1.call-start = ((), (), s32[]{:S(2)}) async-start(), calls=%async_computation.6 | async-start | bytes 2359296 | tf_op jit(solution)/shard_map/reduce_scatter | solution.py:203
  150.3 3.3 copy-start.11
  150.3 14.4 %collective-permute-start = (bf16[64,128,256]{2,1,0:T(8,128)(2,1)}, bf16[64,128,256]{2,1,0:T(8,128)(2,1)}, u32[]{:S(2)}, u32[]{:S(2)}) collective-permute-start(bf16[64,128,256]{2,1,0:T(8,128)(2,1)} %gather_fusion.2), channel_id=1, source_target_pairs={{0,1},{1,0},{2,3},{3,2},{4,5},{5,4},{6,7},{7,6},{8,9},{9,8},{10,11... | collective-permute-start | bytes 12582920 | tf_op jit(solution)/shard_map/ppermute | solution.py:159
  150.3 3.5 copy-start.2
  153.8 2.2 copy-start.18
  156.0 7.2 %copy-start.3 = (bf16[1024,2048]{1,0:T(8,128)(2,1)}, bf16[1024,2048]{1,0:T(8,128)(2,1)S(1)}, u32[]{:S(2)}) copy-start(bf16[1024,2048]{1,0:T(8,128)(2,1)S(1)} %fusion.2) | copy-start | bytes 12582916
  156.0 2.0 copy-start.19
  157.9 1.3 copy-start.16
  158.0 1.3 copy-start.17
  163.2 2.2 copy-start.1
  184.9 2.2 copy-start.6
  184.9 2.4 copy-start.7
  184.9 2.4 copy-start.8
  185.0 66.0 %reduce-scatter.9.cloned.1.call-start = ((), (), s32[]{:S(2)}) async-start(), calls=%async_computation.9 | async-start | bytes 2359296 | tf_op jit(solution)/shard_map/reduce_scatter | solution.py:203
  187.1 65.0 %copy-start.12 = (f32[2048]{0:T(1024)S(1)}, f32[2048]{0:T(1024)}, u32[]{:S(2)}) copy-start(f32[2048]{0:T(1024)} %param.37) | copy-start | bytes 24580
  187.1 65.0 %copy-start.13 = (f32[2048]{0:T(1024)S(1)}, f32[2048]{0:T(1024)}, u32[]{:S(2)}) copy-start(f32[2048]{0:T(1024)} %param.34) | copy-start | bytes 24580
  187.1 92.4 %all-gather.8.cloned.1.call-start = ((), (), s32[]{:S(2)}) async-start(), calls=%async_computation.10 | async-start | bytes 2359296 | tf_op jit(solution)/shard_map/all_gather | solution.py:223
  187.2 67.1 %copy-start.14 = (f32[2048]{0:T(1024)S(1)}, f32[2048]{0:T(1024)}, u32[]{:S(2)}) copy-start(f32[2048]{0:T(1024)} %param.38) | copy-start | bytes 24580
  255.2 51.5 %all-gather.6.cloned.1.call-start = ((), (), s32[]{:S(2)}) async-start(), calls=%async_computation.7 | async-start | bytes 2359296 | tf_op jit(solution)/shard_map/all_gather | solution.py:223
  255.8 87.5 %reduce-scatter.11.cloned.1.call-start = ((), (), s32[]{:S(2)}) async-start(), calls=%async_computation.11 | async-start | bytes 2359296 | tf_op jit(solution)/shard_map/reduce_scatter | solution.py:224
  296.9 81.5 %reduce-scatter.7.cloned.1.call-start = ((), (), s32[]{:S(2)}) async-start(), calls=%async_computation.8 | async-start | bytes 2359296 | tf_op jit(solution)/shard_map/reduce_scatter | solution.py:224
  313.3 31.2 %copy-start.4 = (bf16[256,2048]{1,0:T(8,128)(2,1)S(1)}, bf16[256,2048]{1,0:T(8,128)(2,1)}, u32[]{:S(2)}) copy-start(bf16[256,2048]{1,0:T(8,128)(2,1)} %param.44) | copy-start | bytes 3145732
  313.3 31.2 %copy-start.9 = (f32[2048]{0:T(1024)S(1)}, f32[2048]{0:T(1024)}, u32[]{:S(2)}) copy-start(f32[2048]{0:T(1024)} %param.42) | copy-start | bytes 24580
  313.3 31.2 %copy-start.10 = (bf16[128,256]{1,0:T(8,128)(2,1)S(1)}, bf16[128,256]{1,0:T(8,128)(2,1)}, u32[]{:S(2)}) copy-start(bf16[128,256]{1,0:T(8,128)(2,1)} %param.24) | copy-start | bytes 196612
  324.2 58.4 %copy-start.15 = (f32[2048]{0:T(1024)S(1)}, f32[2048]{0:T(1024)}, u32[]{:S(2)}) copy-start(f32[2048]{0:T(1024)} %param.45) | copy-start | bytes 24580
  343.3 39.3 %copy-start.5 = (bf16[64,2048]{1,0:T(8,128)(2,1)S(1)}, bf16[64,2048]{1,0:T(8,128)(2,1)}, u32[]{:S(2)}) copy-start(bf16[64,2048]{1,0:T(8,128)(2,1)} %reduce-scatter.11.cloned.1.call-done) | copy-start | bytes 786436
Sparse Core Ops, SparseCore 0:
  32.3 66.7 all-gather.3
  185.1 30.6 reduce-scatter.4
  218.2 32.7 reduce-scatter.8
  255.3 24.1 all-gather.7
  281.1 25.6 all-gather.5
  309.0 34.1 reduce-scatter.10
  345.7 32.6 reduce-scatter.6

commit v5 on v3

--- a/solution.py
+++ b/solution.py
@@ -82,6 +82,20 @@
     gate_part = jnp.dot(block, w_gate, preferred_element_type=jnp.float32)
     up_part = jnp.dot(block, w_up, preferred_element_type=jnp.float32)
     return (jax.nn.gelu(gate_part, approximate=True) * up_part).astype(jnp.bfloat16)
+
+
+def exchange_sum(partial):
+    peers = lax.axis_size("tx") * lax.axis_size("tc")
+    blocks = partial.reshape(peers, -1, partial.shape[-1])
+    got = lax.all_to_all(blocks, TP, split_axis=0, concat_axis=0, tiled=True)
+    return jnp.sum(got.astype(jnp.float32), axis=0)
+
+
+def exchange_gather(rows):
+    peers = lax.axis_size("tx") * lax.axis_size("tc")
+    sent = jnp.broadcast_to(rows[None], (peers,) + rows.shape)
+    got = lax.all_to_all(sent, TP, split_axis=0, concat_axis=0, tiled=True)
+    return got.reshape(peers * rows.shape[0], rows.shape[-1])
 
 
 def per_device(
@@ -193,24 +207,18 @@
         )
     attended = jnp.concatenate(pieces, axis=0)
     own_x = hidden_in.astype(jnp.float32)
-    projected = lax.psum_scatter(
-        jnp.dot(attended, w_out, preferred_element_type=jnp.float32).astype(jnp.bfloat16),
-        TP,
-        scatter_dimension=0,
-        tiled=True,
-    ).astype(jnp.float32)
+    projected = exchange_sum(
+        jnp.dot(attended, w_out, preferred_element_type=jnp.float32).astype(jnp.bfloat16)
+    )
     own_normed = lax.dynamic_slice_in_dim(normed, tp_at * own_rows, own_rows, 0)
     mixed_rows = residual_mix(
         own_x, projected, own_normed, post_attn_gain, laurel_left, laurel_right, laurel_gain
     )
     ffn_in = norm_rows(mixed_rows, pre_ffn_gain).astype(jnp.bfloat16)
-    hidden = geglu(lax.all_gather(ffn_in, TP, axis=0, tiled=True), w_gate, w_up)
-    down = lax.psum_scatter(
-        jnp.dot(hidden, w_down, preferred_element_type=jnp.float32).astype(jnp.bfloat16),
-        TP,
-        scatter_dimension=0,
-        tiled=True,
-    ).astype(jnp.float32)
+    hidden = geglu(exchange_gather(ffn_in), w_gate, w_up)
+    down = exchange_sum(
+        jnp.dot(hidden, w_down, preferred_element_type=jnp.float32).astype(jnp.bfloat16)
+    )
     settled = mixed_rows + norm_rows(down, post_ffn_gain)
     settled_half = settled.astype(jnp.bfloat16)
     gated = jax.nn.gelu(

time: 334 us -> 390 us (1.17)
  blocking collectives: 0 us -> 106 us
  waiting for transfers between devices: 213 us -> 158 us
  starting transfers between devices: 11.9 us -> 16.2 us
  matrix products: 47.2 us -> 43.2 us
    all_to_all x0 -> x2, blocking collectives: none -> 106 us  [the longest x1 53.3 us: exchange_sum(): got = lax.all_to_all(blocks, TP, split_axis=0, concat_axis=0, tiled=True)]
    reduce_scatter x2 -> x0, waiting for transfers between devices: 70.9 us -> none  [the longest x1 38 us: per_device(): lax.psum_scatter(jnp.dot(hidden, w_down, preferred_element_type=jnp.float...]
    all_to_all x0 -> x1, waiting for transfers between devices: none -> 47.6 us  [exchange_sum(): got = lax.all_to_all(blocks, TP, split_axis=0, concat_axis=0, tiled=True)]
    all_gather x1 -> x0, waiting for transfers between devices: 31 us -> none  [per_device(): hidden = geglu(lax.all_gather(ffn_in, TP, axis=0, tiled=True), w_gate, w_up)]
    all_to_all x0 -> x1, starting transfers between devices: none -> 4.68 us  [exchange_sum(): got = lax.all_to_all(blocks, TP, split_axis=0, concat_axis=0, tiled=True)]
    dot_general x1, matrix products: 9.93 us -> 6.02 us  [geglu(): gate_part = jnp.dot(block, w_gate, preferred_element_type=jnp.float32)]
  transfers between devices with their start and end apart: 6 -> 4, of which waited for: 4 -> 2; matrix products, arithmetic and copies ran while one was open for 7% -> 6% of each run, Pallas kernels for 0% -> 0%
where the time goes in v5:
time: 390 us; the launch traced here: 389 us
  waiting for transfers between devices  158 us (41%)
  blocking collectives  106 us (27%)
  matrix products  43.2 us (11%)
  other arithmetic  26.8 us (7%)
  local copies, waits for them, and re-layouts  24.2 us (6%)
  starting transfers between devices  16.2 us (4%)
  between operations  13.9 us (4%)
    all_to_all x1, waiting for transfers between devices, per_device(): lax.all_to_all(outgoing, ALL, split_axis=0, concat_axis=0, tiled=True)  110 us
    all_to_all x1, blocking collectives, exchange_sum(): got = lax.all_to_all(blocks, TP, split_axis=0, concat_axis=0, tiled=True)  53.3 us
    all_to_all x1, blocking collectives, exchange_gather(): got = lax.all_to_all(sent, TP, split_axis=0, concat_axis=0, tiled=True)  53 us
    all_to_all x1, waiting for transfers between devices, exchange_sum(): got = lax.all_to_all(blocks, TP, split_axis=0, concat_axis=0, tiled=True)  47.6 us
    dot_general x1, matrix products, per_device(): jnp.dot(hidden, w_down, preferred_element_type=jnp.float32)  15.6 us
    all_to_all x1, starting transfers between devices, per_device(): lax.all_to_all(outgoing, ALL, split_axis=0, concat_axis=0, tiled=True)  11.5 us
    gather x1, local copies, waits for them, and re-layouts, per_device(): kv_pool.reshape(pool_dev * 2 * KVH, page_len, head_dim)[row_ids.reshape(-1)]  8.76 us
  transfers between devices with their start and end apart: 4, of which 2 were waited for; matrix products, arithmetic and copies ran while one was open for 6% of the time, Pallas kernels for 0%

profile of v5, /device:TPU:0, one launch (start us, length us, event | category | flops | bytes accessed | tf_op | source)
XLA Modules:
  0.0 389.0 jit_solution(2263892901893867298)
XLA Ops:
  6.5 0.8 and_select_fusion.1
  7.5 0.8 eq.45
  8.4 0.4 and_reduce_fusion
  9.5 8.8 %gather_fusion = bf16[128,128,256]{2,1,0:T(8,128)(2,1)} fusion(bf16[64,128,256]{2,1,0:T(8,128)(2,1)} %bitcast.192, s32[1024]{0:T(1024)S(1)} %pad_clamp_fusion.2), kind=kCustom, calls=%fused_computation | custom fusion | bytes 16777728 | tf_op jit(solution)/shard_map/gather | solution.py:161
  18.2 11.5 %all-to-all-start = ((bf16[128,1,128,256]{3,2,1,0:T(8,128)(2,1)}), bf16[128,1,128,256]{3,2,1,0:T(8,128)(2,1)}, u32[]{:S(2)}, u32[]{:S(2)}) async-start(bf16[128,1,128,256]{3,2,1,0:T(8,128)(2,1)} %bitcast.190), calls=%async_computation | async-start | bytes 16777216 | tf_op jit(solution)/shard_map/all_to_all | solution.py:163
  29.8 0.7 all-gather.2.cloned.1.call-update
  31.4 0.8 gather_fusion.1
  32.2 0.6 fusion.144
  32.8 0.7 iota_compare_fusion.3
  33.5 0.6 iota_compare_fusion.2
  34.1 110.0 %all-to-all-done = bf16[128,1,128,256]{3,2,1,0:T(8,128)(2,1)} async-done(((bf16[128,1,128,256]{3,2,1,0:T(8,128)(2,1)}), bf16[128,1,128,256]{3,2,1,0:T(8,128)(2,1)}, u32[]{:S(2)}, u32[]{:S(2)}) %all-to-all-start) | async-done | bytes 8388640 | tf_op jit(solution)/shard_map/all_to_all | solution.py:163
  144.1 6.2 %gather_fusion.2 = bf16[64,128,256]{2,1,0:T(8,128)(2,1)} fusion(bf16[128,128,256]{2,1,0:T(8,128)(2,1)} %bitcast.3, s32[1024]{0:T(1024)S(1)} %pad_clamp_fusion), kind=kCustom, calls=%fused_computation.2 | custom fusion | bytes 8388864 | tf_op jit(solution)/shard_map/gather | solution.py:172
  150.3 3.2 fusion
  153.8 1.0 fusion.2
  154.8 1.2 copy-done.16
  156.0 1.4 multiply_reduce_fusion.6
  157.3 0.6 copy-done.18
  157.9 1.3 multiply_reduce_fusion.7
  159.6 2.6 fusion.56
  162.2 0.3 fusion.148
  162.5 0.3 fusion.147
  162.9 1.3 multiply_reduce_fusion.5
  164.3 0.7 copy-done.1
  165.0 2.5 broadcast_select_fusion.1
  167.6 0.9 fusion.142
  168.5 1.3 fusion.3
  170.0 2.4 fusion.5
  172.4 1.3 fusion.4
  173.9 2.6 fusion.6
  176.5 0.4 fusion.68
  176.9 0.4 fusion.66
  177.3 2.5 fusion.34
  179.8 2.5 fusion.37
  182.3 3.3 convolution_convert_fusion
  185.6 4.7 %all-to-all-start.1 = ((bf16[8,128,2048]{2,1,0:T(8,128)(2,1)}), bf16[8,128,2048]{2,1,0:T(8,128)(2,1)}, u32[]{:S(2)}, u32[]{:S(2)}) async-start(bf16[8,128,2048]{2,1,0:T(8,128)(2,1)} %bitcast.191), calls=%async_computation.1 | async-start | bytes 8388608 | tf_op jit(solution)/shard_map/all_to_all | solution.py:90
  190.3 2.0 multiply_reduce_fusion.3
  192.3 47.6 %all-to-all-done.1 = bf16[8,128,2048]{2,1,0:T(8,128)(2,1)} async-done(((bf16[8,128,2048]{2,1,0:T(8,128)(2,1)}), bf16[8,128,2048]{2,1,0:T(8,128)(2,1)}, u32[]{:S(2)}, u32[]{:S(2)}) %all-to-all-start.1) | async-done | bytes 4194336 | tf_op jit(solution)/shard_map/all_to_all | solution.py:90
  239.9 3.0 convert_reduce_fusion.1
  243.1 1.8 multiply_reduce_fusion.2
  245.0 0.5 broadcast_in_dim.40
  245.6 53.0 %all_to_all.20 = bf16[8,128,2048]{2,1,0:T(8,128)(2,1)S(1)} all-to-all(bf16[8,128,2048]{2,1,0:T(8,128)(2,1)S(1)} %broadcast_in_dim.40), channel_id=1, replica_groups=mesh['dp'=16,'tx'=4,'tc'=2] {'tx','tc'}, dimensions={0} | all-to-all | bytes 8388608 | tf_op jit(solution)/shard_map/all_to_all | solution.py:97
  298.6 2.0 copy-done.4
  300.5 6.0 %fusion.151 = f32[1024,1024]{1,0:T(8,128)} fusion(bf16[1024,2048]{1,0:T(8,128)(2,1)S(1)} %bitcast.195, bf16[2048,1024]{1,0:T(8,128)(2,1)S(1)} %copy-done.17), kind=kOutput, calls=%fused_computation.211 | convolution fusion | flops 4294967296 | bytes 12582912 | tf_op jit(solution)/shard_map/dot_general | solution.py:82
  306.6 15.6 %convolution_convert_fusion.1 = bf16[1024,2048]{1,0:T(8,128)(2,1)} fusion(bf16[1024,2048]{1,0:T(8,128)(2,1)} %param.41, f32[1024,1024]{1,0:T(8,128)} %fusion.151, bf16[1024,2048]{1,0:T(8,128)(2,1)} %bitcast.196, bf16[2048,1024]{1,0:T(8,128)(2,1)} %param.40), kind=kOutput, calls=%fused_computation.37 | convolution fusion | flops 8602517504 | bytes 20971520 | tf_op jit(solution)/shard_map/dot_general | solution.py:220
  322.2 53.3 %all_to_all.21 = bf16[8,128,2048]{2,1,0:T(8,128)(2,1)S(1)} all-to-all(bf16[8,128,2048]{2,1,0:T(8,128)(2,1)} %bitcast.197), channel_id=1, replica_groups=mesh['dp'=16,'tx'=4,'tc'=2] {'tx','tc'}, dimensions={0} | all-to-all | bytes 8388608 | tf_op jit(solution)/shard_map/all_to_all | solution.py:90
  375.5 0.7 convert_reduce_fusion
  376.4 3.4 multiply_reduce_fusion
  379.8 2.4 add_convert_fusion
  (97 shorter events, 3.4 us)
Async XLA Ops:
  6.5 175.7 %copy-start = (bf16[256,2048]{1,0:T(8,128)(2,1)S(1)}, bf16[256,2048]{1,0:T(8,128)(2,1)}, u32[]{:S(2)}) copy-start(bf16[256,2048]{1,0:T(8,128)(2,1)} %param.33) | copy-start | bytes 3145732
  18.2 13.0 %copy-start.19 = (s32[32]{0:T(128)S(1)}, s32[32]{0:T(128)}, u32[]{:S(2)}) copy-start(s32[32]{0:T(128)} %param.25) | copy-start | bytes 388
  18.2 125.9 %all-to-all-start = ((bf16[128,1,128,256]{3,2,1,0:T(8,128)(2,1)}), bf16[128,1,128,256]{3,2,1,0:T(8,128)(2,1)}, u32[]{:S(2)}, u32[]{:S(2)}) async-start(bf16[128,1,128,256]{3,2,1,0:T(8,128)(2,1)} %bitcast.190), calls=%async_computation | async-start | bytes 16777216 | tf_op jit(solution)/shard_map/all_to_all | solution.py:163
  29.8 120.6 %all-gather.2.cloned.1.call-start = ((), (), s32[]{:S(2)}) async-start(), calls=%async_computation.4 | async-start | bytes 4718592 | tf_op jit(solution)/shard_map/all_gather | solution.py:178
  150.3 3.3 copy-start.9
  150.3 14.0 %collective-permute-start = (bf16[64,128,256]{2,1,0:T(8,128)(2,1)}, bf16[64,128,256]{2,1,0:T(8,128)(2,1)}, u32[]{:S(2)}, u32[]{:S(2)}) collective-permute-start(bf16[64,128,256]{2,1,0:T(8,128)(2,1)} %gather_fusion.2), channel_id=1, source_target_pairs={{0,1},{1,0},{2,3},{3,2},{4,5},{5,4},{6,7},{7,6},{8,9},{9,8},{10,11... | collective-permute-start | bytes 12582920 | tf_op jit(solution)/shard_map/ppermute | solution.py:173
  150.3 3.5 copy-start.2
  153.8 2.2 copy-start.16
  156.0 6.9 %copy-start.3 = (bf16[1024,2048]{1,0:T(8,128)(2,1)}, bf16[1024,2048]{1,0:T(8,128)(2,1)S(1)}, u32[]{:S(2)}) copy-start(bf16[1024,2048]{1,0:T(8,128)(2,1)S(1)} %fusion.2) | copy-start | bytes 12582916
  156.0 2.0 copy-start.18
  157.9 1.3 copy-start.14
  157.9 1.4 copy-start.15
  162.9 2.2 copy-start.1
  185.6 4.7 %copy-start.5 = (bf16[64,2048]{1,0:T(8,128)(2,1)S(1)}, bf16[64,2048]{1,0:T(8,128)(2,1)}, u32[]{:S(2)}) copy-start(bf16[64,2048]{1,0:T(8,128)(2,1)} %param.36) | copy-start | bytes 786436
  185.6 4.7 %copy-start.6 = (bf16[2048,64]{0,1:T(8,128)(2,1)S(1)}, bf16[2048,64]{0,1:T(8,128)(2,1)}, u32[]{:S(2)}) copy-start(bf16[2048,64]{0,1:T(8,128)(2,1)} %param.35) | copy-start | bytes 786436
  185.6 54.3 %all-to-all-start.1 = ((bf16[8,128,2048]{2,1,0:T(8,128)(2,1)}), bf16[8,128,2048]{2,1,0:T(8,128)(2,1)}, u32[]{:S(2)}, u32[]{:S(2)}) async-start(bf16[8,128,2048]{2,1,0:T(8,128)(2,1)} %bitcast.191), calls=%async_computation.1 | async-start | bytes 8388608 | tf_op jit(solution)/shard_map/all_to_all | solution.py:90
  190.3 52.8 %copy-start.10 = (f32[2048]{0:T(1024)S(1)}, f32[2048]{0:T(1024)}, u32[]{:S(2)}) copy-start(f32[2048]{0:T(1024)} %param.37) | copy-start | bytes 24580
  190.3 52.8 %copy-start.11 = (f32[2048]{0:T(1024)S(1)}, f32[2048]{0:T(1024)}, u32[]{:S(2)}) copy-start(f32[2048]{0:T(1024)} %param.34) | copy-start | bytes 24580
  192.3 52.6 %copy-start.12 = (f32[2048]{0:T(1024)S(1)}, f32[2048]{0:T(1024)}, u32[]{:S(2)}) copy-start(f32[2048]{0:T(1024)} %param.38) | copy-start | bytes 24580
  245.6 55.0 %copy-start.17 = (bf16[2048,1024]{1,0:T(8,128)(2,1)S(1)}, bf16[2048,1024]{1,0:T(8,128)(2,1)}, u32[]{:S(2)}) copy-start(bf16[2048,1024]{1,0:T(8,128)(2,1)} %param.39) | copy-start | bytes 12582916
  298.6 2.0 copy-start.4
  375.5 0.9 copy-start.7
  375.5 0.9 copy-start.8
  376.2 3.6 copy-start.13
Sparse Core Ops, SparseCore 0:
  32.3 66.7 all-gather.1

commit v6 on v3

--- a/solution.py
+++ b/solution.py
@@ -192,19 +192,21 @@
             )
         )
     attended = jnp.concatenate(pieces, axis=0)
-    own_x = hidden_in.astype(jnp.float32)
-    projected = lax.psum_scatter(
-        jnp.dot(attended, w_out, preferred_element_type=jnp.float32).astype(jnp.bfloat16),
-        TP,
-        scatter_dimension=0,
-        tiled=True,
+    projected = lax.psum(
+        jnp.dot(attended, w_out, preferred_element_type=jnp.float32).astype(jnp.bfloat16), TP
     ).astype(jnp.float32)
-    own_normed = lax.dynamic_slice_in_dim(normed, tp_at * own_rows, own_rows, 0)
-    mixed_rows = residual_mix(
-        own_x, projected, own_normed, post_attn_gain, laurel_left, laurel_right, laurel_gain
-    )
-    ffn_in = norm_rows(mixed_rows, pre_ffn_gain).astype(jnp.bfloat16)
-    hidden = geglu(lax.all_gather(ffn_in, TP, axis=0, tiled=True), w_gate, w_up)
+    every_mixed = residual_mix(
+        gathered.astype(jnp.float32),
+        projected,
+        normed,
+        post_attn_gain,
+        laurel_left,
+        laurel_right,
+        laurel_gain,
+    )
+    ffn_in = norm_rows(every_mixed, pre_ffn_gain).astype(jnp.bfloat16)
+    mixed_rows = lax.dynamic_slice_in_dim(every_mixed, tp_at * own_rows, own_rows, 0)
+    hidden = geglu(ffn_in, w_gate, w_up)
     down = lax.psum_scatter(
         jnp.dot(hidden, w_down, preferred_element_type=jnp.float32).astype(jnp.bfloat16),
         TP,

time: 334 us -> 350 us (1.048)
  other arithmetic: 26.4 us -> 35 us
  matrix products: 47.2 us -> 54.4 us
    psum x0 -> x1, waiting for transfers between devices: none -> 61.2 us  [per_device(): lax.psum(jnp.dot(attended, w_out, preferred_element_type=jnp.float32).ast...]
    reduce_scatter x1 -> x0, waiting for transfers between devices: 32.9 us -> none  [per_device(): lax.psum_scatter(jnp.dot(attended, w_out, preferred_element_type=jnp.floa...]
    all_gather x1 -> x0, waiting for transfers between devices: 31 us -> none  [per_device(): hidden = geglu(lax.all_gather(ffn_in, TP, axis=0, tiled=True), w_gate, w_up)]
    mul x0 -> x1, other arithmetic: none -> 10 us  [residual_mix(): (residual + norm_rows(projected, post_attn_gain) + laurel_out) * HALF_ROOT]
    dot_general x1, matrix products: 1.97 us -> 8.02 us  [residual_mix(): jnp.dot(left_part, laurel_right, preferred_element_type=jnp.float32)]
    dot_general x1, matrix products: 9.93 us -> 6.39 us  [geglu(): gate_part = jnp.dot(block, w_gate, preferred_element_type=jnp.float32)]
  transfers between devices with their start and end apart: 6 -> 5, of which waited for: 4 -> 3; matrix products, arithmetic and copies ran while one was open for 7% -> 9% of each run, Pallas kernels for 0% -> 0%
where the time goes in v6:
time: 350 us
  waiting for transfers between devices  211 us (60%)
  matrix products  54.4 us (16%)
  other arithmetic  35 us (10%)
  local copies, waits for them, and re-layouts  23.4 us (7%)
  between operations  13.7 us (4%)
  starting transfers between devices  11.8 us (3%)
    all_to_all x1, waiting for transfers between devices, per_device(): lax.all_to_all(outgoing, ALL, split_axis=0, concat_axis=0, tiled=True)  111 us
    psum x1, waiting for transfers between devices, per_device(): lax.psum(jnp.dot(attended, w_out, preferred_element_type=jnp.float32).ast...  61.2 us
    reduce_scatter x1, waiting for transfers between devices, per_device(): lax.psum_scatter(jnp.dot(hidden, w_down, preferred_element_type=jnp.float...  38.2 us
    dot_general x1, matrix products, per_device(): jnp.dot(hidden, w_down, preferred_element_type=jnp.float32)  16.6 us
    all_to_all x1, starting transfers between devices, per_device(): lax.all_to_all(outgoing, ALL, split_axis=0, concat_axis=0, tiled=True)  11.7 us
    mul x1, other arithmetic, residual_mix(): (residual + norm_rows(projected, post_attn_gain) + laurel_out) * HALF_ROOT  10 us
    gather x1, local copies, waits for them, and re-layouts, per_device(): kv_pool.reshape(pool_dev * 2 * KVH, page_len, head_dim)[row_ids.reshape(-1)]  8.76 us
    reduce_sum x4, other arithmetic, norm_rows(): jnp.mean(values * values, axis=-1, keepdims=True) + EPS  8.26 us
  transfers between devices with their start and end apart: 5, of which 3 were waited for; matrix products, arithmetic and copies ran while one was open for 9% of the time, Pallas kernels for 0%

profile of v6, /device:TPU:0, one launch (start us, length us, event | category | flops | bytes accessed | tf_op | source)
XLA Modules:
  0.0 349.7 jit_solution(10859326387376163442)
XLA Ops:
  6.5 0.8 and_select_fusion.1
  7.5 0.8 eq.45
  8.4 0.4 and_reduce_fusion
  8.9 0.2 reduce_window_sum.22
  9.5 8.8 %gather_fusion = bf16[128,128,256]{2,1,0:T(8,128)(2,1)} fusion(bf16[64,128,256]{2,1,0:T(8,128)(2,1)} %bitcast.183, s32[1024]{0:T(1024)S(1)} %pad_clamp_fusion.2), kind=kCustom, calls=%fused_computation | custom fusion | bytes 16777728 | tf_op jit(solution)/shard_map/gather | solution.py:147
  18.2 11.7 %all-to-all-start = ((bf16[128,1,128,256]{3,2,1,0:T(8,128)(2,1)}), bf16[128,1,128,256]{3,2,1,0:T(8,128)(2,1)}, u32[]{:S(2)}, u32[]{:S(2)}) async-start(bf16[128,1,128,256]{3,2,1,0:T(8,128)(2,1)} %bitcast.182), calls=%async_computation | async-start | bytes 16777216 | tf_op jit(solution)/shard_map/all_to_all | solution.py:149
  29.9 0.7 all-gather.2.cloned.1.call-update
  31.0 0.2 fusion.82
  31.6 0.8 gather_fusion.1
  32.4 0.6 fusion.157
  33.0 111.3 %all-to-all-done = bf16[128,1,128,256]{3,2,1,0:T(8,128)(2,1)} async-done(((bf16[128,1,128,256]{3,2,1,0:T(8,128)(2,1)}), bf16[128,1,128,256]{3,2,1,0:T(8,128)(2,1)}, u32[]{:S(2)}, u32[]{:S(2)}) %all-to-all-start) | async-done | bytes 8388640 | tf_op jit(solution)/shard_map/all_to_all | solution.py:149
  144.3 6.2 %gather_fusion.2 = bf16[64,128,256]{2,1,0:T(8,128)(2,1)} fusion(bf16[128,128,256]{2,1,0:T(8,128)(2,1)} %bitcast.3, s32[1024]{0:T(1024)S(1)} %pad_clamp_fusion), kind=kCustom, calls=%fused_computation.2 | custom fusion | bytes 8388864 | tf_op jit(solution)/shard_map/gather | solution.py:158
  150.4 0.7 iota_compare_fusion.3
  151.1 0.6 iota_compare_fusion.2
  151.8 3.1 fusion.2
  154.9 4.2 %multiply_reduce_fusion.4 = (f32[1024]{0:T(1024)S(1)}, f32[1024,256]{0,1:T(8,128)S(1)}) fusion(bf16[2048,1024]{1,0:T(8,128)(2,1)} %param.30, s32[]{:T(128)S(6)} %select_n.132, bf16[1024,2048]{1,0:T(8,128)(2,1)} %all-gather.2.cloned.1.call-done, f32[2048]{0:T(1024)S(1)} %copy-done.8, f32[1024]{0:T(1024)S(1)} %add_rsqrt_fusion.5), kind=kOutput, calls=%fused_computation.74 | convolution fusion | flops 1082653696 | bytes 6307844 | tf_op jit(solution)/shard_map/dot_general | solution.py:176
  159.1 1.5 multiply_reduce_fusion.5
  160.7 0.2 multiply_bitcast_fusion
  160.9 2.6 fusion.65
  163.5 0.3 fusion.160
  163.9 0.4 fusion.161
  164.2 2.9 multiply_reduce_fusion.3
  167.3 2.5 broadcast_select_fusion.1
  169.8 0.9 fusion.155
  170.8 1.3 fusion.7
  172.0 0.2 fusion.52
  172.2 2.4 fusion.9
  174.7 1.3 fusion.6
  175.9 0.2 fusion.51
  176.1 2.6 fusion.8
  178.8 0.4 fusion.75
  179.2 0.4 fusion.77
  179.6 2.5 fusion.40
  182.1 2.5 fusion.37
  184.6 3.2 convolution_convert_fusion
  187.9 8.0 %multiply_reduce_fusion.1 = (f32[1024]{0:T(1024)S(1)}, f32[1024,2048]{1,0:T(8,128)}) fusion(bf16[64,2048]{1,0:T(8,128)(2,1)S(1)} %copy-done.5, bf16[2048,64]{0,1:T(8,128)(2,1)S(1)} %copy-done.6, bf16[1024,2048]{1,0:T(8,128)(2,1)} %all-gather.2.cloned.1.call-done, f32[2048]{0:T(1024)S(1)} %copy-done.8, f32[1024]{0:T(1024)S(1)} %add_rsqrt_fusion.5), kind=kOutput, calls=%fused_computation.18 | convolution fusion | flops 549518336 | bytes 13123584 | tf_op jit(solution)/shard_map/dot_general | solution.py:76
  195.9 61.2 %all-reduce.2.cloned.1.call-done = bf16[1024,2048]{1,0:T(8,128)(2,1)} async-done(((bf16[1024,2048]{1,0:T(8,128)(2,1)}), bf16[1024,2048]{1,0:T(8,128)(2,1)}) %all-reduce.2.cloned.1.call-update) | async-done | bytes 4194320 | tf_op jit(solution)/shard_map/psum | solution.py:195
  257.1 3.1 fusion
  260.2 10.0 %broadcast_multiply_fusion = (f32[1024,2048]{1,0:T(8,128)}, f32[1024,2048]{1,0:T(8,128)S(1)}) fusion(f32[2048]{0:T(1024)S(1)} %copy-done.10, f32[1024,2048]{1,0:T(8,128)} %get-tuple-element.22, f32[1024]{0:T(1024)S(1)} %add_rsqrt_fusion, f32[2048]{0:T(1024)S(1)} %copy-done.8, f32[1024]{0:T(1024)S(1)} %add_rsqrt_fusion.5, f32[2048]{0:T(1024)S(1)} %copy-done.11, ...), kind=kLoop, calls=%fused_computation.41 | loop fusion | flops 29360128 | bytes 33591296 | tf_op jit(solution)/shard_map/mul | solution.py:78
  270.3 0.9 multiply_reduce_fusion
  271.2 3.3 copy-done.2
  274.5 1.0 copy-done.15
  275.5 6.4 %fusion.147 = f32[1024,1024]{1,0:T(8,128)} fusion(bf16[2048,1024]{1,0:T(8,128)(2,1)S(1)} %copy-done.15, f32[1024,2048]{1,0:T(8,128)S(1)} %get-tuple-element.6, f32[2048]{0:T(1024)S(1)} %copy-done.17, f32[1024]{0:T(1024)S(1)} %rsqrt_multiply_fusion), kind=kOutput, calls=%fused_computation.212 | convolution fusion | flops 4301258752 | bytes 16789504 | tf_op jit(solution)/shard_map/dot_general | solution.py:82
  281.9 16.6 %convolution_convert_fusion.1 = bf16[1024,2048]{1,0:T(8,128)(2,1)} fusion(bf16[1024,2048]{1,0:T(8,128)(2,1)} %param.41, f32[1024,1024]{1,0:T(8,128)} %fusion.147, bf16[2048,1024]{1,0:T(8,128)(2,1)} %param.40, f32[1024,2048]{1,0:T(8,128)} %copy-done.2, f32[2048]{0:T(1024)S(1)} %copy-done.17, f32[1024]{0:T(1024)S(1)} %rsqrt_multiply_fusion), kind=kOutput, calls=%fused_computation.45 | convolution fusion | flops 8608808960 | bytes 25178112 | tf_op jit(solution)/shard_map/dot_general | solution.py:211
  298.5 38.2 %reduce-scatter.2.cloned.1.call-done = bf16[128,2048]{1,0:T(8,128)(2,1)} async-done(((bf16[1024,2048]{1,0:T(8,128)(2,1)}), bf16[128,2048]{1,0:T(8,128)(2,1)}) %reduce-scatter.2.cloned.1.call-update) | async-done | bytes 524304 | tf_op jit(solution)/shard_map/reduce_scatter | solution.py:210
  336.7 1.2 fusion.44
  337.9 2.6 multiply_reduce_fusion.2
  340.6 2.5 add_convert_fusion
  (93 shorter events, 1.9 us)
Async XLA Ops:
  6.5 178.0 %copy-start = (bf16[256,2048]{1,0:T(8,128)(2,1)S(1)}, bf16[256,2048]{1,0:T(8,128)(2,1)}, u32[]{:S(2)}) copy-start(bf16[256,2048]{1,0:T(8,128)(2,1)} %param.33) | copy-start | bytes 3145732
  18.2 12.5 %copy-start.18 = (s32[32]{0:T(128)S(1)}, s32[32]{0:T(128)}, u32[]{:S(2)}) copy-start(s32[32]{0:T(128)} %param.25) | copy-start | bytes 388
  18.2 126.0 %all-to-all-start = ((bf16[128,1,128,256]{3,2,1,0:T(8,128)(2,1)}), bf16[128,1,128,256]{3,2,1,0:T(8,128)(2,1)}, u32[]{:S(2)}, u32[]{:S(2)}) async-start(bf16[128,1,128,256]{3,2,1,0:T(8,128)(2,1)} %bitcast.182), calls=%async_computation | async-start | bytes 16777216 | tf_op jit(solution)/shard_map/all_to_all | solution.py:149
  29.9 125.0 %copy-start.8 = (f32[2048]{0:T(1024)S(1)}, f32[2048]{0:T(1024)}, u32[]{:S(2)}) copy-start(f32[2048]{0:T(1024)} %param.28) | copy-start | bytes 24580
  29.9 121.9 %all-gather.2.cloned.1.call-start = ((), (), s32[]{:S(2)}) async-start(), calls=%async_computation.2 | async-start | bytes 4718592 | tf_op jit(solution)/shard_map/all_gather | solution.py:164
  30.6 226.5 %all-reduce.2.cloned.1.call-start = ((), (), s32[]{:S(2)}) async-start(), calls=%async_computation.3 | async-start | bytes 8388608 | tf_op jit(solution)/shard_map/psum | solution.py:195
  150.4 16.9 %collective-permute-start = (bf16[64,128,256]{2,1,0:T(8,128)(2,1)}, bf16[64,128,256]{2,1,0:T(8,128)(2,1)}, u32[]{:S(2)}, u32[]{:S(2)}) collective-permute-start(bf16[64,128,256]{2,1,0:T(8,128)(2,1)} %gather_fusion.2), channel_id=1, source_target_pairs={{0,1},{1,0},{2,3},{3,2},{4,5},{5,4},{6,7},{7,6},{8,9},{9,8},{10,11... | collective-permute-start | bytes 12582920 | tf_op jit(solution)/shard_map/ppermute | solution.py:159
  154.8 4.2 %copy-start.1 = (bf16[1024,2048]{1,0:T(8,128)(2,1)S(1)}, bf16[1024,2048]{1,0:T(8,128)(2,1)}, u32[]{:S(2)}) copy-start(bf16[1024,2048]{1,0:T(8,128)(2,1)} %all-gather.2.cloned.1.call-done) | copy-start | bytes 12582916
  154.8 4.2 %copy-start.16 = (bf16[2048,256]{1,0:T(8,128)(2,1)S(1)}, bf16[2048,256]{1,0:T(8,128)(2,1)}, u32[]{:S(2)}) copy-start(bf16[2048,256]{1,0:T(8,128)(2,1)} %param.29) | copy-start | bytes 3145732
  159.1 1.6 copy-start.13
  159.1 1.6 copy-start.14
  164.2 3.1 copy-start.3
  184.5 3.4 copy-start.5
  184.6 3.4 copy-start.6
  187.8 72.4 %copy-start.10 = (f32[2048]{0:T(1024)S(1)}, f32[2048]{0:T(1024)}, u32[]{:S(2)}) copy-start(f32[2048]{0:T(1024)} %param.37) | copy-start | bytes 24580
  187.8 72.4 %copy-start.11 = (f32[2048]{0:T(1024)S(1)}, f32[2048]{0:T(1024)}, u32[]{:S(2)}) copy-start(f32[2048]{0:T(1024)} %param.34) | copy-start | bytes 24580
  187.8 148.8 %reduce-scatter.2.cloned.1.call-start = ((), (), s32[]{:S(2)}) async-start(), calls=%async_computation.4 | async-start | bytes 4718592 | tf_op jit(solution)/shard_map/reduce_scatter | solution.py:210
  270.2 4.3 %copy-start.2 = (f32[1024,2048]{1,0:T(8,128)}, f32[1024,2048]{1,0:T(8,128)S(1)}, u32[]{:S(2)}) copy-start(f32[1024,2048]{1,0:T(8,128)S(1)} %get-tuple-element.6) | copy-start | bytes 25165828
  270.2 5.2 %copy-start.15 = (bf16[2048,1024]{1,0:T(8,128)(2,1)S(1)}, bf16[2048,1024]{1,0:T(8,128)(2,1)}, u32[]{:S(2)}) copy-start(bf16[2048,1024]{1,0:T(8,128)(2,1)} %param.39) | copy-start | bytes 12582916
  270.2 5.2 %copy-start.17 = (f32[2048]{0:T(1024)S(1)}, f32[2048]{0:T(1024)}, u32[]{:S(2)}) copy-start(f32[2048]{0:T(1024)} %param.38) | copy-start | bytes 24580
  281.9 56.1 %copy-start.4 = (bf16[256,2048]{1,0:T(8,128)(2,1)S(1)}, bf16[256,2048]{1,0:T(8,128)(2,1)}, u32[]{:S(2)}) copy-start(bf16[256,2048]{1,0:T(8,128)(2,1)} %param.44) | copy-start | bytes 3145732
  281.9 56.1 %copy-start.7 = (bf16[128,256]{1,0:T(8,128)(2,1)S(1)}, bf16[128,256]{1,0:T(8,128)(2,1)}, u32[]{:S(2)}) copy-start(bf16[128,256]{1,0:T(8,128)(2,1)} %param.24) | copy-start | bytes 196612
  281.9 56.1 %copy-start.9 = (f32[2048]{0:T(1024)S(1)}, f32[2048]{0:T(1024)}, u32[]{:S(2)}) copy-start(f32[2048]{0:T(1024)} %param.42) | copy-start | bytes 24580
  298.4 42.2 %copy-start.12 = (f32[2048]{0:T(1024)S(1)}, f32[2048]{0:T(1024)}, u32[]{:S(2)}) copy-start(f32[2048]{0:T(1024)} %param.45) | copy-start | bytes 24580
Sparse Core Ops, SparseCore 0:
  32.4 66.7 all-gather.1
  187.9 69.1 all-reduce.1
  298.6 38.0 reduce-scatter.1

commit v7 on v3

--- a/solution.py
+++ b/solution.py
@@ -34,35 +34,39 @@
     )
 
 
-def attend(queries, cache_keys, cache_values, fresh_keys, fresh_values, length):
+def attend(queries, cached, fresh_keys, fresh_values, length):
     new_count = queries.shape[0]
     offsets = jnp.arange(new_count, dtype=jnp.int32)
-    visible_cache = (jnp.arange(cache_keys.shape[0], dtype=jnp.int32) < length)[None, None, :]
     visible_new = (offsets[:, None] >= offsets[None, :])[None, :, :]
-    score_cache = jnp.where(
-        visible_cache,
-        jnp.einsum("nhd,ld->hnl", queries, cache_keys, preferred_element_type=jnp.float32),
-        -BIG,
-    )
-    score_new = jnp.where(
-        visible_new,
-        jnp.einsum("nhd,md->hnm", queries, fresh_keys, preferred_element_type=jnp.float32),
-        -BIG,
-    )
-    top = jnp.maximum(
-        jnp.max(score_cache, axis=-1, keepdims=True), jnp.max(score_new, axis=-1, keepdims=True)
-    )
-    exp_cache = jnp.exp(score_cache - top)
-    exp_new = jnp.exp(score_new - top)
-    total = jnp.sum(exp_cache, axis=-1, keepdims=True) + jnp.sum(exp_new, axis=-1, keepdims=True)
-    weight_cache = (exp_cache / total).astype(jnp.bfloat16)
-    weight_new = (exp_new / total).astype(jnp.bfloat16)
-    mixed = jnp.einsum(
-        "hnl,ld->nhd", weight_cache, cache_values, preferred_element_type=jnp.float32
-    )
-    mixed = mixed + jnp.einsum(
-        "hnm,md->nhd", weight_new, fresh_values, preferred_element_type=jnp.float32
-    )
+    scores = []
+    for keys, _, positions in cached:
+        scores.append(
+            jnp.where(
+                (positions < length)[None, None, :],
+                jnp.einsum("nhd,ld->hnl", queries, keys, preferred_element_type=jnp.float32),
+                -BIG,
+            )
+        )
+    scores.append(
+        jnp.where(
+            visible_new,
+            jnp.einsum("nhd,md->hnm", queries, fresh_keys, preferred_element_type=jnp.float32),
+            -BIG,
+        )
+    )
+    top = scores[0].max(axis=-1, keepdims=True)
+    for score in scores[1:]:
+        top = jnp.maximum(top, score.max(axis=-1, keepdims=True))
+    exps = [jnp.exp(score - top) for score in scores]
+    total = exps[0].sum(axis=-1, keepdims=True)
+    for part in exps[1:]:
+        total = total + part.sum(axis=-1, keepdims=True)
+    values = [entry[1] for entry in cached] + [fresh_values]
+    mixed = None
+    for part, value in zip(exps, values):
+        weight = (part / total).astype(jnp.bfloat16)
+        term = jnp.einsum("hnl,ld->nhd", weight, value, preferred_element_type=jnp.float32)
+        mixed = term if mixed is None else mixed + term
     return mixed.reshape(new_count, -1).astype(jnp.bfloat16)
 
 
@@ -140,12 +144,19 @@
     )
     local_ids = jnp.arange(pool_dev, dtype=jnp.int32)
     picked_id = jnp.sum(jnp.where(selector > 0, local_ids[None, None, :], 0), axis=-1)
-    head_ids = jnp.arange(KVH, dtype=jnp.int32)[None, :, None, None, None]
-    copy_ids = jnp.zeros((1, 1, sharing // 2, 1, 1), jnp.int32)
-    kind_ids = jnp.arange(2, dtype=jnp.int32)[None, None, None, :, None]
-    row_ids = (picked_id[:, None, None, None, :] * 2 + kind_ids) * KVH + head_ids + copy_ids
-    outgoing = kv_pool.reshape(pool_dev * 2 * KVH, page_len, head_dim)[row_ids.reshape(-1)]
-    outgoing = outgoing.reshape(devices, capacity, page_len, head_dim)
+    cores = lax.axis_size("tc")
+    half_len = page_len // cores
+    head_ids = jnp.arange(KVH, dtype=jnp.int32)[None, :, None, None, None, None]
+    copy_ids = jnp.zeros((1, 1, sharing // cores, 1, 1, 1), jnp.int32)
+    half_ids = jnp.arange(cores, dtype=jnp.int32)[None, None, None, :, None, None]
+    kind_ids = jnp.arange(2, dtype=jnp.int32)[None, None, None, None, None, :]
+    row_ids = (
+        ((picked_id[:, None, None, None, :, None] * 2 + kind_ids) * KVH + head_ids) * cores
+        + half_ids
+        + copy_ids
+    )
+    outgoing = kv_pool.reshape(pool_dev * 2 * KVH * cores, half_len, head_dim)[row_ids.reshape(-1)]
+    outgoing = outgoing.reshape(devices, capacity, 2, half_len, head_dim)
     arrived = lax.all_to_all(outgoing, ALL, split_axis=0, concat_axis=0, tiled=True)
     own_used = lax.dynamic_index_in_dim(group_used, dp_at, 0, keepdims=False)
     own_table = lax.dynamic_index_in_dim(group_table, dp_at, 0, keepdims=False)
@@ -155,11 +166,6 @@
         jnp.cumsum(present.reshape(devices, pool_dev).astype(jnp.int32), axis=1) - 1
     ).reshape(-1)
     position_at = jnp.where(own_used, own_table // pool_dev * capacity + present_rank[own_table], 0)
-    fetched = arrived.reshape(devices * capacity, page_len, head_dim)[position_at]
-    other = lax.ppermute(fetched, "tc", perm=[(0, 1), (1, 0)])
-    holds_keys = lax.axis_index("tc") == 0
-    cache_keys = jnp.where(holds_keys, fetched, other).reshape(REQ_DEV, -1, head_dim)
-    cache_values = jnp.where(holds_keys, other, fetched).reshape(REQ_DEV, -1, head_dim)
     own_lengths = lax.dynamic_slice_in_dim(cached_len, dp_at * REQ_DEV, REQ_DEV, 0)
     gathered = lax.all_gather(hidden_in, TP, axis=0, tiled=True)
     token_count = gathered.shape[0]
@@ -178,14 +184,28 @@
     fresh_values = norm_rows(
         jnp.dot(normed, value_weight, preferred_element_type=jnp.float32), 1.0
     ).astype(jnp.bfloat16)
+    arrived, queries, fresh_keys, fresh_values = lax.optimization_barrier(
+        (arrived, queries, fresh_keys, fresh_values)
+    )
+    fetched = arrived.reshape(devices * capacity, 2, half_len, head_dim)[position_at]
+    fetched = fetched.reshape(REQ_DEV, slot_count, 2, half_len, head_dim)
+    core_at = lax.axis_index("tc")
+    slot_base = jnp.arange(slot_count, dtype=jnp.int32)[:, None] * page_len
+    token_in = jnp.arange(half_len, dtype=jnp.int32)[None, :]
+    mine_pos = (slot_base + core_at * half_len + token_in).reshape(-1)
+    other_pos = (slot_base + (cores - 1 - core_at) * half_len + token_in).reshape(-1)
     pieces = []
     for request in range(REQ_DEV):
         lower = request * new_count
+        mine = fetched[request]
+        other = lax.ppermute(mine, "tc", perm=[(0, 1), (1, 0)])
         pieces.append(
             attend(
                 queries[lower : lower + new_count],
-                cache_keys[request],
-                cache_values[request],
+                (
+                    (mine[:, 0].reshape(-1, head_dim), mine[:, 1].reshape(-1, head_dim), mine_pos),
+                    (other[:, 0].reshape(-1, head_dim), other[:, 1].reshape(-1, head_dim), other_pos),
+                ),
                 fresh_keys[lower : lower + new_count],
                 fresh_values[lower : lower + new_count],
                 own_lengths[request],

time: 334 us -> 329 us (0.985)
  waiting for transfers between devices: 213 us -> 199 us
  local copies, waits for them, and re-layouts: 21.7 us -> 31.8 us
  other arithmetic: 26.4 us -> 22.9 us
    all_to_all x1, waiting for transfers between devices: 110 us -> 68.9 us  [per_device(): lax.all_to_all(outgoing, ALL, split_axis=0, concat_axis=0, tiled=True)]
    all_gather x1, waiting for transfers between devices: 0.01 us -> 22.1 us  [per_device(): gathered = lax.all_gather(hidden_in, TP, axis=0, tiled=True)]
    slice x1 -> x4, local copies, waits for them, and re-layouts: 0.91 us -> 9.21 us  [the longest x1 4.83 us: per_device(): mine = fetched[request]]
    reduce_scatter x1, waiting for transfers between devices: 32.9 us -> 38.5 us  [per_device(): lax.psum_scatter(jnp.dot(attended, w_out, preferred_element_type=jnp.floa...]
    dot_general x6 -> x10, matrix products: 8.23 us -> 9.05 us  [the longest x6 6.14 us: attend(): jnp.einsum('hnl,ld->nhd', weight, value, preferred_element_type=jnp.float32)]
  transfers between devices with their start and end apart: 6 -> 7, of which waited for: 4 -> 5; matrix products, arithmetic and copies ran while one was open for 7% -> 13% of each run, Pallas kernels for 0% -> 0%
where the time goes in v7:
time: 329 us; the launch traced here: 328 us
  waiting for transfers between devices  199 us (60%)
  matrix products  48 us (15%)
  local copies, waits for them, and re-layouts  31.8 us (10%)
  other arithmetic  22.9 us (7%)
  between operations  13.7 us (4%)
  starting transfers between devices  12.8 us (4%)
    all_to_all x1, waiting for transfers between devices, per_device(): lax.all_to_all(outgoing, ALL, split_axis=0, concat_axis=0, tiled=True)  68.9 us
    reduce_scatter x1, waiting for transfers between devices, per_device(): lax.psum_scatter(jnp.dot(attended, w_out, preferred_element_type=jnp.floa...  38.5 us
    reduce_scatter x1, waiting for transfers between devices, per_device(): lax.psum_scatter(jnp.dot(hidden, w_down, preferred_element_type=jnp.float...  38 us
    all_gather x1, waiting for transfers between devices, per_device(): hidden = geglu(lax.all_gather(ffn_in, TP, axis=0, tiled=True), w_gate, w_up)  31 us
    all_gather x1, waiting for transfers between devices, per_device(): gathered = lax.all_gather(hidden_in, TP, axis=0, tiled=True)  22.1 us
    dot_general x1, matrix products, per_device(): jnp.dot(hidden, w_down, preferred_element_type=jnp.float32)  15.6 us
    all_to_all x1, starting transfers between devices, per_device(): lax.all_to_all(outgoing, ALL, split_axis=0, concat_axis=0, tiled=True)  11.5 us
    gather x1, local copies, waits for them, and re-layouts, per_device(): kv_pool.reshape(pool_dev * 2 * KVH * cores, half_len, head_dim)  10.9 us
  transfers between devices with their start and end apart: 7, of which 5 were waited for; matrix products, arithmetic and copies ran while one was open for 13% of the time, Pallas kernels for 0%

profile of v7, /device:TPU:0, one launch (start us, length us, event | category | flops | bytes accessed | tf_op | source)
XLA Modules:
  0.0 328.5 jit_solution(1630038383537155713)
XLA Ops:
  6.5 0.7 all-gather.3.cloned.1.call-update
  7.3 0.8 eq.41
  8.1 0.7 and_select_fusion.1
  9.1 0.4 and_reduce_fusion
  10.1 10.9 %gather_fusion = bf16[256,64,256]{2,1,0:T(8,128)(2,1)} fusion(bf16[128,64,256]{2,1,0:T(8,128)(2,1)} %bitcast.219, s32[1024]{0:T(1024)S(1)} %pad_clamp_fusion.2), kind=kCustom, calls=%fused_computation | custom fusion | bytes 16778240 | tf_op jit(solution)/shard_map/gather | solution.py:158
  21.1 11.5 %all-to-all-start = ((bf16[128,1,2,64,256]{4,3,2,1,0:T(8,128)(2,1)}), bf16[128,1,2,64,256]{4,3,2,1,0:T(8,128)(2,1)}, u32[]{:S(2)}, u32[]{:S(2)}) async-start(bf16[128,1,2,64,256]{4,3,2,1,0:T(8,128)(2,1)} %bitcast.218), calls=%async_computation | async-start | bytes 16777216 | tf_op jit(solution)/shard_map/all_to_all | solution.py:160
  33.7 0.8 gather_fusion.1
  34.6 22.1 %all-gather.3.cloned.1.call-done = bf16[1024,2048]{1,0:T(8,128)(2,1)} async-done(((bf16[128,2048]{1,0:T(8,128)(2,1)}), bf16[1024,2048]{1,0:T(8,128)(2,1)}) %all-gather.3.cloned.1.call-update) | async-done | bytes 4194320 | tf_op jit(solution)/shard_map/all_gather | solution.py:170
  56.7 3.2 fusion
  60.1 1.0 fusion.2
  61.1 1.2 copy-done.15
  62.3 1.4 multiply_reduce_fusion.4
  63.7 0.6 copy-done.16
  64.3 1.3 multiply_reduce_fusion.5
  65.9 2.4 fusion.70
  68.4 1.3 multiply_reduce_fusion.3
  69.9 68.9 %all-to-all-done = bf16[128,1,2,64,256]{4,3,2,1,0:T(8,128)(2,1)} async-done(((bf16[128,1,2,64,256]{4,3,2,1,0:T(8,128)(2,1)}), bf16[128,1,2,64,256]{4,3,2,1,0:T(8,128)(2,1)}, u32[]{:S(2)}, u32[]{:S(2)}) %all-to-all-start) | async-done | bytes 8388640 | tf_op jit(solution)/shard_map/all_to_all | solution.py:160
  138.8 6.2 %gather_fusion.2 = bf16[64,2,64,256]{3,2,1,0:T(8,128)(2,1)} fusion(bf16[128,2,64,256]{3,2,1,0:T(8,128)(2,1)} %bitcast.6, s32[1024]{0:T(1024)S(1)} %pad_clamp_fusion), kind=kCustom, calls=%fused_computation.2 | custom fusion | bytes 8388864 | tf_op jit(solution)/shard_map/gather | solution.py:190
  145.0 4.8 %fusion.161 = (bf16[32,2,64,256]{3,2,1,0:T(8,128)(2,1)}, bf16[32,2,64,256]{3,2,1,0:T(8,128)(2,1)}) fusion(bf16[64,2,64,256]{3,2,1,0:T(8,128)(2,1)} %gather_fusion.2), kind=kLoop, calls=%fused_computation.243 | loop fusion | bytes 8388608 | tf_op jit(solution)/shard_map/slice | solution.py:200
  149.8 0.6 fusion.165
  150.4 1.3 fusion.131
  152.1 0.7 collective-permute-start.1
  153.5 2.5 fusion.162
  156.0 0.7 fusion.12
  156.8 0.7 fusion.14
  157.5 1.7 fusion.163
  159.2 0.7 fusion.13
  159.9 2.1 fusion.17
  162.2 1.3 fusion.26
  163.6 1.3 fusion.30
  165.5 0.7 fusion.15
  166.4 2.1 fusion.19
  168.5 1.3 fusion.22
  169.9 1.4 fusion.33
  171.2 0.4 fusion.38
  171.7 3.2 convolution_convert_fusion
  175.2 2.0 multiply_reduce_fusion.2
  177.2 38.5 %reduce-scatter.3.cloned.1.call-done = bf16[128,2048]{1,0:T(8,128)(2,1)} async-done(((bf16[1024,2048]{1,0:T(8,128)(2,1)}), bf16[128,2048]{1,0:T(8,128)(2,1)}) %reduce-scatter.3.cloned.1.call-update) | async-done | bytes 524304 | tf_op jit(solution)/shard_map/reduce_scatter | solution.py:216
  215.7 1.2 fusion.41
  216.9 2.0 multiply_reduce_fusion.1
  218.9 0.9 multiply_convert_fusion
  219.9 31.0 %all-gather.5.cloned.1.call-done = bf16[1024,2048]{1,0:T(8,128)(2,1)} async-done(((bf16[128,2048]{1,0:T(8,128)(2,1)}), bf16[1024,2048]{1,0:T(8,128)(2,1)}) %all-gather.5.cloned.1.call-update) | async-done | bytes 4194320 | tf_op jit(solution)/shard_map/all_gather | solution.py:227
  250.9 9.9 %fusion.172 = f32[1024,1024]{1,0:T(8,128)} fusion(bf16[1024,2048]{1,0:T(8,128)(2,1)} %all-gather.5.cloned.1.call-done, bf16[2048,1024]{1,0:T(8,128)(2,1)} %param.39), kind=kOutput, calls=%fused_computation.250 | convolution fusion | flops 4294967296 | bytes 12582912 | tf_op jit(solution)/shard_map/dot_general | solution.py:86
  260.8 15.6 %convolution_convert_fusion.1 = bf16[1024,2048]{1,0:T(8,128)(2,1)} fusion(bf16[1024,2048]{1,0:T(8,128)(2,1)} %param.41, f32[1024,1024]{1,0:T(8,128)} %fusion.172, bf16[1024,2048]{1,0:T(8,128)(2,1)} %all-gather.5.cloned.1.call-done, bf16[2048,1024]{1,0:T(8,128)(2,1)} %param.40), kind=kOutput, calls=%fused_computation.35 | convolution fusion | flops 8602517504 | bytes 20971520 | tf_op jit(solution)/shard_map/dot_general | solution.py:229
  276.5 38.0 %reduce-scatter.5.cloned.1.call-done = bf16[128,2048]{1,0:T(8,128)(2,1)} async-done(((bf16[1024,2048]{1,0:T(8,128)(2,1)}), bf16[128,2048]{1,0:T(8,128)(2,1)}) %reduce-scatter.5.cloned.1.call-update) | async-done | bytes 524304 | tf_op jit(solution)/shard_map/reduce_scatter | solution.py:228
  314.5 1.3 fusion.45
  315.9 3.5 %multiply_reduce_fusion = (f32[128]{0:T(128)S(1)}, f32[128,2048]{1,0:T(8,128)}) fusion(bf16[256,2048]{1,0:T(8,128)(2,1)} %param.44, bf16[2048,256]{1,0:T(8,128)(2,1)} %param.43, bf16[128,2048]{1,0:T(8,128)(2,1)} %reduce-scatter.5.cloned.1.call-done, f32[128,2048]{1,0:T(8,128)S(1)} %get-tuple-element.18, f32[2048]{0:T(1024)S(1)} %copy-done.7, ...), kind=kOutput, calls=%fused_computation.74 | convolution fusion | flops 270892928 | bytes 4793344 | tf_op jit(solution)/shard_map/dot_general | solution.py:241
  319.4 2.5 add_convert_fusion
  (111 shorter events, 5.2 us)
Async XLA Ops:
  6.5 165.1 %copy-start = (bf16[256,2048]{1,0:T(8,128)(2,1)S(1)}, bf16[256,2048]{1,0:T(8,128)(2,1)}, u32[]{:S(2)}) copy-start(bf16[256,2048]{1,0:T(8,128)(2,1)} %param.33) | copy-start | bytes 3145732
  6.5 50.1 %all-gather.3.cloned.1.call-start = ((), (), s32[]{:S(2)}) async-start(), calls=%async_computation.3 | async-start | bytes 4718592 | tf_op jit(solution)/shard_map/all_gather | solution.py:170
  21.1 11.8 %copy-start.17 = (s32[32]{0:T(128)S(1)}, s32[32]{0:T(128)}, u32[]{:S(2)}) copy-start(s32[32]{0:T(128)} %param.25) | copy-start | bytes 388
  21.1 117.7 %all-to-all-start = ((bf16[128,1,2,64,256]{4,3,2,1,0:T(8,128)(2,1)}), bf16[128,1,2,64,256]{4,3,2,1,0:T(8,128)(2,1)}, u32[]{:S(2)}, u32[]{:S(2)}) async-start(bf16[128,1,2,64,256]{4,3,2,1,0:T(8,128)(2,1)} %bitcast.218), calls=%async_computation | async-start | bytes 16777216 | tf_op jit(solution)/shard_map/all_to_all | solution.py:160
  32.6 27.3 %copy-start.8 = (f32[2048]{0:T(1024)S(1)}, f32[2048]{0:T(1024)}, u32[]{:S(2)}) copy-start(f32[2048]{0:T(1024)} %param.28) | copy-start | bytes 24580
  32.6 183.1 %reduce-scatter.3.cloned.1.call-start = ((), (), s32[]{:S(2)}) async-start(), calls=%async_computation.4 | async-start | bytes 4718592 | tf_op jit(solution)/shard_map/reduce_scatter | solution.py:216
  56.7 3.4 %copy-start.1 = (bf16[1024,2048]{1,0:T(8,128)(2,1)S(1)}, bf16[1024,2048]{1,0:T(8,128)(2,1)}, u32[]{:S(2)}) copy-start(bf16[1024,2048]{1,0:T(8,128)(2,1)} %all-gather.3.cloned.1.call-done) | copy-start | bytes 12582916
  60.1 2.2 copy-start.15
  62.3 6.1 %copy-start.2 = (bf16[1024,2048]{1,0:T(8,128)(2,1)}, bf16[1024,2048]{1,0:T(8,128)(2,1)S(1)}, u32[]{:S(2)}) copy-start(bf16[1024,2048]{1,0:T(8,128)(2,1)S(1)} %fusion.2) | copy-start | bytes 12582916
  62.3 2.0 copy-start.16
  64.3 1.3 copy-start.13
  64.3 1.4 copy-start.14
  149.8 7.7 %collective-permute-start = (bf16[32,2,64,256]{3,2,1,0:T(8,128)(2,1)}, bf16[32,2,64,256]{3,2,1,0:T(8,128)(2,1)}, u32[]{:S(2)}, u32[]{:S(2)}) collective-permute-start(bf16[32,2,64,256]{3,2,1,0:T(8,128)(2,1)} %get-tuple-element.19), channel_id=1, source_target_pairs={{0,1},{1,0},{2,3},{3,2},{4,5},{5,4},{6,7},{7,6},{8,9},{9,8},{10,11... | collective-permute-start | bytes 6291464 | tf_op jit(solution)/shard_map/ppermute | solution.py:201
  152.1 13.2 %collective-permute-start.1 = (bf16[32,2,64,256]{3,2,1,0:T(8,128)(2,1)}, bf16[32,2,64,256]{3,2,1,0:T(8,128)(2,1)S(1)}, u32[]{:S(2)}, u32[]{:S(2)}) collective-permute-start(bf16[32,2,64,256]{3,2,1,0:T(8,128)(2,1)} %get-tuple-element.20), channel_id=1, source_target_pairs={{0,1},{1,0},{2,3},{3,2},{4,5},{5,4},{6,7},{7,6},{8,9},{9,8},{10,11... | collective-permute-start | bytes 6291464 | tf_op jit(solution)/shard_map/ppermute | solution.py:201
  171.6 3.6 %copy-start.4 = (bf16[64,2048]{1,0:T(8,128)(2,1)S(1)}, bf16[64,2048]{1,0:T(8,128)(2,1)}, u32[]{:S(2)}) copy-start(bf16[64,2048]{1,0:T(8,128)(2,1)} %param.36) | copy-start | bytes 786436
  171.6 3.6 %copy-start.5 = (bf16[2048,64]{0,1:T(8,128)(2,1)S(1)}, bf16[2048,64]{0,1:T(8,128)(2,1)}, u32[]{:S(2)}) copy-start(bf16[2048,64]{0,1:T(8,128)(2,1)} %param.35) | copy-start | bytes 786436
  174.9 42.1 %copy-start.9 = (f32[2048]{0:T(1024)S(1)}, f32[2048]{0:T(1024)}, u32[]{:S(2)}) copy-start(f32[2048]{0:T(1024)} %param.37) | copy-start | bytes 24580
  174.9 42.1 %copy-start.10 = (f32[2048]{0:T(1024)S(1)}, f32[2048]{0:T(1024)}, u32[]{:S(2)}) copy-start(f32[2048]{0:T(1024)} %param.34) | copy-start | bytes 24580
  174.9 44.0 %copy-start.11 = (f32[2048]{0:T(1024)S(1)}, f32[2048]{0:T(1024)}, u32[]{:S(2)}) copy-start(f32[2048]{0:T(1024)} %param.38) | copy-start | bytes 24580
  174.9 76.0 %all-gather.5.cloned.1.call-start = ((), (), s32[]{:S(2)}) async-start(), calls=%async_computation.5 | async-start | bytes 4718592 | tf_op jit(solution)/shard_map/all_gather | solution.py:227
  219.9 94.6 %reduce-scatter.5.cloned.1.call-start = ((), (), s32[]{:S(2)}) async-start(), calls=%async_computation.6 | async-start | bytes 4718592 | tf_op jit(solution)/shard_map/reduce_scatter | solution.py:228
  276.5 39.4 %copy-start.6 = (bf16[128,256]{1,0:T(8,128)(2,1)S(1)}, bf16[128,256]{1,0:T(8,128)(2,1)}, u32[]{:S(2)}) copy-start(bf16[128,256]{1,0:T(8,128)(2,1)} %param.24) | copy-start | bytes 196612
  276.5 39.4 %copy-start.7 = (f32[2048]{0:T(1024)S(1)}, f32[2048]{0:T(1024)}, u32[]{:S(2)}) copy-start(f32[2048]{0:T(1024)} %param.42) | copy-start | bytes 24580
  276.5 43.0 %copy-start.12 = (f32[2048]{0:T(1024)S(1)}, f32[2048]{0:T(1024)}, u32[]{:S(2)}) copy-start(f32[2048]{0:T(1024)} %param.45) | copy-start | bytes 24580
  314.5 4.9 %copy-start.3 = (bf16[128,2048]{1,0:T(8,128)(2,1)S(1)}, bf16[128,2048]{1,0:T(8,128)(2,1)}, u32[]{:S(2)}) copy-start(bf16[128,2048]{1,0:T(8,128)(2,1)} %reduce-scatter.5.cloned.1.call-done) | copy-start | bytes 1572868
Sparse Core Ops, SparseCore 0:
  9.0 47.5 all-gather.2
  175.0 40.6 reduce-scatter.2
  220.0 30.8 all-gather.4
  276.6 37.8 reduce-scatter.4

commit v8 on v7

--- a/solution.py
+++ b/solution.py
@@ -34,10 +34,11 @@
     )
 
 
-def attend(queries, cached, fresh_keys, fresh_values, length):
+def attend_part(queries, cached, fresh_keys, fresh_values, fresh_start, length):
     new_count = queries.shape[0]
     offsets = jnp.arange(new_count, dtype=jnp.int32)
-    visible_new = (offsets[:, None] >= offsets[None, :])[None, :, :]
+    key_offsets = fresh_start + jnp.arange(fresh_keys.shape[0], dtype=jnp.int32)
+    visible_new = (offsets[:, None] >= key_offsets[None, :])[None, :, :]
     scores = []
     for keys, _, positions in cached:
         scores.append(
@@ -64,10 +65,11 @@
     values = [entry[1] for entry in cached] + [fresh_values]
     mixed = None
     for part, value in zip(exps, values):
-        weight = (part / total).astype(jnp.bfloat16)
-        term = jnp.einsum("hnl,ld->nhd", weight, value, preferred_element_type=jnp.float32)
+        term = jnp.einsum(
+            "hnl,ld->nhd", part.astype(jnp.bfloat16), value, preferred_element_type=jnp.float32
+        )
         mixed = term if mixed is None else mixed + term
-    return mixed.reshape(new_count, -1).astype(jnp.bfloat16)
+    return mixed, top, total
 
 
 def residual_mix(
@@ -145,18 +147,20 @@
     local_ids = jnp.arange(pool_dev, dtype=jnp.int32)
     picked_id = jnp.sum(jnp.where(selector > 0, local_ids[None, None, :], 0), axis=-1)
     cores = lax.axis_size("tc")
-    half_len = page_len // cores
+    pair = sharing // cores
+    part_len = page_len // (cores * pair)
     head_ids = jnp.arange(KVH, dtype=jnp.int32)[None, :, None, None, None, None]
-    copy_ids = jnp.zeros((1, 1, sharing // cores, 1, 1, 1), jnp.int32)
-    half_ids = jnp.arange(cores, dtype=jnp.int32)[None, None, None, :, None, None]
+    pair_ids = jnp.arange(pair, dtype=jnp.int32)[None, None, :, None, None, None]
+    core_ids = jnp.arange(cores, dtype=jnp.int32)[None, None, None, :, None, None]
     kind_ids = jnp.arange(2, dtype=jnp.int32)[None, None, None, None, None, :]
     row_ids = (
         ((picked_id[:, None, None, None, :, None] * 2 + kind_ids) * KVH + head_ids) * cores
-        + half_ids
-        + copy_ids
-    )
-    outgoing = kv_pool.reshape(pool_dev * 2 * KVH * cores, half_len, head_dim)[row_ids.reshape(-1)]
-    outgoing = outgoing.reshape(devices, capacity, 2, half_len, head_dim)
+        + core_ids
+    ) * pair + pair_ids
+    outgoing = kv_pool.reshape(pool_dev * 2 * KVH * cores * pair, part_len, head_dim)[
+        row_ids.reshape(-1)
+    ]
+    outgoing = outgoing.reshape(devices, capacity, 2, part_len, head_dim)
     arrived = lax.all_to_all(outgoing, ALL, split_axis=0, concat_axis=0, tiled=True)
     own_used = lax.dynamic_index_in_dim(group_used, dp_at, 0, keepdims=False)
     own_table = lax.dynamic_index_in_dim(group_table, dp_at, 0, keepdims=False)
@@ -184,33 +188,54 @@
     fresh_values = norm_rows(
         jnp.dot(normed, value_weight, preferred_element_type=jnp.float32), 1.0
     ).astype(jnp.bfloat16)
-    arrived, queries, fresh_keys, fresh_values = lax.optimization_barrier(
-        (arrived, queries, fresh_keys, fresh_values)
-    )
-    fetched = arrived.reshape(devices * capacity, 2, half_len, head_dim)[position_at]
-    fetched = fetched.reshape(REQ_DEV, slot_count, 2, half_len, head_dim)
+    swap_pair = [(t, t ^ cores) for t in range(tp_count)]
+    neighbour_queries = lax.ppermute(queries, TP, perm=swap_pair)
+    arrived, queries, neighbour_queries, fresh_keys, fresh_values = lax.optimization_barrier(
+        (arrived, queries, neighbour_queries, fresh_keys, fresh_values)
+    )
+    both_queries = jnp.concatenate([queries, neighbour_queries], axis=1)
+    fetched = arrived.reshape(devices * capacity, 2, part_len, head_dim)[position_at]
+    fetched = fetched.reshape(REQ_DEV, slot_count, 2, part_len, head_dim)
     core_at = lax.axis_index("tc")
+    pair_at = lax.axis_index("tx") % pair
     slot_base = jnp.arange(slot_count, dtype=jnp.int32)[:, None] * page_len
-    token_in = jnp.arange(half_len, dtype=jnp.int32)[None, :]
-    mine_pos = (slot_base + core_at * half_len + token_in).reshape(-1)
-    other_pos = (slot_base + (cores - 1 - core_at) * half_len + token_in).reshape(-1)
+    token_in = jnp.arange(part_len, dtype=jnp.int32)[None, :]
+    mine_pos = (slot_base + (core_at * pair + pair_at) * part_len + token_in).reshape(-1)
+    other_pos = (slot_base + ((cores - 1 - core_at) * pair + pair_at) * part_len + token_in).reshape(
+        -1
+    )
+    new_part = new_count // pair
     pieces = []
     for request in range(REQ_DEV):
         lower = request * new_count
         mine = fetched[request]
         other = lax.ppermute(mine, "tc", perm=[(0, 1), (1, 0)])
-        pieces.append(
-            attend(
-                queries[lower : lower + new_count],
-                (
-                    (mine[:, 0].reshape(-1, head_dim), mine[:, 1].reshape(-1, head_dim), mine_pos),
-                    (other[:, 0].reshape(-1, head_dim), other[:, 1].reshape(-1, head_dim), other_pos),
-                ),
-                fresh_keys[lower : lower + new_count],
-                fresh_values[lower : lower + new_count],
-                own_lengths[request],
-            )
-        )
+        fresh_k = lax.dynamic_slice_in_dim(
+            fresh_keys[lower : lower + new_count], pair_at * new_part, new_part, 0
+        )
+        fresh_v = lax.dynamic_slice_in_dim(
+            fresh_values[lower : lower + new_count], pair_at * new_part, new_part, 0
+        )
+        out, top, total = attend_part(
+            both_queries[lower : lower + new_count],
+            (
+                (mine[:, 0].reshape(-1, head_dim), mine[:, 1].reshape(-1, head_dim), mine_pos),
+                (other[:, 0].reshape(-1, head_dim), other[:, 1].reshape(-1, head_dim), other_pos),
+            ),
+            fresh_k,
+            fresh_v,
+            pair_at * new_part,
+            own_lengths[request],
+        )
+        far_out, far_top, far_total = lax.ppermute(
+            (out[:, 1].astype(jnp.bfloat16), top[1], total[1]), TP, perm=swap_pair
+        )
+        best = jnp.maximum(top[0], far_top)
+        near_scale = jnp.exp(top[0] - best)
+        far_scale = jnp.exp(far_top - best)
+        whole = total[0] * near_scale + far_total * far_scale
+        merged = out[:, 0] * near_scale + far_out.astype(jnp.float32) * far_scale
+        pieces.append((merged / whole).astype(jnp.bfloat16))
     attended = jnp.concatenate(pieces, axis=0)
     own_x = hidden_in.astype(jnp.float32)
     projected = lax.psum_scatter(

time: 329 us -> 284 us (0.86)
  waiting for transfers between devices: 199 us -> 162 us
  local copies, waits for them, and re-layouts: 31.8 us -> 16.1 us
  starting transfers between devices: 12.8 us -> 20 us
    all_to_all x1, waiting for transfers between devices: 68.9 us -> 10.1 us  [per_device(): lax.all_to_all(outgoing, ALL, split_axis=0, concat_axis=0, tiled=True)]
    all_gather x1, waiting for transfers between devices: 22.1 us -> 34.8 us  [per_device(): gathered = lax.all_gather(hidden_in, TP, axis=0, tiled=True)]
    ppermute x0 -> x7, waiting for transfers between devices: none -> 10.5 us  [the longest x6 5.32 us: per_device(): lax.ppermute((out[:, 1].astype(jnp.bfloat16), top[1], total[1]), TP, perm...]
    gather x2, local copies, waits for them, and re-layouts: 17.1 us -> 7.85 us  [the longest x1 4.99 us: per_device(): kv_pool.reshape(pool_dev * 2 * KVH * cores * pair, part_len, head_dim)]
    ppermute x0 -> x7, starting transfers between devices: none -> 7.78 us  [the longest x6 6.62 us: per_device(): lax.ppermute((out[:, 1].astype(jnp.bfloat16), top[1], total[1]), TP, perm...]
    slice x1, local copies, waits for them, and re-layouts: 4.83 us -> 0.17 us  [per_device(): mine = fetched[request]]
  transfers between devices with their start and end apart: 7 -> 14, of which waited for: 5 -> 7; matrix products, arithmetic and copies ran while one was open for 13% -> 14% of each run, Pallas kernels for 0% -> 0%
where the time goes in v8:
time: 284 us; the launch traced here: 283 us
  waiting for transfers between devices  162 us (57%)
  matrix products  47 us (17%)
  other arithmetic  24.2 us (9%)
  starting transfers between devices  20 us (7%)
  local copies, waits for them, and re-layouts  16.1 us (6%)
  between operations  13.9 us (5%)
    reduce_scatter x1, waiting for transfers between devices, per_device(): lax.psum_scatter(jnp.dot(hidden, w_down, preferred_element_type=jnp.float...  38 us
    reduce_scatter x1, waiting for transfers between devices, per_device(): lax.psum_scatter(jnp.dot(attended, w_out, preferred_element_type=jnp.floa...  37 us
    all_gather x1, waiting for transfers between devices, per_device(): gathered = lax.all_gather(hidden_in, TP, axis=0, tiled=True)  34.8 us
    all_gather x1, waiting for transfers between devices, per_device(): hidden = geglu(lax.all_gather(ffn_in, TP, axis=0, tiled=True), w_gate, w_up)  31.1 us
    dot_general x1, matrix products, per_device(): jnp.dot(hidden, w_down, preferred_element_type=jnp.float32)  15.6 us
    all_to_all x1, starting transfers between devices, per_device(): lax.all_to_all(outgoing, ALL, split_axis=0, concat_axis=0, tiled=True)  11.7 us
    all_to_all x1, waiting for transfers between devices, per_device(): lax.all_to_all(outgoing, ALL, split_axis=0, concat_axis=0, tiled=True)  10.1 us
    dot_general x1, matrix products, geglu(): gate_part = jnp.dot(block, w_gate, preferred_element_type=jnp.float32)  9.93 us
  transfers between devices with their start and end apart: 14, of which 7 were waited for; matrix products, arithmetic and copies ran while one was open for 14% of the time, Pallas kernels for 0%

profile of v8, /device:TPU:0, one launch (start us, length us, event | category | flops | bytes accessed | tf_op | source)
XLA Modules:
  0.0 283.5 jit_solution(7998103976774345288)
XLA Ops:
  8.3 0.8 eq.43
  10.8 0.8 gather_fusion.1
  11.6 5.0 %gather_fusion = bf16[256,32,256]{2,1,0:T(8,128)(2,1)} fusion(bf16[256,32,256]{2,1,0:T(8,128)(2,1)} %bitcast.237, s32[1024]{0:T(1024)S(1)} %get-tuple-element.76), kind=kCustom, calls=%fused_computation | custom fusion | bytes 8389632 | tf_op jit(solution)/shard_map/gather | solution.py:160
  16.6 11.7 %all-to-all-start = ((bf16[128,1,2,32,256]{4,3,2,1,0:T(8,128)(2,1)}), bf16[128,1,2,32,256]{4,3,2,1,0:T(8,128)(2,1)}, u32[]{:S(2)}, u32[]{:S(2)}) async-start(bf16[128,1,2,32,256]{4,3,2,1,0:T(8,128)(2,1)} %bitcast.236), calls=%async_computation | async-start | bytes 8388608 | tf_op jit(solution)/shard_map/all_to_all | solution.py:164
  29.2 1.3 fusion.155
  31.1 34.8 %all-gather.3.cloned.1.call-done = bf16[1024,2048]{1,0:T(8,128)(2,1)} async-done(((bf16[128,2048]{1,0:T(8,128)(2,1)}), bf16[1024,2048]{1,0:T(8,128)(2,1)}) %all-gather.3.cloned.1.call-update) | async-done | bytes 4194320 | tf_op jit(solution)/shard_map/all_gather | solution.py:174
  65.8 3.2 %fusion = f32[1024]{0:T(1024)S(1)} fusion(bf16[1024,2048]{1,0:T(8,128)(2,1)} %all-gather.3.cloned.1.call-done), kind=kLoop, calls=%fused_computation.5 | loop fusion | flops 6290432 | bytes 4198400 | tf_op jit(solution)/shard_map/reduce_sum | solution.py:21
  69.3 1.0 fusion.2
  70.3 1.2 copy-done.22
  71.5 1.3 multiply_reduce_fusion.4
  73.5 1.3 multiply_reduce_fusion.5
  75.1 2.4 fusion.86
  77.5 1.2 collective-permute-start
  78.7 1.4 multiply_reduce_fusion.3
  80.1 0.9 maximum_bitcast_fusion
  80.9 1.0 multiply_convert_fusion.1
  81.9 10.1 %all-to-all-done = bf16[128,1,2,32,256]{4,3,2,1,0:T(8,128)(2,1)} async-done(((bf16[128,1,2,32,256]{4,3,2,1,0:T(8,128)(2,1)}), bf16[128,1,2,32,256]{4,3,2,1,0:T(8,128)(2,1)}, u32[]{:S(2)}, u32[]{:S(2)}) %all-to-all-start) | async-done | bytes 4194336 | tf_op jit(solution)/shard_map/all_to_all | solution.py:164
  92.0 5.2 %collective-permute-done = bf16[1024,1,256]{0,2,1:T(8,128)(2,1)S(1)} collective-permute-done((bf16[1024,1,256]{0,2,1:T(8,128)(2,1)S(1)}, bf16[1024,1,256]{0,2,1:T(8,128)(2,1)S(1)}, u32[]{:S(2)}, u32[]{:S(2)}) %collective-permute-start) | collective-permute-done | bytes 524320 | tf_op jit(solution)/shard_map/ppermute | solution.py:192
  97.2 0.9 constant_dynamic-update-slice_fusion.1
  98.2 2.9 %gather_fusion.2 = bf16[64,2,32,256]{3,2,1,0:T(8,128)(2,1)S(1)} fusion(bf16[128,2,32,256]{3,2,1,0:T(8,128)(2,1)} %bitcast.6, s32[1024]{0:T(1024)S(1)} %get-tuple-element.75), kind=kCustom, calls=%fused_computation.2 | custom fusion | bytes 4194560 | tf_op jit(solution)/shard_map/gather | solution.py:197
  101.4 0.7 copy-done.8
  103.7 0.7 bitcast_reduce_fusion.3
  104.4 0.7 bitcast_reduce_fusion.1
  105.3 0.7 bitcast_reduce_fusion.2
  106.2 1.8 fusion.18
  108.1 2.0 collective-permute-start.2
  110.1 1.1 fusion.30
  111.2 1.1 fusion.48
  112.9 0.7 bitcast_reduce_fusion
  113.9 1.8 fusion.22
  115.7 2.0 collective-permute-start.8
  117.8 1.1 fusion.26
  118.9 1.1 fusion.51
  120.4 2.2 collective-permute-start.7
  122.8 5.3 %collective-permute-done.7 = bf16[512,256]{0,1:T(8,128)(2,1)S(1)} collective-permute-done((bf16[512,256]{0,1:T(8,128)(2,1)S(1)}, bf16[512,256]{0,1:T(8,128)(2,1)S(1)}, u32[]{:S(2)}, u32[]{:S(2)}) %collective-permute-start.7) | collective-permute-done | bytes 262176 | tf_op jit(solution)/shard_map/ppermute | solution.py:230
  128.2 3.3 %convolution_convert_fusion = bf16[1024,2048]{1,0:T(8,128)(2,1)} fusion(bf16[256,2048]{1,0:T(8,128)(2,1)S(1)} %copy-done, bf16[512,256]{0,1:T(8,128)(2,1)S(1)} %fusion.106, bf16[512,256]{0,1:T(8,128)(2,1)S(1)} %fusion.105), kind=kOutput, calls=%fused_computation.30 | convolution fusion | flops 1076887552 | bytes 5767168 | tf_op jit(solution)/shard_map/dot_general | solution.py:242
  131.6 2.0 multiply_reduce_fusion.2
  133.7 37.0 %reduce-scatter.3.cloned.1.call-done = bf16[128,2048]{1,0:T(8,128)(2,1)} async-done(((bf16[1024,2048]{1,0:T(8,128)(2,1)}), bf16[128,2048]{1,0:T(8,128)(2,1)}) %reduce-scatter.3.cloned.1.call-update) | async-done | bytes 524304 | tf_op jit(solution)/shard_map/reduce_scatter | solution.py:241
  170.7 1.2 fusion.55
  172.0 1.8 multiply_reduce_fusion.1
  173.8 0.9 multiply_convert_fusion
  174.8 31.1 %all-gather.5.cloned.1.call-done = bf16[1024,2048]{1,0:T(8,128)(2,1)} async-done(((bf16[128,2048]{1,0:T(8,128)(2,1)}), bf16[1024,2048]{1,0:T(8,128)(2,1)}) %all-gather.5.cloned.1.call-update) | async-done | bytes 4194320 | tf_op jit(solution)/shard_map/all_gather | solution.py:252
  206.0 9.9 %fusion.214 = f32[1024,1024]{1,0:T(8,128)} fusion(bf16[1024,2048]{1,0:T(8,128)(2,1)} %all-gather.5.cloned.1.call-done, bf16[2048,1024]{1,0:T(8,128)(2,1)} %param.39), kind=kOutput, calls=%fused_computation.296 | convolution fusion | flops 4294967296 | bytes 12582912 | tf_op jit(solution)/shard_map/dot_general | solution.py:88
  215.9 15.6 %convolution_convert_fusion.1 = bf16[1024,2048]{1,0:T(8,128)(2,1)} fusion(bf16[1024,2048]{1,0:T(8,128)(2,1)} %param.41, f32[1024,1024]{1,0:T(8,128)} %fusion.214, bf16[1024,2048]{1,0:T(8,128)(2,1)} %all-gather.5.cloned.1.call-done, bf16[2048,1024]{1,0:T(8,128)(2,1)} %param.40), kind=kOutput, calls=%fused_computation.31 | convolution fusion | flops 8602517504 | bytes 20971520 | tf_op jit(solution)/shard_map/dot_general | solution.py:254
  231.5 38.0 %reduce-scatter.5.cloned.1.call-done = bf16[128,2048]{1,0:T(8,128)(2,1)} async-done(((bf16[1024,2048]{1,0:T(8,128)(2,1)}), bf16[128,2048]{1,0:T(8,128)(2,1)}) %reduce-scatter.5.cloned.1.call-update) | async-done | bytes 524304 | tf_op jit(solution)/shard_map/reduce_scatter | solution.py:253
  269.6 1.3 fusion.59
  270.9 3.5 %multiply_reduce_fusion = (f32[128]{0:T(128)S(1)}, f32[128,2048]{1,0:T(8,128)}) fusion(bf16[256,2048]{1,0:T(8,128)(2,1)} %param.44, bf16[2048,256]{1,0:T(8,128)(2,1)} %param.43, bf16[128,2048]{1,0:T(8,128)(2,1)} %reduce-scatter.5.cloned.1.call-done, f32[128,2048]{1,0:T(8,128)S(1)} %get-tuple-element.20, f32[2048]{0:T(1024)S(1)} %copy-done.14, ...), kind=kOutput, calls=%fused_computation.80 | convolution fusion | flops 270892928 | bytes 4793344 | tf_op jit(solution)/shard_map/dot_general | solution.py:266
  274.5 2.5 add_convert_fusion
  (154 shorter events, 10.0 us)
Async XLA Ops:
  6.5 121.7 %copy-start = (bf16[256,2048]{1,0:T(8,128)(2,1)S(1)}, bf16[256,2048]{1,0:T(8,128)(2,1)}, u32[]{:S(2)}) copy-start(bf16[256,2048]{1,0:T(8,128)(2,1)} %param.33) | copy-start | bytes 3145732
  6.5 59.3 %all-gather.3.cloned.1.call-start = ((), (), s32[]{:S(2)}) async-start(), calls=%async_computation.3 | async-start | bytes 4718592 | tf_op jit(solution)/shard_map/all_gather | solution.py:174
  16.6 11.8 %copy-start.24 = (s32[32]{0:T(128)S(1)}, s32[32]{0:T(128)}, u32[]{:S(2)}) copy-start(s32[32]{0:T(128)} %param.25) | copy-start | bytes 388
  16.6 75.4 %all-to-all-start = ((bf16[128,1,2,32,256]{4,3,2,1,0:T(8,128)(2,1)}), bf16[128,1,2,32,256]{4,3,2,1,0:T(8,128)(2,1)}, u32[]{:S(2)}, u32[]{:S(2)}) async-start(bf16[128,1,2,32,256]{4,3,2,1,0:T(8,128)(2,1)} %bitcast.236), calls=%async_computation | async-start | bytes 8388608 | tf_op jit(solution)/shard_map/all_to_all | solution.py:164
  28.3 40.7 %copy-start.15 = (f32[2048]{0:T(1024)S(1)}, f32[2048]{0:T(1024)}, u32[]{:S(2)}) copy-start(f32[2048]{0:T(1024)} %param.28) | copy-start | bytes 24580
  28.4 142.3 %reduce-scatter.3.cloned.1.call-start = ((), (), s32[]{:S(2)}) async-start(), calls=%async_computation.4 | async-start | bytes 4718592 | tf_op jit(solution)/shard_map/reduce_scatter | solution.py:241
  65.8 3.4 %copy-start.2 = (bf16[1024,2048]{1,0:T(8,128)(2,1)S(1)}, bf16[1024,2048]{1,0:T(8,128)(2,1)}, u32[]{:S(2)}) copy-start(bf16[1024,2048]{1,0:T(8,128)(2,1)} %all-gather.3.cloned.1.call-done) | copy-start | bytes 12582916
  69.3 2.2 copy-start.22
  71.5 7.2 %copy-start.4 = (bf16[1024,2048]{1,0:T(8,128)(2,1)}, bf16[1024,2048]{1,0:T(8,128)(2,1)S(1)}, u32[]{:S(2)}) copy-start(bf16[1024,2048]{1,0:T(8,128)(2,1)S(1)} %fusion.2) | copy-start | bytes 12582916
  71.5 2.0 copy-start.23
  73.5 1.4 copy-start.20
  73.5 1.4 copy-start.21
  77.5 19.7 %collective-permute-start = (bf16[1024,1,256]{0,2,1:T(8,128)(2,1)S(1)}, bf16[1024,1,256]{0,2,1:T(8,128)(2,1)S(1)}, u32[]{:S(2)}, u32[]{:S(2)}) collective-permute-start(bf16[1024,1,256]{0,2,1:T(8,128)(2,1)S(1)} %pad_maximum_fusion), channel_id=1, source_target_pairs={{0,2},{1,3},{2,0},{3,1},{4,6},{5,7},{6,4},{7,5},{8,10},{9,11},{10,... | collective-permute-start | bytes 1572872 | tf_op jit(solution)/shard_map/ppermute | solution.py:192
  97.2 1.0 copy-start.9
  101.1 1.0 copy-start.8
  101.1 1.2 copy-start.7
  101.1 1.5 copy-start.3
  101.1 1.7 copy-start.10
  101.3 3.9 %collective-permute-start.1 = (bf16[32,2,32,256]{3,2,1,0:T(8,128)(2,1)S(1)}, bf16[32,2,32,256]{3,2,1,0:T(8,128)(2,1)S(1)}, u32[]{:S(2)}, u32[]{:S(2)}) collective-permute-start(bf16[32,2,32,256]{3,2,1,0:T(8,128)(2,1)S(1)} %get-tuple-element.27), channel_id=1, source_target_pairs={{0,1},{1,0},{2,3},{3,2},{4,5},{5,4},{6,7},{7,6},{8,9},{9,8},{10,11... | collective-permute-start | bytes 3145736 | tf_op jit(solution)/shard_map/ppermute | solution.py:212
  102.3 10.5 %collective-permute-start.5 = (bf16[32,2,32,256]{3,2,1,0:T(8,128)(2,1)S(1)}, bf16[32,2,32,256]{3,2,1,0:T(8,128)(2,1)S(1)}, u32[]{:S(2)}, u32[]{:S(2)}) collective-permute-start(bf16[32,2,32,256]{3,2,1,0:T(8,128)(2,1)S(1)} %get-tuple-element.28), channel_id=1, source_target_pairs={{0,1},{1,0},{2,3},{3,2},{4,5},{5,4},{6,7},{7,6},{8,9},{9,8},{10,11... | collective-permute-start | bytes 3145736 | tf_op jit(solution)/shard_map/ppermute | solution.py:212
  108.0 12.3 %collective-permute-start.4 = (f32[512,1]{0,1:T(1,128)S(1)}, f32[512,1]{0,1:T(1,128)S(1)}, u32[]{:S(2)}, u32[]{:S(2)}) collective-permute-start(f32[512,1]{0,1:T(1,128)S(1)} %slice_bitcast_fusion.6), channel_id=1, source_target_pairs={{0,2},{1,3},{2,0},{3,1},{4,6},{5,7},{6,4},{7,5},{8,10},{9,11},{10,... | collective-permute-start | bytes 6152 | tf_op jit(solution)/shard_map/ppermute | solution.py:230
  108.1 14.5 %collective-permute-start.2 = (f32[512,1]{0,1:T(1,128)S(1)}, f32[512,1]{0,1:T(1,128)S(1)}, u32[]{:S(2)}, u32[]{:S(2)}) collective-permute-start(f32[512,1]{0,1:T(1,128)S(1)} %slice_bitcast_fusion.8), channel_id=1, source_target_pairs={{0,2},{1,3},{2,0},{3,1},{4,6},{5,7},{6,4},{7,5},{8,10},{9,11},{10,... | collective-permute-start | bytes 6152 | tf_op jit(solution)/shard_map/ppermute | solution.py:230
  112.7 10.0 %collective-permute-start.3 = (bf16[512,256]{0,1:T(8,128)(2,1)S(1)}, bf16[512,256]{0,1:T(8,128)(2,1)S(1)}, u32[]{:S(2)}, u32[]{:S(2)}) collective-permute-start(bf16[512,256]{0,1:T(8,128)(2,1)S(1)} %fusion.121), channel_id=1, source_target_pairs={{0,2},{1,3},{2,0},{3,1},{4,6},{5,7},{6,4},{7,5},{8,10},{9,11},{10,... | collective-permute-start | bytes 786440 | tf_op jit(solution)/shard_map/ppermute | solution.py:230
  115.7 6.9 %collective-permute-start.8 = (f32[512,1]{0,1:T(1,128)S(1)}, f32[512,1]{0,1:T(1,128)S(1)}, u32[]{:S(2)}, u32[]{:S(2)}) collective-permute-start(f32[512,1]{0,1:T(1,128)S(1)} %slice_bitcast_fusion.2), channel_id=1, source_target_pairs={{0,2},{1,3},{2,0},{3,1},{4,6},{5,7},{6,4},{7,5},{8,10},{9,11},{10,... | collective-permute-start | bytes 6152 | tf_op jit(solution)/shard_map/ppermute | solution.py:230
  117.7 4.9 %collective-permute-start.6 = (f32[512,1]{0,1:T(1,128)S(1)}, f32[512,1]{0,1:T(1,128)S(1)}, u32[]{:S(2)}, u32[]{:S(2)}) collective-permute-start(f32[512,1]{0,1:T(1,128)S(1)} %slice_bitcast_fusion.4), channel_id=1, source_target_pairs={{0,2},{1,3},{2,0},{3,1},{4,6},{5,7},{6,4},{7,5},{8,10},{9,11},{10,... | collective-permute-start | bytes 6152 | tf_op jit(solution)/shard_map/ppermute | solution.py:230
  120.4 7.7 %collective-permute-start.7 = (bf16[512,256]{0,1:T(8,128)(2,1)S(1)}, bf16[512,256]{0,1:T(8,128)(2,1)S(1)}, u32[]{:S(2)}, u32[]{:S(2)}) collective-permute-start(bf16[512,256]{0,1:T(8,128)(2,1)S(1)} %fusion.122), channel_id=1, source_target_pairs={{0,2},{1,3},{2,0},{3,1},{4,6},{5,7},{6,4},{7,5},{8,10},{9,11},{10,... | collective-permute-start | bytes 786440 | tf_op jit(solution)/shard_map/ppermute | solution.py:230
  128.2 3.4 %copy-start.11 = (bf16[64,2048]{1,0:T(8,128)(2,1)S(1)}, bf16[64,2048]{1,0:T(8,128)(2,1)}, u32[]{:S(2)}) copy-start(bf16[64,2048]{1,0:T(8,128)(2,1)} %param.36) | copy-start | bytes 786436
  128.2 3.4 %copy-start.12 = (bf16[2048,64]{0,1:T(8,128)(2,1)S(1)}, bf16[2048,64]{0,1:T(8,128)(2,1)}, u32[]{:S(2)}) copy-start(bf16[2048,64]{0,1:T(8,128)(2,1)} %param.35) | copy-start | bytes 786436
  131.5 40.4 %copy-start.6 = (bf16[128,2048]{1,0:T(8,128)(2,1)S(1)}, bf16[128,2048]{1,0:T(8,128)(2,1)}, u32[]{:S(2)}) copy-start(bf16[128,2048]{1,0:T(8,128)(2,1)} %param.23) | copy-start | bytes 1572868
  131.5 40.4 %copy-start.16 = (f32[2048]{0:T(1024)S(1)}, f32[2048]{0:T(1024)}, u32[]{:S(2)}) copy-start(f32[2048]{0:T(1024)} %param.37) | copy-start | bytes 24580
  131.5 40.4 %copy-start.17 = (f32[2048]{0:T(1024)S(1)}, f32[2048]{0:T(1024)}, u32[]{:S(2)}) copy-start(f32[2048]{0:T(1024)} %param.34) | copy-start | bytes 24580
  131.5 42.3 %copy-start.18 = (f32[2048]{0:T(1024)S(1)}, f32[2048]{0:T(1024)}, u32[]{:S(2)}) copy-start(f32[2048]{0:T(1024)} %param.38) | copy-start | bytes 24580
  131.6 74.4 %all-gather.5.cloned.1.call-start = ((), (), s32[]{:S(2)}) async-start(), calls=%async_computation.5 | async-start | bytes 4718592 | tf_op jit(solution)/shard_map/all_gather | solution.py:252
  174.8 94.8 %reduce-scatter.5.cloned.1.call-start = ((), (), s32[]{:S(2)}) async-start(), calls=%async_computation.6 | async-start | bytes 4718592 | tf_op jit(solution)/shard_map/reduce_scatter | solution.py:253
  231.5 39.4 %copy-start.13 = (bf16[128,256]{1,0:T(8,128)(2,1)S(1)}, bf16[128,256]{1,0:T(8,128)(2,1)}, u32[]{:S(2)}) copy-start(bf16[128,256]{1,0:T(8,128)(2,1)} %param.24) | copy-start | bytes 196612
  231.5 39.4 %copy-start.14 = (f32[2048]{0:T(1024)S(1)}, f32[2048]{0:T(1024)}, u32[]{:S(2)}) copy-start(f32[2048]{0:T(1024)} %param.42) | copy-start | bytes 24580
  231.5 43.0 %copy-start.19 = (f32[2048]{0:T(1024)S(1)}, f32[2048]{0:T(1024)}, u32[]{:S(2)}) copy-start(f32[2048]{0:T(1024)} %param.45) | copy-start | bytes 24580
  231.5 45.4 %copy-start.1 = (bf16[256,2048]{1,0:T(8,128)(2,1)S(1)}, bf16[256,2048]{1,0:T(8,128)(2,1)}, u32[]{:S(2)}) copy-start(bf16[256,2048]{1,0:T(8,128)(2,1)} %param.33) | copy-start | bytes 3145732
  269.6 4.9 %copy-start.5 = (bf16[128,2048]{1,0:T(8,128)(2,1)S(1)}, bf16[128,2048]{1,0:T(8,128)(2,1)}, u32[]{:S(2)}) copy-start(bf16[128,2048]{1,0:T(8,128)(2,1)} %reduce-scatter.5.cloned.1.call-done) | copy-start | bytes 1572868
Sparse Core Ops, SparseCore 0:
  9.0 56.7 all-gather.2
  131.7 38.9 reduce-scatter.2
  174.9 31.0 all-gather.4
  231.6 37.8 reduce-scatter.4

commit v9 on v8

--- a/solution.py
+++ b/solution.py
@@ -128,6 +128,8 @@
     slot_count = page_table.shape[1]
     page_len = kv_pool.shape[3]
     pool_dev = kv_pool.shape[0]
+    swap_pair = [(t, t ^ lax.axis_size("tc")) for t in range(tp_count)]
+    neighbour_query_weight = lax.ppermute(w_query, TP, perm=swap_pair)
     needed = PROMPT_PAGES + REQ_DEV * (slot_count - PROMPT_PAGES)
     capacity = (needed + devices - 1) // devices
     page_count = (cached_len + page_len - 1) // page_len
@@ -188,8 +190,9 @@
     fresh_values = norm_rows(
         jnp.dot(normed, value_weight, preferred_element_type=jnp.float32), 1.0
     ).astype(jnp.bfloat16)
-    swap_pair = [(t, t ^ cores) for t in range(tp_count)]
-    neighbour_queries = lax.ppermute(queries, TP, perm=swap_pair)
+    neighbour_queries = jnp.dot(normed, neighbour_query_weight, preferred_element_type=jnp.float32)
+    neighbour_queries = neighbour_queries.reshape(token_count, local_heads, head_dim)
+    neighbour_queries = rotate(norm_rows(neighbour_queries, q_gain), position).astype(jnp.bfloat16)
     arrived, queries, neighbour_queries, fresh_keys, fresh_values = lax.optimization_barrier(
         (arrived, queries, neighbour_queries, fresh_keys, fresh_values)
     )

time: 284 us -> 283 us (level)
  waiting for transfers between devices: 162 us -> 158 us
    all_to_all x1, waiting for transfers between devices: 10.1 us -> 24.9 us  [per_device(): lax.all_to_all(outgoing, ALL, split_axis=0, concat_axis=0, tiled=True)]
    all_gather x1, waiting for transfers between devices: 34.8 us -> 27.2 us  [per_device(): gathered = lax.all_gather(hidden_in, TP, axis=0, tiled=True)]
    reduce_scatter x1, waiting for transfers between devices: 37 us -> 30.9 us  [per_device(): lax.psum_scatter(jnp.dot(attended, w_out, preferred_element_type=jnp.floa...]
    ppermute x1, waiting for transfers between devices: 5.2 us -> 0.01 us  [per_device(): neighbour_query_weight = lax.ppermute(w_query, TP, perm=swap_pair)]
  transfers between devices with their start and end apart: 14 -> 14, of which waited for: 7 -> 6; matrix products, arithmetic and copies ran while one was open for 14% -> 15% of each run, Pallas kernels for 0% -> 0%
where the time goes in v9:
time: 283 us; the launch traced here: 282 us
  waiting for transfers between devices  158 us (56%)
  matrix products  49.6 us (18%)
  other arithmetic  25.4 us (9%)
  starting transfers between devices  20.1 us (7%)
  local copies, waits for them, and re-layouts  15.4 us (5%)
  between operations  13.9 us (5%)
    reduce_scatter x1, waiting for transfers between devices, per_device(): lax.psum_scatter(jnp.dot(hidden, w_down, preferred_element_type=jnp.float...  38 us
    reduce_scatter x1, waiting for transfers between devices, per_device(): lax.psum_scatter(jnp.dot(attended, w_out, preferred_element_type=jnp.floa...  30.9 us
    all_gather x1, waiting for transfers between devices, per_device(): hidden = geglu(lax.all_gather(ffn_in, TP, axis=0, tiled=True), w_gate, w_up)  30.8 us
    all_gather x1, waiting for transfers between devices, per_device(): gathered = lax.all_gather(hidden_in, TP, axis=0, tiled=True)  27.2 us
    all_to_all x1, waiting for transfers between devices, per_device(): lax.all_to_all(outgoing, ALL, split_axis=0, concat_axis=0, tiled=True)  24.9 us
    dot_general x1, matrix products, per_device(): jnp.dot(hidden, w_down, preferred_element_type=jnp.float32)  15.6 us
    all_to_all x1, starting transfers between devices, per_device(): lax.all_to_all(outgoing, ALL, split_axis=0, concat_axis=0, tiled=True)  11.3 us
    dot_general x1, matrix products, geglu(): gate_part = jnp.dot(block, w_gate, preferred_element_type=jnp.float32)  9.93 us
  transfers between devices with their start and end apart: 14, of which 6 were waited for; matrix products, arithmetic and copies ran while one was open for 15% of the time, Pallas kernels for 0%

profile of v9, /device:TPU:0, one launch (start us, length us, event | category | flops | bytes accessed | tf_op | source)
XLA Modules:
  0.0 282.4 jit_solution(2975249989496155463)
XLA Ops:
  7.3 1.7 collective-permute-start
  9.9 0.8 eq.43
  12.5 0.8 gather_fusion.1
  13.3 5.0 %gather_fusion = bf16[256,32,256]{2,1,0:T(8,128)(2,1)} fusion(bf16[256,32,256]{2,1,0:T(8,128)(2,1)} %bitcast.241, s32[1024]{0:T(1024)S(1)} %get-tuple-element.84), kind=kCustom, calls=%fused_computation | custom fusion | bytes 8389632 | tf_op jit(solution)/shard_map/gather | solution.py:162
  18.3 11.3 %all-to-all-start = ((bf16[128,1,2,32,256]{4,3,2,1,0:T(8,128)(2,1)}), bf16[128,1,2,32,256]{4,3,2,1,0:T(8,128)(2,1)}, u32[]{:S(2)}, u32[]{:S(2)}) async-start(bf16[128,1,2,32,256]{4,3,2,1,0:T(8,128)(2,1)} %bitcast.240), calls=%async_computation | async-start | bytes 8388608 | tf_op jit(solution)/shard_map/all_to_all | solution.py:166
  30.5 1.3 fusion.163
  32.3 27.2 %all-gather.3.cloned.1.call-done = bf16[1024,2048]{1,0:T(8,128)(2,1)} async-done(((bf16[128,2048]{1,0:T(8,128)(2,1)}), bf16[1024,2048]{1,0:T(8,128)(2,1)}) %all-gather.3.cloned.1.call-update) | async-done | bytes 4194320 | tf_op jit(solution)/shard_map/all_gather | solution.py:176
  59.5 3.2 %fusion = f32[1024]{0:T(1024)S(1)} fusion(bf16[1024,2048]{1,0:T(8,128)(2,1)} %all-gather.3.cloned.1.call-done), kind=kLoop, calls=%fused_computation.5 | loop fusion | flops 6290432 | bytes 4198400 | tf_op jit(solution)/shard_map/reduce_sum | solution.py:21
  63.0 1.0 fusion.2
  64.0 1.2 copy-done.19
  65.2 1.4 multiply_reduce_fusion.4
  66.6 2.6 multiply_reduce_fusion.5
  69.3 1.3 multiply_reduce_fusion.6
  71.1 2.6 fusion.94
  73.6 0.9 maximum_bitcast_fusion
  74.5 0.9 pad_maximum_fusion
  75.4 1.3 multiply_reduce_fusion.3
  76.7 0.9 multiply_convert_fusion.1
  77.7 24.9 %all-to-all-done = bf16[128,1,2,32,256]{4,3,2,1,0:T(8,128)(2,1)} async-done(((bf16[128,1,2,32,256]{4,3,2,1,0:T(8,128)(2,1)}), bf16[128,1,2,32,256]{4,3,2,1,0:T(8,128)(2,1)}, u32[]{:S(2)}, u32[]{:S(2)}) %all-to-all-start) | async-done | bytes 4194336 | tf_op jit(solution)/shard_map/all_to_all | solution.py:166
  102.6 0.9 constant_dynamic-update-slice_fusion.1
  103.5 2.9 %gather_fusion.2 = bf16[64,2,32,256]{3,2,1,0:T(8,128)(2,1)S(1)} fusion(bf16[128,2,32,256]{3,2,1,0:T(8,128)(2,1)} %bitcast.7, s32[1024]{0:T(1024)S(1)} %get-tuple-element.83), kind=kCustom, calls=%fused_computation.2 | custom fusion | bytes 4194560 | tf_op jit(solution)/shard_map/gather | solution.py:200
  109.0 0.7 bitcast_reduce_fusion.3
  109.7 0.7 bitcast_reduce_fusion.1
  110.5 0.7 bitcast_reduce_fusion.2
  111.5 1.8 fusion.18
  113.6 1.8 collective-permute-start.2
  115.4 1.1 fusion.30
  116.5 1.1 fusion.48
  118.4 0.7 bitcast_reduce_fusion
  119.3 1.8 fusion.22
  121.1 1.9 collective-permute-start.8
  123.3 1.1 fusion.26
  124.4 1.1 fusion.51
  125.9 1.8 collective-permute-start.7
  127.8 5.3 %collective-permute-done.7 = bf16[512,256]{0,1:T(8,128)(2,1)S(1)} collective-permute-done((bf16[512,256]{0,1:T(8,128)(2,1)S(1)}, bf16[512,256]{0,1:T(8,128)(2,1)S(1)}, u32[]{:S(2)}, u32[]{:S(2)}) %collective-permute-start.7) | collective-permute-done | bytes 262176 | tf_op jit(solution)/shard_map/ppermute | solution.py:233
  133.3 3.3 %convolution_convert_fusion = bf16[1024,2048]{1,0:T(8,128)(2,1)} fusion(bf16[256,2048]{1,0:T(8,128)(2,1)S(1)} %copy-done, bf16[512,256]{0,1:T(8,128)(2,1)S(1)} %fusion.114, bf16[512,256]{0,1:T(8,128)(2,1)S(1)} %fusion.113), kind=kOutput, calls=%fused_computation.30 | convolution fusion | flops 1076887552 | bytes 5767168 | tf_op jit(solution)/shard_map/dot_general | solution.py:245
  136.7 2.0 multiply_reduce_fusion.2
  138.7 30.9 %reduce-scatter.3.cloned.1.call-done = bf16[128,2048]{1,0:T(8,128)(2,1)} async-done(((bf16[1024,2048]{1,0:T(8,128)(2,1)}), bf16[128,2048]{1,0:T(8,128)(2,1)}) %reduce-scatter.3.cloned.1.call-update) | async-done | bytes 524304 | tf_op jit(solution)/shard_map/reduce_scatter | solution.py:244
  169.6 1.2 fusion.55
  170.8 2.0 multiply_reduce_fusion.1
  172.8 0.9 multiply_convert_fusion
  174.1 30.8 %all-gather.5.cloned.1.call-done = bf16[1024,2048]{1,0:T(8,128)(2,1)} async-done(((bf16[128,2048]{1,0:T(8,128)(2,1)}), bf16[1024,2048]{1,0:T(8,128)(2,1)}) %all-gather.5.cloned.1.call-update) | async-done | bytes 4194320 | tf_op jit(solution)/shard_map/all_gather | solution.py:255
  204.9 9.9 %fusion.222 = f32[1024,1024]{1,0:T(8,128)} fusion(bf16[1024,2048]{1,0:T(8,128)(2,1)} %all-gather.5.cloned.1.call-done, bf16[2048,1024]{1,0:T(8,128)(2,1)} %param.39), kind=kOutput, calls=%fused_computation.308 | convolution fusion | flops 4294967296 | bytes 12582912 | tf_op jit(solution)/shard_map/dot_general | solution.py:88
  214.8 15.6 %convolution_convert_fusion.1 = bf16[1024,2048]{1,0:T(8,128)(2,1)} fusion(bf16[1024,2048]{1,0:T(8,128)(2,1)} %param.41, f32[1024,1024]{1,0:T(8,128)} %fusion.222, bf16[1024,2048]{1,0:T(8,128)(2,1)} %all-gather.5.cloned.1.call-done, bf16[2048,1024]{1,0:T(8,128)(2,1)} %param.40), kind=kOutput, calls=%fused_computation.31 | convolution fusion | flops 8602517504 | bytes 20971520 | tf_op jit(solution)/shard_map/dot_general | solution.py:257
  230.4 38.0 %reduce-scatter.5.cloned.1.call-done = bf16[128,2048]{1,0:T(8,128)(2,1)} async-done(((bf16[1024,2048]{1,0:T(8,128)(2,1)}), bf16[128,2048]{1,0:T(8,128)(2,1)}) %reduce-scatter.5.cloned.1.call-update) | async-done | bytes 524304 | tf_op jit(solution)/shard_map/reduce_scatter | solution.py:256
  268.5 1.3 fusion.59
  269.8 3.5 %multiply_reduce_fusion = (f32[128]{0:T(128)S(1)}, f32[128,2048]{1,0:T(8,128)}) fusion(bf16[256,2048]{1,0:T(8,128)(2,1)} %param.44, bf16[2048,256]{1,0:T(8,128)(2,1)} %param.43, bf16[128,2048]{1,0:T(8,128)(2,1)} %reduce-scatter.5.cloned.1.call-done, f32[128,2048]{1,0:T(8,128)S(1)} %get-tuple-element.20, f32[2048]{0:T(1024)S(1)} %copy-done.11, ...), kind=kOutput, calls=%fused_computation.80 | convolution fusion | flops 270892928 | bytes 4793344 | tf_op jit(solution)/shard_map/dot_general | solution.py:269
  273.4 2.5 add_convert_fusion
  (151 shorter events, 11.0 us)
Async XLA Ops:
  6.5 126.8 %copy-start = (bf16[256,2048]{1,0:T(8,128)(2,1)S(1)}, bf16[256,2048]{1,0:T(8,128)(2,1)}, u32[]{:S(2)}) copy-start(bf16[256,2048]{1,0:T(8,128)(2,1)} %param.33) | copy-start | bytes 3145732
  6.5 53.0 %all-gather.3.cloned.1.call-start = ((), (), s32[]{:S(2)}) async-start(), calls=%async_computation.3 | async-start | bytes 4718592 | tf_op jit(solution)/shard_map/all_gather | solution.py:176
  7.3 59.3 %collective-permute-start = (bf16[2048,256]{1,0:T(8,128)(2,1)}, bf16[2048,256]{1,0:T(8,128)(2,1)}, u32[]{:S(2)}, u32[]{:S(2)}) collective-permute-start(bf16[2048,256]{1,0:T(8,128)(2,1)} %param.29), channel_id=1, source_target_pairs={{0,2},{1,3},{2,0},{3,1},{4,6},{5,7},{6,4},{7,5},{8,10},{9,11},{10,... | collective-permute-start | bytes 3145736 | tf_op jit(solution)/shard_map/ppermute | solution.py:132
  18.3 11.4 %copy-start.21 = (s32[32]{0:T(128)S(1)}, s32[32]{0:T(128)}, u32[]{:S(2)}) copy-start(s32[32]{0:T(128)} %param.25) | copy-start | bytes 388
  18.3 84.3 %all-to-all-start = ((bf16[128,1,2,32,256]{4,3,2,1,0:T(8,128)(2,1)}), bf16[128,1,2,32,256]{4,3,2,1,0:T(8,128)(2,1)}, u32[]{:S(2)}, u32[]{:S(2)}) async-start(bf16[128,1,2,32,256]{4,3,2,1,0:T(8,128)(2,1)} %bitcast.240), calls=%async_computation | async-start | bytes 8388608 | tf_op jit(solution)/shard_map/all_to_all | solution.py:166
  29.6 33.2 %copy-start.12 = (f32[2048]{0:T(1024)S(1)}, f32[2048]{0:T(1024)}, u32[]{:S(2)}) copy-start(f32[2048]{0:T(1024)} %param.28) | copy-start | bytes 24580
  29.6 139.9 %reduce-scatter.3.cloned.1.call-start = ((), (), s32[]{:S(2)}) async-start(), calls=%async_computation.4 | async-start | bytes 4718592 | tf_op jit(solution)/shard_map/reduce_scatter | solution.py:244
  59.5 3.4 %copy-start.1 = (bf16[1024,2048]{1,0:T(8,128)(2,1)S(1)}, bf16[1024,2048]{1,0:T(8,128)(2,1)}, u32[]{:S(2)}) copy-start(bf16[1024,2048]{1,0:T(8,128)(2,1)} %all-gather.3.cloned.1.call-done) | copy-start | bytes 12582916
  63.0 2.2 copy-start.19
  65.2 10.2 %copy-start.3 = (bf16[1024,2048]{1,0:T(8,128)(2,1)}, bf16[1024,2048]{1,0:T(8,128)(2,1)S(1)}, u32[]{:S(2)}) copy-start(bf16[1024,2048]{1,0:T(8,128)(2,1)S(1)} %fusion.2) | copy-start | bytes 12582916
  66.5 2.7 copy-start.20
  69.2 1.4 copy-start.17
  69.2 1.6 copy-start.18
  106.3 1.0 copy-start.6
  106.3 1.2 copy-start.5
  106.4 1.5 copy-start.2
  106.4 1.7 copy-start.7
  106.6 3.9 %collective-permute-start.1 = (bf16[32,2,32,256]{3,2,1,0:T(8,128)(2,1)S(1)}, bf16[32,2,32,256]{3,2,1,0:T(8,128)(2,1)S(1)}, u32[]{:S(2)}, u32[]{:S(2)}) collective-permute-start(bf16[32,2,32,256]{3,2,1,0:T(8,128)(2,1)S(1)} %get-tuple-element.27), channel_id=1, source_target_pairs={{0,1},{1,0},{2,3},{3,2},{4,5},{5,4},{6,7},{7,6},{8,9},{9,8},{10,11... | collective-permute-start | bytes 3145736 | tf_op jit(solution)/shard_map/ppermute | solution.py:215
  107.6 10.7 %collective-permute-start.5 = (bf16[32,2,32,256]{3,2,1,0:T(8,128)(2,1)S(1)}, bf16[32,2,32,256]{3,2,1,0:T(8,128)(2,1)S(1)}, u32[]{:S(2)}, u32[]{:S(2)}) collective-permute-start(bf16[32,2,32,256]{3,2,1,0:T(8,128)(2,1)S(1)} %get-tuple-element.28), channel_id=1, source_target_pairs={{0,1},{1,0},{2,3},{3,2},{4,5},{5,4},{6,7},{7,6},{8,9},{9,8},{10,11... | collective-permute-start | bytes 3145736 | tf_op jit(solution)/shard_map/ppermute | solution.py:215
  113.3 12.6 %collective-permute-start.4 = (f32[512,1]{0,1:T(1,128)S(1)}, f32[512,1]{0,1:T(1,128)S(1)}, u32[]{:S(2)}, u32[]{:S(2)}) collective-permute-start(f32[512,1]{0,1:T(1,128)S(1)} %slice_bitcast_fusion.6), channel_id=1, source_target_pairs={{0,2},{1,3},{2,0},{3,1},{4,6},{5,7},{6,4},{7,5},{8,10},{9,11},{10,... | collective-permute-start | bytes 6152 | tf_op jit(solution)/shard_map/ppermute | solution.py:233
  113.6 14.1 %collective-permute-start.2 = (f32[512,1]{0,1:T(1,128)S(1)}, f32[512,1]{0,1:T(1,128)S(1)}, u32[]{:S(2)}, u32[]{:S(2)}) collective-permute-start(f32[512,1]{0,1:T(1,128)S(1)} %slice_bitcast_fusion.8), channel_id=1, source_target_pairs={{0,2},{1,3},{2,0},{3,1},{4,6},{5,7},{6,4},{7,5},{8,10},{9,11},{10,... | collective-permute-start | bytes 6152 | tf_op jit(solution)/shard_map/ppermute | solution.py:233
  117.9 9.8 %collective-permute-start.3 = (bf16[512,256]{0,1:T(8,128)(2,1)S(1)}, bf16[512,256]{0,1:T(8,128)(2,1)S(1)}, u32[]{:S(2)}, u32[]{:S(2)}) collective-permute-start(bf16[512,256]{0,1:T(8,128)(2,1)S(1)} %fusion.129), channel_id=1, source_target_pairs={{0,2},{1,3},{2,0},{3,1},{4,6},{5,7},{6,4},{7,5},{8,10},{9,11},{10,... | collective-permute-start | bytes 786440 | tf_op jit(solution)/shard_map/ppermute | solution.py:233
  121.1 6.6 %collective-permute-start.8 = (f32[512,1]{0,1:T(1,128)S(1)}, f32[512,1]{0,1:T(1,128)S(1)}, u32[]{:S(2)}, u32[]{:S(2)}) collective-permute-start(f32[512,1]{0,1:T(1,128)S(1)} %slice_bitcast_fusion.2), channel_id=1, source_target_pairs={{0,2},{1,3},{2,0},{3,1},{4,6},{5,7},{6,4},{7,5},{8,10},{9,11},{10,... | collective-permute-start | bytes 6152 | tf_op jit(solution)/shard_map/ppermute | solution.py:233
  123.0 4.7 %collective-permute-start.6 = (f32[512,1]{0,1:T(1,128)S(1)}, f32[512,1]{0,1:T(1,128)S(1)}, u32[]{:S(2)}, u32[]{:S(2)}) collective-permute-start(f32[512,1]{0,1:T(1,128)S(1)} %slice_bitcast_fusion.4), channel_id=1, source_target_pairs={{0,2},{1,3},{2,0},{3,1},{4,6},{5,7},{6,4},{7,5},{8,10},{9,11},{10,... | collective-permute-start | bytes 6152 | tf_op jit(solution)/shard_map/ppermute | solution.py:233
  125.9 7.3 %collective-permute-start.7 = (bf16[512,256]{0,1:T(8,128)(2,1)S(1)}, bf16[512,256]{0,1:T(8,128)(2,1)S(1)}, u32[]{:S(2)}, u32[]{:S(2)}) collective-permute-start(bf16[512,256]{0,1:T(8,128)(2,1)S(1)} %fusion.130), channel_id=1, source_target_pairs={{0,2},{1,3},{2,0},{3,1},{4,6},{5,7},{6,4},{7,5},{8,10},{9,11},{10,... | collective-permute-start | bytes 786440 | tf_op jit(solution)/shard_map/ppermute | solution.py:233
  133.3 3.4 %copy-start.8 = (bf16[64,2048]{1,0:T(8,128)(2,1)S(1)}, bf16[64,2048]{1,0:T(8,128)(2,1)}, u32[]{:S(2)}) copy-start(bf16[64,2048]{1,0:T(8,128)(2,1)} %param.36) | copy-start | bytes 786436
  133.3 3.4 %copy-start.9 = (bf16[2048,64]{0,1:T(8,128)(2,1)S(1)}, bf16[2048,64]{0,1:T(8,128)(2,1)}, u32[]{:S(2)}) copy-start(bf16[2048,64]{0,1:T(8,128)(2,1)} %param.35) | copy-start | bytes 786436
  136.6 34.2 %copy-start.13 = (f32[2048]{0:T(1024)S(1)}, f32[2048]{0:T(1024)}, u32[]{:S(2)}) copy-start(f32[2048]{0:T(1024)} %param.37) | copy-start | bytes 24580
  136.6 34.2 %copy-start.14 = (f32[2048]{0:T(1024)S(1)}, f32[2048]{0:T(1024)}, u32[]{:S(2)}) copy-start(f32[2048]{0:T(1024)} %param.34) | copy-start | bytes 24580
  136.6 36.2 %copy-start.15 = (f32[2048]{0:T(1024)S(1)}, f32[2048]{0:T(1024)}, u32[]{:S(2)}) copy-start(f32[2048]{0:T(1024)} %param.38) | copy-start | bytes 24580
  136.6 68.2 %all-gather.5.cloned.1.call-start = ((), (), s32[]{:S(2)}) async-start(), calls=%async_computation.5 | async-start | bytes 4718592 | tf_op jit(solution)/shard_map/all_gather | solution.py:255
  173.8 94.7 %reduce-scatter.5.cloned.1.call-start = ((), (), s32[]{:S(2)}) async-start(), calls=%async_computation.6 | async-start | bytes 4718592 | tf_op jit(solution)/shard_map/reduce_scatter | solution.py:256
  230.4 39.4 %copy-start.10 = (bf16[128,256]{1,0:T(8,128)(2,1)S(1)}, bf16[128,256]{1,0:T(8,128)(2,1)}, u32[]{:S(2)}) copy-start(bf16[128,256]{1,0:T(8,128)(2,1)} %param.24) | copy-start | bytes 196612
  230.4 39.4 %copy-start.11 = (f32[2048]{0:T(1024)S(1)}, f32[2048]{0:T(1024)}, u32[]{:S(2)}) copy-start(f32[2048]{0:T(1024)} %param.42) | copy-start | bytes 24580
  230.4 43.0 %copy-start.16 = (f32[2048]{0:T(1024)S(1)}, f32[2048]{0:T(1024)}, u32[]{:S(2)}) copy-start(f32[2048]{0:T(1024)} %param.45) | copy-start | bytes 24580
  268.5 4.9 %copy-start.4 = (bf16[128,2048]{1,0:T(8,128)(2,1)S(1)}, bf16[128,2048]{1,0:T(8,128)(2,1)}, u32[]{:S(2)}) copy-start(bf16[128,2048]{1,0:T(8,128)(2,1)} %reduce-scatter.5.cloned.1.call-done) | copy-start | bytes 1572868
Sparse Core Ops, SparseCore 0:
  9.0 50.4 all-gather.2
  136.7 32.7 reduce-scatter.2
  173.9 30.9 all-gather.4
  230.6 37.8 reduce-scatter.4

commit v10 on v9

--- a/solution.py
+++ b/solution.py
@@ -193,8 +193,16 @@
     neighbour_queries = jnp.dot(normed, neighbour_query_weight, preferred_element_type=jnp.float32)
     neighbour_queries = neighbour_queries.reshape(token_count, local_heads, head_dim)
     neighbour_queries = rotate(norm_rows(neighbour_queries, q_gain), position).astype(jnp.bfloat16)
-    arrived, queries, neighbour_queries, fresh_keys, fresh_values = lax.optimization_barrier(
-        (arrived, queries, neighbour_queries, fresh_keys, fresh_values)
+    own_normed = lax.dynamic_slice_in_dim(normed, tp_at * own_rows, own_rows, 0)
+    left_part = jnp.dot(own_normed, laurel_left, preferred_element_type=jnp.float32).astype(
+        jnp.bfloat16
+    )
+    laurel_out = own_normed.astype(jnp.float32) + norm_rows(
+        jnp.dot(left_part, laurel_right, preferred_element_type=jnp.float32), laurel_gain
+    )
+    base = hidden_in.astype(jnp.float32) + laurel_out
+    arrived, queries, neighbour_queries, fresh_keys, fresh_values, base = lax.optimization_barrier(
+        (arrived, queries, neighbour_queries, fresh_keys, fresh_values, base)
     )
     both_queries = jnp.concatenate([queries, neighbour_queries], axis=1)
     fetched = arrived.reshape(devices * capacity, 2, part_len, head_dim)[position_at]
@@ -240,17 +248,13 @@
         merged = out[:, 0] * near_scale + far_out.astype(jnp.float32) * far_scale
         pieces.append((merged / whole).astype(jnp.bfloat16))
     attended = jnp.concatenate(pieces, axis=0)
-    own_x = hidden_in.astype(jnp.float32)
     projected = lax.psum_scatter(
         jnp.dot(attended, w_out, preferred_element_type=jnp.float32).astype(jnp.bfloat16),
         TP,
         scatter_dimension=0,
         tiled=True,
     ).astype(jnp.float32)
-    own_normed = lax.dynamic_slice_in_dim(normed, tp_at * own_rows, own_rows, 0)
-    mixed_rows = residual_mix(
-        own_x, projected, own_normed, post_attn_gain, laurel_left, laurel_right, laurel_gain
-    )
+    mixed_rows = (base + norm_rows(projected, post_attn_gain)) * HALF_ROOT
     ffn_in = norm_rows(mixed_rows, pre_ffn_gain).astype(jnp.bfloat16)
     hidden = geglu(lax.all_gather(ffn_in, TP, axis=0, tiled=True), w_gate, w_up)
     down = lax.psum_scatter(

time: 283 us -> 319 us (1.13)
  waiting for transfers between devices: 158 us -> 180 us
  matrix products: 49.6 us -> 54.1 us
    ppermute x1, waiting for transfers between devices: 0.01 us -> 36.1 us  [per_device(): neighbour_query_weight = lax.ppermute(w_query, TP, perm=swap_pair)]
    all_to_all x1, waiting for transfers between devices: 24.9 us -> 0.01 us  [per_device(): lax.all_to_all(outgoing, ALL, split_axis=0, concat_axis=0, tiled=True)]
    reduce_scatter x1, waiting for transfers between devices: 30.9 us -> 39.1 us  [per_device(): lax.psum_scatter(jnp.dot(attended, w_out, preferred_element_type=jnp.floa...]
    all_gather x1, waiting for transfers between devices: 27.2 us -> 31.9 us  [per_device(): gathered = lax.all_gather(hidden_in, TP, axis=0, tiled=True)]
  transfers between devices with their start and end apart: 14 -> 14, of which waited for: 6 -> 6; matrix products, arithmetic and copies ran while one was open for 15% -> 16% of each run, Pallas kernels for 0% -> 0%
where the time goes in v10:
time: 319 us; the launch traced here: 316 us
  waiting for transfers between devices  180 us (56%)
  matrix products  54.1 us (17%)
  other arithmetic  28.3 us (9%)
  starting transfers between devices  20.4 us (6%)
  local copies, waits for them, and re-layouts  18.3 us (6%)
  between operations  14.3 us (4%)
    reduce_scatter x1, waiting for transfers between devices, per_device(): lax.psum_scatter(jnp.dot(attended, w_out, preferred_element_type=jnp.floa...  39.1 us
    reduce_scatter x1, waiting for transfers between devices, per_device(): lax.psum_scatter(jnp.dot(hidden, w_down, preferred_element_type=jnp.float...  38 us
    ppermute x1, waiting for transfers between devices, per_device(): neighbour_query_weight = lax.ppermute(w_query, TP, perm=swap_pair)  36.1 us
    all_gather x1, waiting for transfers between devices, per_device(): gathered = lax.all_gather(hidden_in, TP, axis=0, tiled=True)  31.9 us
    all_gather x1, waiting for transfers between devices, per_device(): hidden = geglu(lax.all_gather(ffn_in, TP, axis=0, tiled=True), w_gate, w_up)  31 us
    dot_general x1, matrix products, per_device(): jnp.dot(hidden, w_down, preferred_element_type=jnp.float32)  15.6 us
    all_to_all x1, starting transfers between devices, per_device(): lax.all_to_all(outgoing, ALL, split_axis=0, concat_axis=0, tiled=True)  11.7 us
    dot_general x1, matrix products, geglu(): gate_part = jnp.dot(block, w_gate, preferred_element_type=jnp.float32)  9.93 us
  transfers between devices with their start and end apart: 14, of which 6 were waited for; matrix products, arithmetic and copies ran while one was open for 16% of the time, Pallas kernels for 0%

profile of v10, /device:TPU:0, one launch (start us, length us, event | category | flops | bytes accessed | tf_op | source)
XLA Modules:
  0.0 315.8 jit_solution(8646784362756268992)
XLA Ops:
  7.3 0.8 eq.43
  10.8 0.8 gather_fusion.1
  12.2 5.0 %gather_fusion = bf16[256,32,256]{2,1,0:T(8,128)(2,1)} fusion(bf16[256,32,256]{2,1,0:T(8,128)(2,1)} %bitcast.241, s32[1024]{0:T(1024)S(1)} %get-tuple-element.84), kind=kCustom, calls=%fused_computation | custom fusion | bytes 8389632 | tf_op jit(solution)/shard_map/gather | solution.py:162
  17.2 11.7 %all-to-all-start = ((bf16[128,1,2,32,256]{4,3,2,1,0:T(8,128)(2,1)}), bf16[128,1,2,32,256]{4,3,2,1,0:T(8,128)(2,1)}, u32[]{:S(2)}, u32[]{:S(2)}) async-start(bf16[128,1,2,32,256]{4,3,2,1,0:T(8,128)(2,1)} %bitcast.240), calls=%async_computation | async-start | bytes 8388608 | tf_op jit(solution)/shard_map/all_to_all | solution.py:166
  29.0 1.1 collective-permute-start
  30.9 1.3 fusion.162
  32.7 31.9 %all-gather.3.cloned.1.call-done = bf16[1024,2048]{1,0:T(8,128)(2,1)} async-done(((bf16[128,2048]{1,0:T(8,128)(2,1)}), bf16[1024,2048]{1,0:T(8,128)(2,1)}) %all-gather.3.cloned.1.call-update) | async-done | bytes 4194320 | tf_op jit(solution)/shard_map/all_gather | solution.py:176
  64.6 3.2 %fusion = f32[1024]{0:T(1024)S(1)} fusion(bf16[1024,2048]{1,0:T(8,128)(2,1)} %all-gather.3.cloned.1.call-done), kind=kLoop, calls=%fused_computation.5 | loop fusion | flops 6290432 | bytes 4198400 | tf_op jit(solution)/shard_map/reduce_sum | solution.py:21
  68.0 1.0 fusion.2
  69.0 3.4 %multiply_reduce_fusion.4 = (f32[1024]{0:T(1024)S(1)}, f32[1024,256]{0,1:T(8,128)S(1)}) fusion(bf16[1024,2048]{1,0:T(8,128)(2,1)S(1)} %fusion.2, bf16[2048,1024]{1,0:T(8,128)(2,1)} %param.30, s32[]{:T(128)S(6)} %select_n.139), kind=kOutput, calls=%fused_computation.91 | convolution fusion | flops 1074265088 | bytes 6295556 | tf_op jit(solution)/shard_map/dot_general | solution.py:188
  72.4 36.1 %collective-permute-done = bf16[2048,256]{1,0:T(8,128)(2,1)} collective-permute-done((bf16[2048,256]{1,0:T(8,128)(2,1)S(1)}, bf16[2048,256]{1,0:T(8,128)(2,1)}, u32[]{:S(2)}, u32[]{:S(2)}) %collective-permute-start) | collective-permute-done | bytes 1048608 | tf_op jit(solution)/shard_map/ppermute | solution.py:132
  108.6 2.6 multiply_reduce_fusion.5
  111.2 1.3 multiply_reduce_fusion.6
  113.0 2.6 fusion.93
  115.6 0.8 maximum_bitcast_fusion
  116.4 1.1 pad_maximum_fusion
  117.5 2.0 multiply_reduce_fusion.2
  119.4 3.9 %multiply_reduce_fusion.3 = (f32[1024]{0:T(1024)S(1)}, f32[1024,256]{0,1:T(8,128)S(1)}) fusion(bf16[1024,2048]{1,0:T(8,128)(2,1)} %copy-done.4, bf16[2048,1024]{1,0:T(8,128)(2,1)} %param.30, s32[]{:T(128)S(6)} %select_n.140), kind=kOutput, calls=%fused_computation.87 | convolution fusion | flops 1074265088 | bytes 6295556 | tf_op jit(solution)/shard_map/dot_general | solution.py:191
  123.3 0.9 multiply_convert_fusion.1
  124.3 1.3 add_add_fusion
  125.6 1.1 constant_dynamic-update-slice_fusion.1
  126.7 1.8 fusion.214
  128.5 4.3 %gather_fusion.2 = bf16[64,2,32,256]{3,2,1,0:T(8,128)(2,1)} fusion(bf16[128,2,32,256]{3,2,1,0:T(8,128)(2,1)} %bitcast.7, s32[1024]{0:T(1024)} %get-tuple-element.83), kind=kCustom, calls=%fused_computation.2 | custom fusion | bytes 4194560 | tf_op jit(solution)/shard_map/gather | solution.py:208
  132.8 1.9 fusion.209
  135.6 0.8 collective-permute-start.1
  139.1 1.1 fusion.26
  140.1 1.1 fusion.51
  141.8 1.8 fusion.22
  143.6 2.0 collective-permute-start.8
  145.8 0.7 bitcast_reduce_fusion.2
  146.7 1.1 fusion.30
  147.8 1.8 fusion.18
  149.6 1.1 fusion.48
  151.1 2.0 collective-permute-start.3
  153.3 2.2 collective-permute-start.2
  155.5 3.4 %collective-permute-done.4 = f32[512,1]{0,1:T(1,128)S(1)} collective-permute-done((f32[512,1]{0,1:T(1,128)S(1)}, f32[512,1]{0,1:T(1,128)S(1)}, u32[]{:S(2)}, u32[]{:S(2)}) %collective-permute-start.4) | collective-permute-done | bytes 2080 | tf_op jit(solution)/shard_map/ppermute | solution.py:241
  159.2 3.2 %convolution_convert_fusion = bf16[1024,2048]{1,0:T(8,128)(2,1)} fusion(bf16[256,2048]{1,0:T(8,128)(2,1)S(1)} %copy-done, bf16[512,256]{0,1:T(8,128)(2,1)S(1)} %fusion.113, bf16[512,256]{0,1:T(8,128)(2,1)S(1)} %fusion.112), kind=kOutput, calls=%fused_computation.30 | convolution fusion | flops 1076887552 | bytes 5767168 | tf_op jit(solution)/shard_map/dot_general | solution.py:252
  162.5 39.1 %reduce-scatter.3.cloned.1.call-done = bf16[128,2048]{1,0:T(8,128)(2,1)} async-done(((bf16[1024,2048]{1,0:T(8,128)(2,1)}), bf16[128,2048]{1,0:T(8,128)(2,1)}) %reduce-scatter.3.cloned.1.call-update) | async-done | bytes 524304 | tf_op jit(solution)/shard_map/reduce_scatter | solution.py:251
  201.6 1.2 fusion.55
  202.9 1.4 multiply_reduce_fusion.1
  204.3 2.1 multiply_convert_fusion
  206.6 31.0 %all-gather.5.cloned.1.call-done = bf16[1024,2048]{1,0:T(8,128)(2,1)} async-done(((bf16[128,2048]{1,0:T(8,128)(2,1)}), bf16[1024,2048]{1,0:T(8,128)(2,1)}) %all-gather.5.cloned.1.call-update) | async-done | bytes 4194320 | tf_op jit(solution)/shard_map/all_gather | solution.py:259
  237.6 9.9 %fusion.222 = f32[1024,1024]{1,0:T(8,128)} fusion(bf16[1024,2048]{1,0:T(8,128)(2,1)} %all-gather.5.cloned.1.call-done, bf16[2048,1024]{1,0:T(8,128)(2,1)} %param.39), kind=kOutput, calls=%fused_computation.308 | convolution fusion | flops 4294967296 | bytes 12582912 | tf_op jit(solution)/shard_map/dot_general | solution.py:88
  247.5 15.6 %convolution_convert_fusion.1 = bf16[1024,2048]{1,0:T(8,128)(2,1)} fusion(bf16[1024,2048]{1,0:T(8,128)(2,1)} %param.41, f32[1024,1024]{1,0:T(8,128)} %fusion.222, bf16[1024,2048]{1,0:T(8,128)(2,1)} %all-gather.5.cloned.1.call-done, bf16[2048,1024]{1,0:T(8,128)(2,1)} %param.40), kind=kOutput, calls=%fused_computation.31 | convolution fusion | flops 8602517504 | bytes 20971520 | tf_op jit(solution)/shard_map/dot_general | solution.py:261
  263.2 38.0 %reduce-scatter.5.cloned.1.call-done = bf16[128,2048]{1,0:T(8,128)(2,1)} async-done(((bf16[1024,2048]{1,0:T(8,128)(2,1)}), bf16[128,2048]{1,0:T(8,128)(2,1)}) %reduce-scatter.5.cloned.1.call-update) | async-done | bytes 524304 | tf_op jit(solution)/shard_map/reduce_scatter | solution.py:260
  301.3 1.3 fusion.58
  302.6 3.6 %multiply_reduce_fusion = (f32[128]{0:T(128)S(1)}, f32[128,2048]{1,0:T(8,128)}) fusion(bf16[256,2048]{1,0:T(8,128)(2,1)} %param.44, bf16[2048,256]{1,0:T(8,128)(2,1)} %param.43, bf16[128,2048]{1,0:T(8,128)(2,1)} %reduce-scatter.5.cloned.1.call-done, f32[2048]{0:T(1024)S(1)} %copy-done.14, f32[128]{0:T(128)S(1)} %add_rsqrt_fusion.6, ...), kind=kOutput, calls=%fused_computation.79 | convolution fusion | flops 271941504 | bytes 5326336 | tf_op jit(solution)/shard_map/dot_general | solution.py:273
  306.2 2.7 add_convert_fusion
  (154 shorter events, 11.5 us)
Async XLA Ops:
  6.5 152.6 %copy-start = (bf16[256,2048]{1,0:T(8,128)(2,1)S(1)}, bf16[256,2048]{1,0:T(8,128)(2,1)}, u32[]{:S(2)}) copy-start(bf16[256,2048]{1,0:T(8,128)(2,1)} %param.33) | copy-start | bytes 3145732
  6.5 58.0 %all-gather.3.cloned.1.call-start = ((), (), s32[]{:S(2)}) async-start(), calls=%async_computation.3 | async-start | bytes 4718592 | tf_op jit(solution)/shard_map/all_gather | solution.py:176
  17.2 11.8 %copy-start.21 = (bf16[2048,256]{1,0:T(8,128)(2,1)S(1)}, bf16[2048,256]{1,0:T(8,128)(2,1)}, u32[]{:S(2)}) copy-start(bf16[2048,256]{1,0:T(8,128)(2,1)} %param.29) | copy-start | bytes 3145732
  17.2 12.9 %copy-start.22 = (s32[32]{0:T(128)S(1)}, s32[32]{0:T(128)}, u32[]{:S(2)}) copy-start(s32[32]{0:T(128)} %param.25) | copy-start | bytes 388
  17.2 108.4 %all-to-all-start = ((bf16[128,1,2,32,256]{4,3,2,1,0:T(8,128)(2,1)}), bf16[128,1,2,32,256]{4,3,2,1,0:T(8,128)(2,1)}, u32[]{:S(2)}, u32[]{:S(2)}) async-start(bf16[128,1,2,32,256]{4,3,2,1,0:T(8,128)(2,1)} %bitcast.240), calls=%async_computation | async-start | bytes 8388608 | tf_op jit(solution)/shard_map/all_to_all | solution.py:166
  28.9 38.9 %copy-start.15 = (f32[2048]{0:T(1024)S(1)}, f32[2048]{0:T(1024)}, u32[]{:S(2)}) copy-start(f32[2048]{0:T(1024)} %param.28) | copy-start | bytes 24580
  28.9 172.7 %reduce-scatter.3.cloned.1.call-start = ((), (), s32[]{:S(2)}) async-start(), calls=%async_computation.4 | async-start | bytes 4718592 | tf_op jit(solution)/shard_map/reduce_scatter | solution.py:251
  29.0 79.6 %collective-permute-start = (bf16[2048,256]{1,0:T(8,128)(2,1)S(1)}, bf16[2048,256]{1,0:T(8,128)(2,1)}, u32[]{:S(2)}, u32[]{:S(2)}) collective-permute-start(bf16[2048,256]{1,0:T(8,128)(2,1)S(1)} %copy-done.21), channel_id=1, source_target_pairs={{0,2},{1,3},{2,0},{3,1},{4,6},{5,7},{6,4},{7,5},{8,10},{9,11},{10,... | collective-permute-start | bytes 3145736 | tf_op jit(solution)/shard_map/ppermute | solution.py:132
  64.6 3.4 %copy-start.2 = (bf16[1024,2048]{1,0:T(8,128)(2,1)S(1)}, bf16[1024,2048]{1,0:T(8,128)(2,1)}, u32[]{:S(2)}) copy-start(bf16[1024,2048]{1,0:T(8,128)(2,1)} %all-gather.3.cloned.1.call-done) | copy-start | bytes 12582916
  69.0 42.1 %copy-start.4 = (bf16[1024,2048]{1,0:T(8,128)(2,1)}, bf16[1024,2048]{1,0:T(8,128)(2,1)S(1)}, u32[]{:S(2)}) copy-start(bf16[1024,2048]{1,0:T(8,128)(2,1)S(1)} %fusion.2) | copy-start | bytes 12582916
  111.2 1.4 copy-start.19
  111.2 1.6 copy-start.20
  113.0 4.5 %copy-start.10 = (bf16[64,2048]{1,0:T(8,128)(2,1)S(1)}, bf16[64,2048]{1,0:T(8,128)(2,1)}, u32[]{:S(2)}) copy-start(bf16[64,2048]{1,0:T(8,128)(2,1)} %param.36) | copy-start | bytes 786436
  113.0 4.5 %copy-start.11 = (bf16[2048,64]{0,1:T(8,128)(2,1)S(1)}, bf16[2048,64]{0,1:T(8,128)(2,1)}, u32[]{:S(2)}) copy-start(bf16[2048,64]{0,1:T(8,128)(2,1)} %param.35) | copy-start | bytes 786436
  119.4 4.8 %copy-start.7 = (bf16[128,2048]{1,0:T(8,128)(2,1)S(1)}, bf16[128,2048]{1,0:T(8,128)(2,1)}, u32[]{:S(2)}) copy-start(bf16[128,2048]{1,0:T(8,128)(2,1)} %param.23) | copy-start | bytes 1572868
  119.4 4.8 %copy-start.16 = (f32[2048]{0:T(1024)S(1)}, f32[2048]{0:T(1024)}, u32[]{:S(2)}) copy-start(f32[2048]{0:T(1024)} %param.37) | copy-start | bytes 24580
  132.8 2.0 copy-start.8
  132.8 2.0 copy-start.9
  132.8 2.8 copy-start.6
  132.8 3.6 %copy-start.1 = (bf16[64,2,32,256]{3,2,1,0:T(8,128)(2,1)S(1)}, bf16[64,2,32,256]{3,2,1,0:T(8,128)(2,1)}, u32[]{:S(2)}) copy-start(bf16[64,2,32,256]{3,2,1,0:T(8,128)(2,1)} %gather_fusion.2) | copy-start | bytes 6291460
  134.7 3.4 %collective-permute-start.5 = (bf16[32,2,32,256]{3,2,1,0:T(8,128)(2,1)S(1)}, bf16[32,2,32,256]{3,2,1,0:T(8,128)(2,1)S(1)}, u32[]{:S(2)}, u32[]{:S(2)}) collective-permute-start(bf16[32,2,32,256]{3,2,1,0:T(8,128)(2,1)S(1)} %get-tuple-element.28), channel_id=1, source_target_pairs={{0,1},{1,0},{2,3},{3,2},{4,5},{5,4},{6,7},{7,6},{8,9},{9,8},{10,11... | collective-permute-start | bytes 3145736 | tf_op jit(solution)/shard_map/ppermute | solution.py:223
  135.6 10.1 %collective-permute-start.1 = (bf16[32,2,32,256]{3,2,1,0:T(8,128)(2,1)S(1)}, bf16[32,2,32,256]{3,2,1,0:T(8,128)(2,1)S(1)}, u32[]{:S(2)}, u32[]{:S(2)}) collective-permute-start(bf16[32,2,32,256]{3,2,1,0:T(8,128)(2,1)S(1)} %get-tuple-element.27), channel_id=1, source_target_pairs={{0,1},{1,0},{2,3},{3,2},{4,5},{5,4},{6,7},{7,6},{8,9},{9,8},{10,11... | collective-permute-start | bytes 3145736 | tf_op jit(solution)/shard_map/ppermute | solution.py:223
  141.6 17.3 %collective-permute-start.7 = (bf16[512,256]{0,1:T(8,128)(2,1)S(1)}, bf16[512,256]{0,1:T(8,128)(2,1)S(1)}, u32[]{:S(2)}, u32[]{:S(2)}) collective-permute-start(bf16[512,256]{0,1:T(8,128)(2,1)S(1)} %fusion.129), channel_id=1, source_target_pairs={{0,2},{1,3},{2,0},{3,1},{4,6},{5,7},{6,4},{7,5},{8,10},{9,11},{10,... | collective-permute-start | bytes 786440 | tf_op jit(solution)/shard_map/ppermute | solution.py:241
  143.6 9.7 %collective-permute-start.8 = (f32[512,1]{0,1:T(1,128)S(1)}, f32[512,1]{0,1:T(1,128)S(1)}, u32[]{:S(2)}, u32[]{:S(2)}) collective-permute-start(f32[512,1]{0,1:T(1,128)S(1)} %slice_bitcast_fusion.2), channel_id=1, source_target_pairs={{0,2},{1,3},{2,0},{3,1},{4,6},{5,7},{6,4},{7,5},{8,10},{9,11},{10,... | collective-permute-start | bytes 6152 | tf_op jit(solution)/shard_map/ppermute | solution.py:241
  145.6 9.8 %collective-permute-start.6 = (f32[512,1]{0,1:T(1,128)S(1)}, f32[512,1]{0,1:T(1,128)S(1)}, u32[]{:S(2)}, u32[]{:S(2)}) collective-permute-start(f32[512,1]{0,1:T(1,128)S(1)} %slice_bitcast_fusion.4), channel_id=1, source_target_pairs={{0,2},{1,3},{2,0},{3,1},{4,6},{5,7},{6,4},{7,5},{8,10},{9,11},{10,... | collective-permute-start | bytes 6152 | tf_op jit(solution)/shard_map/ppermute | solution.py:241
  151.1 8.0 %collective-permute-start.3 = (bf16[512,256]{0,1:T(8,128)(2,1)S(1)}, bf16[512,256]{0,1:T(8,128)(2,1)S(1)}, u32[]{:S(2)}, u32[]{:S(2)}) collective-permute-start(bf16[512,256]{0,1:T(8,128)(2,1)S(1)} %fusion.128), channel_id=1, source_target_pairs={{0,2},{1,3},{2,0},{3,1},{4,6},{5,7},{6,4},{7,5},{8,10},{9,11},{10,... | collective-permute-start | bytes 786440 | tf_op jit(solution)/shard_map/ppermute | solution.py:241
  153.1 5.8 %collective-permute-start.4 = (f32[512,1]{0,1:T(1,128)S(1)}, f32[512,1]{0,1:T(1,128)S(1)}, u32[]{:S(2)}, u32[]{:S(2)}) collective-permute-start(f32[512,1]{0,1:T(1,128)S(1)} %slice_bitcast_fusion.6), channel_id=1, source_target_pairs={{0,2},{1,3},{2,0},{3,1},{4,6},{5,7},{6,4},{7,5},{8,10},{9,11},{10,... | collective-permute-start | bytes 6152 | tf_op jit(solution)/shard_map/ppermute | solution.py:241
  153.3 5.6 %collective-permute-start.2 = (f32[512,1]{0,1:T(1,128)S(1)}, f32[512,1]{0,1:T(1,128)S(1)}, u32[]{:S(2)}, u32[]{:S(2)}) collective-permute-start(f32[512,1]{0,1:T(1,128)S(1)} %slice_bitcast_fusion.8), channel_id=1, source_target_pairs={{0,2},{1,3},{2,0},{3,1},{4,6},{5,7},{6,4},{7,5},{8,10},{9,11},{10,... | collective-permute-start | bytes 6152 | tf_op jit(solution)/shard_map/ppermute | solution.py:241
  162.4 40.5 %copy-start.12 = (f32[2048]{0:T(1024)S(1)}, f32[2048]{0:T(1024)}, u32[]{:S(2)}) copy-start(f32[2048]{0:T(1024)} %param.34) | copy-start | bytes 24580
  162.4 41.9 %copy-start.17 = (f32[2048]{0:T(1024)S(1)}, f32[2048]{0:T(1024)}, u32[]{:S(2)}) copy-start(f32[2048]{0:T(1024)} %param.38) | copy-start | bytes 24580
  162.5 75.1 %all-gather.5.cloned.1.call-start = ((), (), s32[]{:S(2)}) async-start(), calls=%async_computation.5 | async-start | bytes 4718592 | tf_op jit(solution)/shard_map/all_gather | solution.py:259
  206.5 94.7 %reduce-scatter.5.cloned.1.call-start = ((), (), s32[]{:S(2)}) async-start(), calls=%async_computation.6 | async-start | bytes 4718592 | tf_op jit(solution)/shard_map/reduce_scatter | solution.py:260
  263.2 39.4 %copy-start.3 = (bf16[128,2048]{1,0:T(8,128)(2,1)S(1)}, bf16[128,2048]{1,0:T(8,128)(2,1)}, u32[]{:S(2)}) copy-start(bf16[128,2048]{1,0:T(8,128)(2,1)} %reduce-scatter.3.cloned.1.call-done) | copy-start | bytes 1572868
  263.2 39.4 %copy-start.13 = (bf16[128,256]{1,0:T(8,128)(2,1)S(1)}, bf16[128,256]{1,0:T(8,128)(2,1)}, u32[]{:S(2)}) copy-start(bf16[128,256]{1,0:T(8,128)(2,1)} %param.24) | copy-start | bytes 196612
  263.2 39.4 %copy-start.14 = (f32[2048]{0:T(1024)S(1)}, f32[2048]{0:T(1024)}, u32[]{:S(2)}) copy-start(f32[2048]{0:T(1024)} %param.42) | copy-start | bytes 24580
  263.2 43.0 %copy-start.18 = (f32[2048]{0:T(1024)S(1)}, f32[2048]{0:T(1024)}, u32[]{:S(2)}) copy-start(f32[2048]{0:T(1024)} %param.45) | copy-start | bytes 24580
  301.3 4.9 %copy-start.5 = (bf16[128,2048]{1,0:T(8,128)(2,1)S(1)}, bf16[128,2048]{1,0:T(8,128)(2,1)}, u32[]{:S(2)}) copy-start(bf16[128,2048]{1,0:T(8,128)(2,1)} %reduce-scatter.5.cloned.1.call-done) | copy-start | bytes 1572868
Sparse Core Ops, SparseCore 0:
  9.0 55.4 all-gather.2
  162.6 39.0 reduce-scatter.2
  206.6 30.9 all-gather.4
  263.3 37.8 reduce-scatter.4
